TPU v7x, 256 devices: a whole 4x4x8 slice. The times are simulated.
256 devices in a mesh: dp: 64 (over x, z, core), tensor: 4 (over y).
Axes of the slice: x: 4, y: 4, z: 8, core: 2. Of those that a mesh axis runs over, the one named last changes fastest.
Arguments:
- tokens: bfloat16 [512, 16384], P('dp', 'tensor'), may hold values from -6 to 6
- clip_act: float32 [16384], P('tensor'), may hold values from 0.5 to 4
- weight: bfloat16 [16384, 49152], P('tensor', 'dp'), may hold values from -0.046875 to 0.046875
- clip_weight: float32 [49152], P('dp'), may hold values from 0.003 to 0.03
- cotangent: bfloat16 [512, 49152], P('tensor', 'dp'), may hold values from -16 to 16
Outputs:
- projected: bfloat16 [512, 49152], P('tensor', 'dp')
- token_grad: bfloat16 [512, 16384], P('dp', 'tensor')
- weight_grad: bfloat16 [16384, 49152], P('tensor', 'dp')
- clip_act_grad: float32 [16384], P('tensor')
- clip_weight_grad: float32 [49152], P('dp')
All inputs are finite; a program needn't handle non-finite values.
Results may differ from a plain program's by a relative error of at most 0.009.
Values may be sent and summed in bfloat16 or wider, within the bound.
No kernel may reach another device: no remote copies, remote signals or barrier semaphores. Data moves between devices by JAX's collectives and lax.ppermute only.
A program may use at most 128 MiB of HBM per device.

v0:
```python
import math

import jax
import jax.numpy as jnp
from jax import lax
from jax.sharding import PartitionSpec as P


def swapped(block, axis, bit):
    count = lax.axis_size(axis)
    route = []
    for low in range(count):
        high = low | 1 << bit
        if high != low and high < count:
            route += [(low, high), (high, low)]
    return lax.ppermute(block, axis, route)


def sylvester(order):
    index = lax.iota(jnp.int32, order)
    joined = jnp.bitwise_and(index[:, None], index[None, :])
    parity = jnp.zeros((order, order), jnp.int32)
    for bit_number in range(max(order.bit_length() - 1, 0)):
        parity = parity + jnp.bitwise_and(jnp.right_shift(joined, bit_number), 1)
    return (1 - 2 * jnp.bitwise_and(parity, 1)).astype(jnp.float32)


def local_rotate(values, norm_factor):
    row_total, width = values.shape
    levels = width.bit_length() - 1
    outer = 2 ** (levels // 2)
    inner = width // outer
    blocks = values.reshape(row_total, outer, inner)
    blocks = jnp.einsum("rab,ac->rcb", blocks, sylvester(outer), precision=lax.Precision.HIGHEST)
    blocks = jnp.einsum("rcb,bd->rcd", blocks, sylvester(inner), precision=lax.Precision.HIGHEST)
    return blocks.reshape(row_total, width) * norm_factor


def rotate(values):
    group_size = lax.axis_size("tensor")
    norm_factor = 1.0 / math.sqrt(values.shape[1] * group_size)
    mixed = local_rotate(values, norm_factor)
    position = lax.axis_index("tensor")
    for bit_number in range(group_size.bit_length() - 1):
        partner = swapped(mixed, "tensor", bit_number)
        upper = jnp.bitwise_and(jnp.right_shift(position, bit_number), 1) == 1
        mixed = jnp.where(upper, partner - mixed, mixed + partner)
    return mixed


def body(tokens, clip_act, weight, clip_weight, cotangent):
    rotated = rotate(tokens.astype(jnp.float32))
    ratio_act = rotated / clip_act
    tanh_act = jnp.tanh(ratio_act)
    quant_act = (clip_act * tanh_act).astype(jnp.bfloat16)
    slope_act = 1.0 - tanh_act * tanh_act
    edge_act = tanh_act - ratio_act * slope_act
    all_act = lax.all_gather(quant_act, "dp", axis=0, tiled=True)
    ratio_weight = weight.astype(jnp.float32) / clip_weight
    tanh_weight = jnp.tanh(ratio_weight)
    quant_weight = (clip_weight * tanh_weight).astype(jnp.bfloat16)
    block = all_act
    projected = lax.psum_scatter(
        jnp.dot(block, quant_weight, preferred_element_type=jnp.float32),
        "tensor",
        scatter_dimension=0,
        tiled=True,
    ).astype(jnp.bfloat16)
    all_cot = lax.all_gather(cotangent, "tensor", axis=0, tiled=True)
    weight_prod = lax.dot_general(
        all_act, all_cot, (((0,), (0,)), ((), ())), preferred_element_type=jnp.float32
    )
    slope_weight = 1.0 - tanh_weight * tanh_weight
    weight_grad = (weight_prod * slope_weight).astype(jnp.bfloat16)
    weight_terms = jnp.sum(weight_prod * (tanh_weight - ratio_weight * slope_weight), axis=0)
    clip_weight_grad = lax.psum(weight_terms, "tensor")
    block = all_cot
    act_prod = lax.psum_scatter(
        lax.dot_general(
            block, quant_weight, (((1,), (1,)), ((), ())), preferred_element_type=jnp.float32
        ),
        "dp",
        scatter_dimension=0,
        tiled=True,
    )
    clip_act_grad = lax.psum(jnp.sum(act_prod * edge_act, axis=0), "dp")
    pre_rotation = act_prod * slope_act
    token_grad = rotate(pre_rotation).astype(jnp.bfloat16)
    return (projected, token_grad, weight_grad, clip_act_grad, clip_weight_grad)


def solution(mesh):
    in_specs = (P("dp", "tensor"), P("tensor"), P("tensor", "dp"), P("dp"), P("tensor", "dp"))
    out_specs = (P("tensor", "dp"), P("dp", "tensor"), P("tensor", "dp"), P("tensor"), P("dp"))
    return jax.shard_map(body, mesh=mesh, in_specs=in_specs, out_specs=out_specs, check_vma=False)
```

profile of v0, /device:TPU:2, one launch (start us, length us, event | category | flops | bytes accessed | tf_op | source)
XLA Modules:
  0.0 487.0 jit_solution(6198169342169980642)
XLA Ops:
  7.2 0.0 reduce-scatter.7.cloned.1.call-start
  7.2 14.0 %all_gather.7 = bf16[512,768]{1,0:T(8,128)(2,1)S(1)} all-gather(bf16[128,768]{1,0:T(8,128)(2,1)} %param.9), channel_id=1, replica_groups=mesh['dp'=64,'tensor'=4] {'tensor'}, dimensions={0}, use_global_device_ids=true | all-gather | bytes 983040 | tf_op jit(solution)/shard_map/all_gather | solution.py:69
  21.3 9.5 %convolution_bitcast_fusion = f32[512,4096]{0,1:T(8,128)} fusion(bf16[512,768]{1,0:T(8,128)(2,1)S(1)} %all_gather.7, f32[768]{0:T(1024)} %param.8, bf16[4096,768]{1,0:T(8,128)(2,1)} %param.7), kind=kOutput, calls=%fused_computation.5 | convolution fusion | flops 3233808384 | bytes 15469568 | tf_op jit(solution)/shard_map/dot_general | solution.py:79
  30.8 8.9 %copy.19 = f32[512,4096]{1,0:T(8,128)} copy(f32[512,4096]{0,1:T(8,128)} %convolution_bitcast_fusion) | data formatting | bytes 16777216
  39.7 0.0 reduce-scatter.7.cloned.1.call-update
  39.7 0.0 all-gather.2.cloned.1.call-start
  39.8 0.8 copy-done
  40.5 0.2 reshape.24
  40.7 0.3 convolution_bitcast_fusion.2
  41.1 0.4 convolution_multiply_fusion.1
  41.4 0.1 mul.67
  41.6 2.2 collective-permute-start
  43.7 3.2 collective-permute-done
  47.0 3.3 collective-permute-start.1
  50.3 3.2 collective-permute-done.1
  53.5 140.9 %reduce-scatter.7.cloned.1.call-done = f32[8,4096]{1,0:T(8,128)} async-done(((f32[512,4096]{1,0:T(8,128)}), f32[8,4096]{1,0:T(8,128)}) %reduce-scatter.7.cloned.1.call-update) | async-done | bytes 131088 | tf_op jit(solution)/shard_map/reduce_scatter | solution.py:78
  194.5 1.0 multiply_reduce_fusion.1
  195.4 1.6 fusion
  197.0 0.0 reduce-scatter.5.cloned.1.call-start
  197.1 0.1 reshape.25
  197.2 0.4 convolution_bitcast_fusion.1
  197.6 0.4 convolution_multiply_fusion
  198.0 0.1 mul.74
  198.1 1.7 collective-permute-start.2
  199.8 212.1 %psum.14 = f32[4096]{0:T(1024)} all-reduce(f32[4096]{0:T(1024)S(1)} %get-tuple-element.10), channel_id=1, replica_groups=mesh['dp'=64,'tensor'=4] {'dp'}, use_global_device_ids=true, to_apply=%region_3.4 | all-reduce | flops 4096 | bytes 32768 | tf_op jit(solution)/shard_map/psum | solution.py:86
  411.9 3.0 collective-permute-start.3
  414.9 8.7 %fusion.33 = f32[512,768]{1,0:T(8,128)} fusion(bf16[512,4096]{1,0:T(8,128)(2,1)} %all-gather.2.cloned.1.call-done, f32[768]{0:T(1024)S(1)} %copy-done.2, bf16[4096,768]{1,0:T(8,128)(2,1)} %param.7), kind=kOutput, calls=%fused_computation.51 | convolution fusion | flops 3233808384 | bytes 12061696 | tf_op jit(solution)/shard_map/dot_general | solution.py:64
  423.6 0.7 select_convert_fusion
  424.3 12.4 %multiply_reduce_fusion = (f32[768]{0:T(1024)S(1)}, bf16[4096,768]{1,0:T(8,128)(2,1)}) fusion(f32[768]{0:T(1024)S(1)} %copy-done.2, bf16[4096,768]{1,0:T(8,128)(2,1)} %param.7, bf16[512,4096]{1,0:T(8,128)(2,1)} %all-gather.2.cloned.1.call-done, bf16[512,768]{1,0:T(8,128)(2,1)S(1)} %all_gather.7), kind=kOutput, calls=%fused_computation | convolution fusion | flops 3252681984 | bytes 17569792 | tf_op jit(solution)/shard_map/dot_general | solution.py:70
  436.7 8.8 %psum.15 = f32[768]{0:T(1024)} all-reduce(f32[768]{0:T(1024)S(1)} %get-tuple-element.12), channel_id=1, replica_groups=mesh['dp'=64,'tensor'=4] {'tensor'}, use_global_device_ids=true, to_apply=%region_5.6 | all-reduce | flops 768 | bytes 6144 | tf_op jit(solution)/shard_map/psum | solution.py:76
  445.5 33.3 %reduce-scatter.5.cloned.1.call-done = f32[128,768]{1,0:T(8,128)} async-done(((f32[512,768]{1,0:T(8,128)}), f32[128,768]{1,0:T(8,128)}) %reduce-scatter.5.cloned.1.call-update) | async-done | bytes 393232 | tf_op jit(solution)/shard_map/reduce_scatter | solution.py:63
  478.8 1.7 convert_element_type.35
  (12 shorter events, 0.1 us)
Async XLA Ops:
  7.2 187.3 %reduce-scatter.7.cloned.1.call-start = ((), (), s32[]{:S(2)}) async-start(), calls=%async_computation.4 | async-start | bytes 8519680 | tf_op jit(solution)/shard_map/reduce_scatter | solution.py:78
  39.7 0.8 copy-start
  39.7 154.8 %copy-start.1 = (f32[4096]{0:T(1024)S(1)}, f32[4096]{0:T(1024)}, u32[]{:S(2)}) copy-start(f32[4096]{0:T(1024)} %param.6) | copy-start | bytes 49156
  39.7 375.2 %copy-start.2 = (f32[768]{0:T(1024)S(1)}, f32[768]{0:T(1024)}, u32[]{:S(2)}) copy-start(f32[768]{0:T(1024)} %param.8) | copy-start | bytes 9220
  39.7 375.2 %all-gather.2.cloned.1.call-start = ((), (), s32[]{:S(2)}) async-start(), calls=%async_computation.2 | async-start | bytes 4259840 | tf_op jit(solution)/shard_map/all_gather | solution.py:58
  41.6 5.4 %collective-permute-start = (f32[8,4096]{1,0:T(8,128)S(1)}, f32[8,4096]{1,0:T(8,128)S(1)}, u32[]{:S(2)}, u32[]{:S(2)}) collective-permute-start(f32[8,4096]{1,0:T(8,128)S(1)} %mul.67), channel_id=1, source_target_pairs={{0,1},{1,0},{2,3},{3,2},{4,5},{5,4},{6,7},{7,6},{8,9},{9,8},{10,11... | collective-permute-start | bytes 393224 | tf_op jit(solution)/shard_map/ppermute | solution.py:16
  47.0 6.6 %collective-permute-start.1 = (f32[8,4096]{1,0:T(8,128)S(1)}, f32[8,4096]{1,0:T(8,128)S(1)}, u32[]{:S(2)}, u32[]{:S(2)}) collective-permute-start(f32[8,4096]{1,0:T(8,128)S(1)} %add_select_fusion.1), channel_id=1, source_target_pairs={{0,2},{2,0},{1,3},{3,1},{4,6},{6,4},{5,7},{7,5},{8,10},{10,8},{9,1... | collective-permute-start | bytes 393224 | tf_op jit(solution)/shard_map/ppermute | solution.py:16
  197.0 281.8 %reduce-scatter.5.cloned.1.call-start = ((), (), s32[]{:S(2)}) async-start(), calls=%async_computation.3 | async-start | bytes 1966080 | tf_op jit(solution)/shard_map/reduce_scatter | solution.py:63
  198.1 213.7 %collective-permute-start.2 = (f32[8,4096]{1,0:T(8,128)S(1)}, f32[8,4096]{1,0:T(8,128)S(1)}, u32[]{:S(2)}, u32[]{:S(2)}) collective-permute-start(f32[8,4096]{1,0:T(8,128)S(1)} %mul.74), channel_id=1, source_target_pairs={{0,1},{1,0},{2,3},{3,2},{4,5},{5,4},{6,7},{7,6},{8,9},{9,8},{10,11... | collective-permute-start | bytes 393224 | tf_op jit(solution)/shard_map/ppermute | solution.py:16
  411.9 11.7 %collective-permute-start.3 = (f32[8,4096]{1,0:T(8,128)S(1)}, f32[8,4096]{1,0:T(8,128)S(1)}, u32[]{:S(2)}, u32[]{:S(2)}) collective-permute-start(f32[8,4096]{1,0:T(8,128)S(1)} %add_select_fusion), channel_id=1, source_target_pairs={{0,2},{2,0},{1,3},{3,1},{4,6},{6,4},{5,7},{7,5},{8,10},{10,8},{9,1... | collective-permute-start | bytes 393224 | tf_op jit(solution)/shard_map/ppermute | solution.py:16
Sparse Core Ops, SparseCore 0:
  39.8 154.5 reduce-scatter.6
  197.8 76.9 all-gather.1
  423.8 55.0 reduce-scatter.4
where the time goes:
time: 490 us; the launch traced here: 487 us
  blocking collectives  235 us (48%)
  waiting for transfers between devices  181 us (37%)
  matrix products  32.2 us (7%)
  between operations  13.8 us (3%)
  starting transfers between devices  10.3 us (2%)
  local copies, waits for them, and re-layouts  10.2 us (2%)
  other arithmetic  4.94 us (1%)
    psum x1, blocking collectives, body(): clip_act_grad = lax.psum(jnp.sum(act_prod * edge_act, axis=0), 'dp')  212 us
    reduce_scatter x1, waiting for transfers between devices, body(): lax.psum_scatter(lax.dot_general(block, quant_weight, (((1,), (1,)), ((),...  141 us
    reduce_scatter x1, waiting for transfers between devices, body(): lax.psum_scatter(jnp.dot(block, quant_weight, preferred_element_type=jnp....  33.3 us
    all_gather x1, blocking collectives, body(): all_cot = lax.all_gather(cotangent, 'tensor', axis=0, tiled=True)  14 us
    dot_general x1, matrix products, body(): lax.dot_general(all_act, all_cot, (((0,), (0,)), ((), ())), preferred_ele...  12.4 us
    ppermute x4, starting transfers between devices, swapped(): return lax.ppermute(block, axis, route)  10.2 us
  transfers between devices with their start and end apart: 7, of which 4 were waited for; matrix products, arithmetic and copies ran while one was open for 5% of the time, Pallas kernels for 0%

commit v1 on v0

--- a/solution.py
+++ b/solution.py
@@ -55,7 +55,7 @@
     quant_act = (clip_act * tanh_act).astype(jnp.bfloat16)
     slope_act = 1.0 - tanh_act * tanh_act
     edge_act = tanh_act - ratio_act * slope_act
-    all_act = lax.all_gather(quant_act, "dp", axis=0, tiled=True)
+    all_act = lax.all_gather(quant_act, DP, axis=0, tiled=True)
     ratio_weight = weight.astype(jnp.float32) / clip_weight
     tanh_weight = jnp.tanh(ratio_weight)
     quant_weight = (clip_weight * tanh_weight).astype(jnp.bfloat16)
@@ -78,18 +78,29 @@
     act_prod = lax.psum_scatter(
         lax.dot_general(
             block, quant_weight, (((1,), (1,)), ((), ())), preferred_element_type=jnp.float32
-        ),
-        "dp",
+        ).astype(jnp.bfloat16),
+        DP,
         scatter_dimension=0,
         tiled=True,
-    )
-    clip_act_grad = lax.psum(jnp.sum(act_prod * edge_act, axis=0), "dp")
+    ).astype(jnp.float32)
+    act_terms = jnp.sum(act_prod * edge_act, axis=0)
+    for axis in ("dc", "dx", "dz"):
+        act_terms = lax.psum(act_terms, axis)
+    clip_act_grad = act_terms
     pre_rotation = act_prod * slope_act
     token_grad = rotate(pre_rotation).astype(jnp.bfloat16)
     return (projected, token_grad, weight_grad, clip_act_grad, clip_weight_grad)
 
 
+DP = ("dx", "dz", "dc")
+
+
 def solution(mesh):
-    in_specs = (P("dp", "tensor"), P("tensor"), P("tensor", "dp"), P("dp"), P("tensor", "dp"))
-    out_specs = (P("tensor", "dp"), P("dp", "tensor"), P("tensor", "dp"), P("tensor"), P("dp"))
-    return jax.shard_map(body, mesh=mesh, in_specs=in_specs, out_specs=out_specs, check_vma=False)
+    rows, cols = mesh.devices.shape
+    cores = 2
+    across = 4 if rows % (4 * cores) == 0 else 1
+    grid = mesh.devices.reshape(across, rows // (across * cores), cores, cols)
+    fine = jax.sharding.Mesh(grid, ("dx", "dz", "dc", "tensor"))
+    in_specs = (P(DP, "tensor"), P("tensor"), P("tensor", DP), P(DP), P("tensor", DP))
+    out_specs = (P("tensor", DP), P(DP, "tensor"), P("tensor", DP), P("tensor"), P(DP))
+    return jax.shard_map(body, mesh=fine, in_specs=in_specs, out_specs=out_specs, check_vma=False)

time: 490 us -> 308 us (0.63)
  blocking collectives: 235 us -> 72.2 us
  waiting for transfers between devices: 181 us -> 168 us
    psum x1 -> x3, blocking collectives: 212 us -> 47.1 us  [body(): act_terms = lax.psum(act_terms, axis)]
    reduce_scatter x1, waiting for transfers between devices: 33.3 us -> 2.81 us  [body(): lax.psum_scatter(jnp.dot(block, quant_weight, preferred_element_type=jnp....]
    all_gather x1, waiting for transfers between devices: 0.01 us -> 25.3 us  [body(): all_act = lax.all_gather(quant_act, DP, axis=0, tiled=True)]
    reduce_scatter x1, waiting for transfers between devices: 141 us -> 134 us  [body(): lax.psum_scatter(lax.dot_general(block, quant_weight, (((1,), (1,)), ((),...]
  transfers between devices with their start and end apart: 7 -> 7, of which waited for: 4 -> 5; matrix products, arithmetic and copies ran while one was open for 5% -> 8% of each run, Pallas kernels for 0% -> 0%
where the time goes in v1:
time: 308 us; the launch traced here: 307 us
  waiting for transfers between devices  168 us (55%)
  blocking collectives  72.2 us (23%)
  matrix products  31 us (10%)
  between operations  13.8 us (4%)
  starting transfers between devices  10.2 us (3%)
  local copies, waits for them, and re-layouts  6.96 us (2%)
  other arithmetic  4.82 us (2%)
    reduce_scatter x1, waiting for transfers between devices, body(): lax.psum_scatter(lax.dot_general(block, quant_weight, (((1,), (1,)), ((),...  134 us
    psum x3, blocking collectives, body(): act_terms = lax.psum(act_terms, axis)  47.1 us
    all_gather x1, waiting for transfers between devices, body(): all_act = lax.all_gather(quant_act, DP, axis=0, tiled=True)  25.3 us
    all_gather x1, blocking collectives, body(): all_cot = lax.all_gather(cotangent, 'tensor', axis=0, tiled=True)  14 us
    dot_general x1, matrix products, body(): lax.dot_general(all_act, all_cot, (((0,), (0,)), ((), ())), preferred_ele...  12.4 us
    psum x1, blocking collectives, body(): clip_weight_grad = lax.psum(weight_terms, 'tensor')  11 us
    ppermute x4, starting transfers between devices, swapped(): return lax.ppermute(block, axis, route)  10.1 us
    dot_general x1, matrix products, body(): jnp.dot(block, quant_weight, preferred_element_type=jnp.float32)  8.71 us
  transfers between devices with their start and end apart: 7, of which 5 were waited for; matrix products, arithmetic and copies ran while one was open for 8% of the time, Pallas kernels for 0%

profile of v1, /device:TPU:2, one launch (start us, length us, event | category | flops | bytes accessed | tf_op | source)
XLA Modules:
  0.0 307.3 jit_solution(14311970619142982010)
XLA Ops:
  7.2 14.0 %all_gather.7 = bf16[512,768]{1,0:T(8,128)(2,1)S(1)} all-gather(bf16[128,768]{1,0:T(8,128)(2,1)} %param.9), channel_id=1, replica_groups=mesh['dx'=4,'dz'=8,'dc'=2,'tensor'=4] {'tensor'}, dimensions={0}, use_global_device_ids=true | all-gather | bytes 983040 | tf_op jit(solution)/shard_map/all_gather | solution.py:69
  21.3 8.3 %fusion = bf16[512,4096]{0,1:T(8,128)(2,1)} fusion(bf16[512,768]{1,0:T(8,128)(2,1)S(1)} %all_gather.7, f32[768]{0:T(1024)} %param.8, bf16[4096,768]{1,0:T(8,128)(2,1)} %param.7), kind=kOutput, calls=%fused_computation.6 | convolution fusion | flops 3235905536 | bytes 11275264 | tf_op jit(solution)/shard_map/dot_general | solution.py:79
  29.6 6.4 %copy.18 = bf16[512,4096]{1,0:T(8,128)(2,1)} copy(bf16[512,4096]{0,1:T(8,128)(2,1)} %fusion) | data formatting | bytes 8388608
  36.0 0.0 all-gather.2.cloned.1.call-start
  36.1 0.2 reshape.24
  36.3 0.3 convolution_bitcast_fusion.1
  36.6 0.4 convolution_multiply_fusion.1
  37.0 0.1 mul.67
  37.1 2.2 collective-permute-start
  39.3 3.2 %collective-permute-done = f32[8,4096]{1,0:T(8,128)S(1)} collective-permute-done((f32[8,4096]{1,0:T(8,128)S(1)}, f32[8,4096]{1,0:T(8,128)S(1)}, u32[]{:S(2)}, u32[]{:S(2)}) %collective-permute-start) | collective-permute-done | bytes 131104 | tf_op jit(solution)/shard_map/ppermute | solution.py:16
  42.5 3.3 %collective-permute-start.1 = (f32[8,4096]{1,0:T(8,128)S(1)}, f32[8,4096]{1,0:T(8,128)S(1)}, u32[]{:S(2)}, u32[]{:S(2)}) collective-permute-start(f32[8,4096]{1,0:T(8,128)S(1)} %add_select_fusion.1), channel_id=1, source_target_pairs={{0,2},{2,0},{1,3},{3,1},{4,6},{6,4},{5,7},{7,5},{8,10},{10,8},{9,1... | collective-permute-start | bytes 393224 | tf_op jit(solution)/shard_map/ppermute | solution.py:16
  45.9 3.2 %collective-permute-done.1 = f32[8,4096]{1,0:T(8,128)S(1)} collective-permute-done((f32[8,4096]{1,0:T(8,128)S(1)}, f32[8,4096]{1,0:T(8,128)S(1)}, u32[]{:S(2)}, u32[]{:S(2)}) %collective-permute-start.1) | collective-permute-done | bytes 131104 | tf_op jit(solution)/shard_map/ppermute | solution.py:16
  49.1 133.8 %reduce-scatter.7.cloned.1.call-done = bf16[8,4096]{1,0:T(8,128)(2,1)} async-done(((bf16[512,4096]{1,0:T(8,128)(2,1)}), bf16[8,4096]{1,0:T(8,128)(2,1)}) %reduce-scatter.7.cloned.1.call-update) | async-done | bytes 65552 | tf_op jit(solution)/shard_map/reduce_scatter | solution.py:78
  182.9 0.9 fusion.1
  183.8 1.5 convert_multiply_fusion.1
  185.3 0.0 reduce-scatter.5.cloned.1.call-start
  185.4 0.1 reshape.25
  185.5 0.4 convolution_bitcast_fusion
  185.9 0.4 convolution_multiply_fusion
  186.3 0.1 mul.74
  186.4 1.6 collective-permute-start.2
  188.0 3.3 %psum.28 = f32[4096]{0:T(1024)S(1)} all-reduce(f32[4096]{0:T(1024)S(1)} %get-tuple-element.10), channel_id=1, replica_groups=mesh['dx'=4,'dz'=8,'dc'=2,'tensor'=4] {'dc'}, use_global_device_ids=true, to_apply=%region_3.4 | all-reduce | flops 4096 | bytes 32768 | tf_op jit(solution)/shard_map/psum | solution.py:88
  191.3 14.4 %psum.29 = f32[4096]{0:T(1024)S(1)} all-reduce(f32[4096]{0:T(1024)S(1)} %psum.28), channel_id=1, replica_groups=mesh['dx'=4,'dz'=8,'dc'=2,'tensor'=4] {'dx'}, use_global_device_ids=true, to_apply=%region_4.5 | all-reduce | flops 4096 | bytes 32768 | tf_op jit(solution)/shard_map/psum | solution.py:88
  205.7 29.3 %psum.30 = f32[4096]{0:T(1024)} all-reduce(f32[4096]{0:T(1024)S(1)} %psum.29), channel_id=1, replica_groups=mesh['dx'=4,'dz'=8,'dc'=2,'tensor'=4] {'dz'}, use_global_device_ids=true, to_apply=%region_5.6 | all-reduce | flops 4096 | bytes 32768 | tf_op jit(solution)/shard_map/psum | solution.py:88
  235.1 3.0 collective-permute-start.3
  238.1 25.3 %all-gather.2.cloned.1.call-done = bf16[512,4096]{1,0:T(8,128)(2,1)} async-done(((bf16[8,4096]{1,0:T(8,128)(2,1)}), bf16[512,4096]{1,0:T(8,128)(2,1)}) %all-gather.2.cloned.1.call-update) | async-done | bytes 4194320 | tf_op jit(solution)/shard_map/all_gather | solution.py:58
  263.4 8.7 %fusion.34 = f32[512,768]{1,0:T(8,128)} fusion(bf16[512,4096]{1,0:T(8,128)(2,1)} %all-gather.2.cloned.1.call-done, f32[768]{0:T(1024)S(1)} %copy-done.2, bf16[4096,768]{1,0:T(8,128)(2,1)} %param.7), kind=kOutput, calls=%fused_computation.53 | convolution fusion | flops 3233808384 | bytes 12061696 | tf_op jit(solution)/shard_map/dot_general | solution.py:64
  272.1 0.7 select_convert_fusion
  272.8 12.4 %multiply_reduce_fusion = (f32[768]{0:T(1024)S(1)}, bf16[4096,768]{1,0:T(8,128)(2,1)}) fusion(f32[768]{0:T(1024)S(1)} %copy-done.2, bf16[4096,768]{1,0:T(8,128)(2,1)} %param.7, bf16[512,4096]{1,0:T(8,128)(2,1)} %all-gather.2.cloned.1.call-done, bf16[512,768]{1,0:T(8,128)(2,1)S(1)} %all_gather.7), kind=kOutput, calls=%fused_computation | convolution fusion | flops 3252681984 | bytes 17569792 | tf_op jit(solution)/shard_map/dot_general | solution.py:70
  285.2 11.0 %psum.31 = f32[768]{0:T(1024)} all-reduce(f32[768]{0:T(1024)S(1)} %get-tuple-element.12), channel_id=1, replica_groups=mesh['dx'=4,'dz'=8,'dc'=2,'tensor'=4] {'tensor'}, use_global_device_ids=true, to_apply=%region_7.8 | all-reduce | flops 768 | bytes 6144 | tf_op jit(solution)/shard_map/psum | solution.py:76
  296.3 2.8 reduce-scatter.5.cloned.1.call-done
  299.1 1.7 convert_element_type.44
  (14 shorter events, 0.1 us)
Async XLA Ops:
  7.2 175.7 %reduce-scatter.7.cloned.1.call-start = ((), (), s32[]{:S(2)}) async-start(), calls=%async_computation.4 | async-start | bytes 4259840 | tf_op jit(solution)/shard_map/reduce_scatter | solution.py:78
  29.5 6.5 %copy-start = (bf16[8,4096]{1,0:T(8,128)(2,1)S(1)}, bf16[8,4096]{1,0:T(8,128)(2,1)}, u32[]{:S(2)}) copy-start(bf16[8,4096]{1,0:T(8,128)(2,1)} %param.5) | copy-start | bytes 196612
  29.6 153.3 %copy-start.1 = (f32[4096]{0:T(1024)S(1)}, f32[4096]{0:T(1024)}, u32[]{:S(2)}) copy-start(f32[4096]{0:T(1024)} %param.6) | copy-start | bytes 49156
  36.0 227.4 %copy-start.2 = (f32[768]{0:T(1024)S(1)}, f32[768]{0:T(1024)}, u32[]{:S(2)}) copy-start(f32[768]{0:T(1024)} %param.8) | copy-start | bytes 9220
  36.0 227.4 %all-gather.2.cloned.1.call-start = ((), (), s32[]{:S(2)}) async-start(), calls=%async_computation.2 | async-start | bytes 4259840 | tf_op jit(solution)/shard_map/all_gather | solution.py:58
  37.1 5.4 %collective-permute-start = (f32[8,4096]{1,0:T(8,128)S(1)}, f32[8,4096]{1,0:T(8,128)S(1)}, u32[]{:S(2)}, u32[]{:S(2)}) collective-permute-start(f32[8,4096]{1,0:T(8,128)S(1)} %mul.67), channel_id=1, source_target_pairs={{0,1},{1,0},{2,3},{3,2},{4,5},{5,4},{6,7},{7,6},{8,9},{9,8},{10,11... | collective-permute-start | bytes 393224 | tf_op jit(solution)/shard_map/ppermute | solution.py:16
  42.5 6.6 %collective-permute-start.1 = (f32[8,4096]{1,0:T(8,128)S(1)}, f32[8,4096]{1,0:T(8,128)S(1)}, u32[]{:S(2)}, u32[]{:S(2)}) collective-permute-start(f32[8,4096]{1,0:T(8,128)S(1)} %add_select_fusion.1), channel_id=1, source_target_pairs={{0,2},{2,0},{1,3},{3,1},{4,6},{6,4},{5,7},{7,5},{8,10},{10,8},{9,1... | collective-permute-start | bytes 393224 | tf_op jit(solution)/shard_map/ppermute | solution.py:16
  185.3 113.8 %reduce-scatter.5.cloned.1.call-start = ((), (), s32[]{:S(2)}) async-start(), calls=%async_computation.3 | async-start | bytes 1966080 | tf_op jit(solution)/shard_map/reduce_scatter | solution.py:63
  186.4 48.7 %collective-permute-start.2 = (f32[8,4096]{1,0:T(8,128)S(1)}, f32[8,4096]{1,0:T(8,128)S(1)}, u32[]{:S(2)}, u32[]{:S(2)}) collective-permute-start(f32[8,4096]{1,0:T(8,128)S(1)} %mul.74), channel_id=1, source_target_pairs={{0,1},{1,0},{2,3},{3,2},{4,5},{5,4},{6,7},{7,6},{8,9},{9,8},{10,11... | collective-permute-start | bytes 393224 | tf_op jit(solution)/shard_map/ppermute | solution.py:16
  235.1 37.1 %collective-permute-start.3 = (f32[8,4096]{1,0:T(8,128)S(1)}, f32[8,4096]{1,0:T(8,128)S(1)}, u32[]{:S(2)}, u32[]{:S(2)}) collective-permute-start(f32[8,4096]{1,0:T(8,128)S(1)} %add_select_fusion), channel_id=1, source_target_pairs={{0,2},{2,0},{1,3},{3,1},{4,6},{6,4},{5,7},{7,5},{8,10},{10,8},{9,1... | collective-permute-start | bytes 393224 | tf_op jit(solution)/shard_map/ppermute | solution.py:16
Sparse Core Ops, SparseCore 0:
  36.1 146.6 reduce-scatter.6
  186.2 77.1 all-gather.1
  272.3 26.7 reduce-scatter.4

commit v2 on v1

--- a/solution.py
+++ b/solution.py
@@ -55,7 +55,15 @@
     quant_act = (clip_act * tanh_act).astype(jnp.bfloat16)
     slope_act = 1.0 - tanh_act * tanh_act
     edge_act = tanh_act - ratio_act * slope_act
-    all_act = lax.all_gather(quant_act, DP, axis=0, tiled=True)
+    rows, width = quant_act.shape
+    chips = lax.axis_size("dx") * lax.axis_size("dz")
+    cores = lax.axis_size("dc")
+    core = lax.axis_index("dc")
+    half_act = lax.all_gather(quant_act, CHIPS, axis=0, tiled=True)
+    both_act = lax.all_gather(half_act, "dc", axis=0, tiled=False)
+    all_act = (
+        both_act.reshape(cores, chips, rows, width).transpose(1, 0, 2, 3).reshape(-1, width)
+    )
     ratio_weight = weight.astype(jnp.float32) / clip_weight
     tanh_weight = jnp.tanh(ratio_weight)
     quant_weight = (clip_weight * tanh_weight).astype(jnp.bfloat16)
@@ -75,24 +83,24 @@
     weight_terms = jnp.sum(weight_prod * (tanh_weight - ratio_weight * slope_weight), axis=0)
     clip_weight_grad = lax.psum(weight_terms, "tensor")
     block = all_cot
-    act_prod = lax.psum_scatter(
-        lax.dot_general(
-            block, quant_weight, (((1,), (1,)), ((), ())), preferred_element_type=jnp.float32
-        ).astype(jnp.bfloat16),
-        DP,
-        scatter_dimension=0,
-        tiled=True,
-    ).astype(jnp.float32)
-    act_terms = jnp.sum(act_prod * edge_act, axis=0)
-    for axis in ("dc", "dx", "dz"):
-        act_terms = lax.psum(act_terms, axis)
-    clip_act_grad = act_terms
+    partial = lax.dot_general(
+        block, quant_weight, (((1,), (1,)), ((), ())), preferred_element_type=jnp.float32
+    ).reshape(chips, cores, rows, width)
+    mine = lax.dynamic_index_in_dim(partial, core, axis=1, keepdims=False)
+    other = lax.dynamic_index_in_dim(partial, cores - 1 - core, axis=1, keepdims=False)
+    pair = [(0, 1), (1, 0)]
+    chip_sum = mine + lax.ppermute(other.astype(jnp.bfloat16), "dc", pair).astype(jnp.float32)
+    pieces = lax.all_to_all(chip_sum.astype(jnp.bfloat16), CHIPS, 0, 0, tiled=True)
+    act_prod = jnp.sum(pieces.astype(jnp.float32), axis=0)
+    act_terms = lax.psum(jnp.sum(act_prod * edge_act, axis=0), "dc")
+    clip_act_grad = jnp.sum(lax.all_gather(act_terms, CHIPS, axis=0, tiled=False), axis=0)
     pre_rotation = act_prod * slope_act
     token_grad = rotate(pre_rotation).astype(jnp.bfloat16)
     return (projected, token_grad, weight_grad, clip_act_grad, clip_weight_grad)
 
 
 DP = ("dx", "dz", "dc")
+CHIPS = ("dx", "dz")
 
 
 def solution(mesh):

time: 308 us -> 282 us (0.916)
  waiting for transfers between devices: 168 us -> 127 us
  starting transfers between devices: 10.2 us -> 21.3 us
  other arithmetic: 4.82 us -> 14.5 us
  matrix products: 31 us -> 22 us
    reduce_scatter x1 -> x0, waiting for transfers between devices: 134 us -> none  [body(): lax.psum_scatter(lax.dot_general(block, quant_weight, (((1,), (1,)), ((),...]
    all_gather x1 -> x2, waiting for transfers between devices: 25.3 us -> 76.9 us  [the longest x1 76.9 us: body(): half_act = lax.all_gather(quant_act, CHIPS, axis=0, tiled=True)]
    all_gather x0 -> x1, blocking collectives: none -> 48 us  [body(): lax.all_gather(act_terms, CHIPS, axis=0, tiled=False)]
    psum x3 -> x1, blocking collectives: 47.1 us -> 3.94 us  [body(): act_terms = lax.psum(jnp.sum(act_prod * edge_act, axis=0), 'dc')]
    all_to_all x0 -> x1, waiting for transfers between devices: none -> 38.5 us  [body(): lax.all_to_all(chip_sum.astype(jnp.bfloat16), CHIPS, 0, 0, tiled=True)]
    all_to_all x0 -> x1, starting transfers between devices: none -> 11.6 us  [body(): lax.all_to_all(chip_sum.astype(jnp.bfloat16), CHIPS, 0, 0, tiled=True)]
    convert_element_type x0 -> x2, other arithmetic: none -> 9.22 us  [the longest x1 4.72 us: body(): chip_sum.astype(jnp.bfloat16)]
    dot_general x1, matrix products: 8.29 us -> 3.45 us  [body(): lax.dot_general(block, quant_weight, (((1,), (1,)), ((), ())), preferred_...]
  transfers between devices with their start and end apart: 7 -> 9, of which waited for: 5 -> 5; matrix products, arithmetic and copies ran while one was open for 8% -> 9% of each run, Pallas kernels for 0% -> 0%
where the time goes in v2:
time: 282 us
  waiting for transfers between devices  127 us (45%)
  blocking collectives  74.7 us (26%)
  matrix products  22 us (8%)
  starting transfers between devices  21.3 us (8%)
  other arithmetic  14.5 us (5%)
  between operations  13.9 us (5%)
  local copies, waits for them, and re-layouts  8.58 us (3%)
    all_gather x1, waiting for transfers between devices, body(): half_act = lax.all_gather(quant_act, CHIPS, axis=0, tiled=True)  76.9 us
    all_gather x1, blocking collectives, body(): lax.all_gather(act_terms, CHIPS, axis=0, tiled=False)  48 us
    all_to_all x1, waiting for transfers between devices, body(): lax.all_to_all(chip_sum.astype(jnp.bfloat16), CHIPS, 0, 0, tiled=True)  38.5 us
    all_gather x1, blocking collectives, body(): all_cot = lax.all_gather(cotangent, 'tensor', axis=0, tiled=True)  14 us
    dot_general x1, matrix products, body(): lax.dot_general(all_act, all_cot, (((0,), (0,)), ((), ())), preferred_ele...  12.4 us
    all_to_all x1, starting transfers between devices, body(): lax.all_to_all(chip_sum.astype(jnp.bfloat16), CHIPS, 0, 0, tiled=True)  11.6 us
    ppermute x4, starting transfers between devices, swapped(): return lax.ppermute(block, axis, route)  9.49 us
    psum x1, blocking collectives, body(): clip_weight_grad = lax.psum(weight_terms, 'tensor')  8.78 us
  transfers between devices with their start and end apart: 9, of which 5 were waited for; matrix products, arithmetic and copies ran while one was open for 9% of the time, Pallas kernels for 0%

profile of v2, /device:TPU:2, one launch (start us, length us, event | category | flops | bytes accessed | tf_op | source)
XLA Modules:
  0.0 281.8 jit_solution(9901720379922243371)
XLA Ops:
  7.2 14.0 %all_gather.21 = bf16[512,768]{1,0:T(8,128)(2,1)S(1)} all-gather(bf16[128,768]{1,0:T(8,128)(2,1)} %param.9), channel_id=1, replica_groups=mesh['dx'=4,'dz'=8,'dc'=2,'tensor'=4] {'tensor'}, dimensions={0}, use_global_device_ids=true | all-gather | bytes 983040 | tf_op jit(solution)/shard_map/all_gather | solution.py:77
  21.2 4.5 %multiply_convert_fusion.1 = bf16[4096,768]{1,0:T(8,128)(2,1)S(1)} fusion(f32[768]{0:T(1024)} %param.8, bf16[4096,768]{1,0:T(8,128)(2,1)} %param.7), kind=kLoop, calls=%fused_computation.3 | loop fusion | flops 12582912 | bytes 12585984 | tf_op jit(solution)/shard_map/convert_element_type | solution.py:69
  25.7 3.5 %fusion.36 = f32[4096,512]{0,1:T(8,128)S(1)} fusion(bf16[4096,768]{1,0:T(8,128)(2,1)S(1)} %multiply_convert_fusion.1, bf16[512,768]{1,0:T(8,128)(2,1)S(1)} %all_gather.21), kind=kOutput, calls=%fused_computation.56 | convolution fusion | flops 3221225472 | bytes 15466496 | tf_op jit(solution)/shard_map/dot_general | solution.py:86
  29.2 3.2 %copy-done.1 = f32[4096,512]{0,1:T(8,128)} copy-done((f32[4096,512]{0,1:T(8,128)}, f32[4096,512]{0,1:T(8,128)S(1)}, u32[]{:S(2)}) %copy-start.1) | copy-done | bytes 8388632
  32.8 4.3 %collective-permute-done.2 = bf16[32,8,4096]{2,1,0:T(8,128)(2,1)} collective-permute-done((bf16[32,8,4096]{2,1,0:T(8,128)(2,1)S(1)}, bf16[32,8,4096]{2,1,0:T(8,128)(2,1)}, u32[]{:S(2)}, u32[]{:S(2)}) %collective-permute-start.2) | collective-permute-done | bytes 2097184 | tf_op jit(solution)/shard_map/ppermute | solution.py:92
  37.1 4.7 %fusion = bf16[32,8,4096]{2,1,0:T(8,128)(2,1)} fusion(bf16[32,8,4096]{2,1,0:T(8,128)(2,1)} %collective-permute-done.2, f32[32,2,8,4096]{3,2,1,0:T(8,128)} %bitcast.43, s32[]{:T(128)S(6)} %select_n.33), kind=kLoop, calls=%fused_computation.6 | loop fusion | flops 3145728 | bytes 8388612 | tf_op jit(solution)/shard_map/convert_element_type | solution.py:93
  41.8 11.6 %all-to-all-start = ((bf16[32,8,4096]{2,1,0:T(8,128)(2,1)}), bf16[32,8,4096]{2,1,0:T(8,128)(2,1)S(1)}, u32[]{:S(2)}, u32[]{:S(2)}) async-start(bf16[32,8,4096]{2,1,0:T(8,128)(2,1)} %fusion), calls=%async_computation.1 | async-start | bytes 4194304 | tf_op jit(solution)/shard_map/all_to_all | solution.py:93
  53.7 0.3 convolution_bitcast_fusion.1
  54.0 0.4 convolution_multiply_fusion.1
  54.5 2.2 collective-permute-start
  56.7 3.2 %collective-permute-done = f32[8,4096]{1,0:T(8,128)S(1)} collective-permute-done((f32[8,4096]{1,0:T(8,128)S(1)}, f32[8,4096]{1,0:T(8,128)S(1)}, u32[]{:S(2)}, u32[]{:S(2)}) %collective-permute-start) | collective-permute-done | bytes 131104 | tf_op jit(solution)/shard_map/ppermute | solution.py:16
  60.0 2.7 collective-permute-start.1
  62.7 38.5 %all-to-all-done = bf16[32,8,4096]{2,1,0:T(8,128)(2,1)S(1)} async-done(((bf16[32,8,4096]{2,1,0:T(8,128)(2,1)}), bf16[32,8,4096]{2,1,0:T(8,128)(2,1)S(1)}, u32[]{:S(2)}, u32[]{:S(2)}) %all-to-all-start) | async-done | bytes 2097184 | tf_op jit(solution)/shard_map/all_to_all | solution.py:93
  101.3 0.3 convert_reduce_fusion
  101.7 0.7 fusion.2
  102.4 76.9 %all-gather.5.cloned.1.call-done = bf16[256,4096]{1,0:T(8,128)(2,1)} async-done(((bf16[8,4096]{1,0:T(8,128)(2,1)}), bf16[256,4096]{1,0:T(8,128)(2,1)}) %all-gather.5.cloned.1.call-update) | async-done | bytes 2097168 | tf_op jit(solution)/shard_map/all_gather | solution.py:62
  179.5 0.4 convolution_bitcast_fusion
  180.0 0.4 convolution_multiply_fusion
  180.5 1.6 collective-permute-start.3
  182.0 3.9 %psum.14 = f32[1,4096]{1,0:T(1,128)} all-reduce(f32[1,4096]{1,0:T(1,128)S(1)} %bitcast.47), channel_id=1, replica_groups=mesh['dx'=4,'dz'=8,'dc'=2,'tensor'=4] {'dc'}, use_global_device_ids=true, to_apply=%region_3.4 | all-reduce | flops 4096 | bytes 32768 | tf_op jit(solution)/shard_map/psum | solution.py:95
  186.0 48.0 %all-gather.1 = f32[32,1,4096]{2,1,0:T(1,128)S(1)} all-gather(f32[1,1,4096]{2,1,0:T(1,128)} %bitcast.48), channel_id=1, replica_groups=mesh['dx'=4,'dz'=8,'dc'=2,'tensor'=4] {'dx','dz'}, dimensions={0}, use_global_device_ids=true | all-gather | bytes 540672 | tf_op jit(solution)/shard_map/all_gather | solution.py:96
  234.0 1.0 reduce_sum.38
  235.0 0.9 add_select_fusion
  235.9 3.0 %collective-permute-start.4 = (f32[8,4096]{1,0:T(8,128)S(1)}, f32[8,4096]{1,0:T(8,128)S(1)}, u32[]{:S(2)}, u32[]{:S(2)}) collective-permute-start(f32[8,4096]{1,0:T(8,128)S(1)} %add_select_fusion), channel_id=1, source_target_pairs={{0,2},{2,0},{1,3},{3,1},{4,6},{6,4},{5,7},{7,5},{8,10},{10,8},{9,1... | collective-permute-start | bytes 393224 | tf_op jit(solution)/shard_map/ppermute | solution.py:16
  238.9 2.6 copy.14
  241.5 1.9 copy-done.2
  243.4 4.6 %fusion.35 = f32[512,768]{1,0:T(8,128)} fusion(bf16[512,4096]{1,0:T(8,128)(2,1)S(1)} %bitcast.45, bf16[4096,768]{1,0:T(8,128)(2,1)S(1)} %bitcast.41), kind=kOutput, calls=%fused_computation.55 | convolution fusion | flops 3221225472 | bytes 12058624 | tf_op jit(solution)/shard_map/dot_general | solution.py:72
  248.1 0.7 select_convert_fusion
  248.7 12.4 %multiply_reduce_fusion = (f32[768]{0:T(1024)S(1)}, bf16[4096,768]{1,0:T(8,128)(2,1)}) fusion(f32[768]{0:T(1024)S(1)} %copy-done.5, bf16[4096,768]{1,0:T(8,128)(2,1)} %param.7, bf16[512,4096]{1,0:T(8,128)(2,1)} %bitcast.46, bf16[512,768]{1,0:T(8,128)(2,1)S(1)} %all_gather.21), kind=kOutput, calls=%fused_computation | convolution fusion | flops 3252681984 | bytes 17569792 | tf_op jit(solution)/shard_map/dot_general | solution.py:78
  261.2 8.8 %psum.15 = f32[768]{0:T(1024)} all-reduce(f32[768]{0:T(1024)S(1)} %get-tuple-element.7), channel_id=1, replica_groups=mesh['dx'=4,'dz'=8,'dc'=2,'tensor'=4] {'tensor'}, use_global_device_ids=true, to_apply=%region_6.7 | all-reduce | flops 768 | bytes 6144 | tf_op jit(solution)/shard_map/psum | solution.py:84
  270.0 3.7 %reduce-scatter.2.cloned.1.call-done = f32[128,768]{1,0:T(8,128)} async-done(((f32[512,768]{1,0:T(8,128)}), f32[128,768]{1,0:T(8,128)}) %reduce-scatter.2.cloned.1.call-update) | async-done | bytes 393232 | tf_op jit(solution)/shard_map/reduce_scatter | solution.py:71
  273.6 1.7 convert_element_type.50
  (33 shorter events, 1.2 us)
Async XLA Ops:
  25.7 3.5 %copy-start = (bf16[4096,768]{1,0:T(8,128)(2,1)}, bf16[4096,768]{1,0:T(8,128)(2,1)S(1)}, u32[]{:S(2)}) copy-start(bf16[4096,768]{1,0:T(8,128)(2,1)S(1)} %multiply_convert_fusion.1) | copy-start | bytes 18874372
  29.2 3.2 %copy-start.1 = (f32[4096,512]{0,1:T(8,128)}, f32[4096,512]{0,1:T(8,128)S(1)}, u32[]{:S(2)}) copy-start(f32[4096,512]{0,1:T(8,128)S(1)} %fusion.36) | copy-start | bytes 25165828
  32.7 4.4 %collective-permute-start.2 = (bf16[32,8,4096]{2,1,0:T(8,128)(2,1)S(1)}, bf16[32,8,4096]{2,1,0:T(8,128)(2,1)}, u32[]{:S(2)}, u32[]{:S(2)}) collective-permute-start(bf16[32,8,4096]{2,1,0:T(8,128)(2,1)S(1)} %fusion.1), channel_id=1, source_target_pairs={{0,4},{4,0},{1,5},{5,1},{2,6},{6,2},{3,7},{7,3},{8,12},{12,8},{9,1... | collective-permute-start | bytes 6291464 | tf_op jit(solution)/shard_map/ppermute | solution.py:92
  32.8 20.7 %copy-start.3 = (bf16[8,4096]{1,0:T(8,128)(2,1)S(1)}, bf16[8,4096]{1,0:T(8,128)(2,1)}, u32[]{:S(2)}) copy-start(bf16[8,4096]{1,0:T(8,128)(2,1)} %param.5) | copy-start | bytes 196612
  32.8 68.7 %copy-start.4 = (f32[4096]{0:T(1024)S(1)}, f32[4096]{0:T(1024)}, u32[]{:S(2)}) copy-start(f32[4096]{0:T(1024)} %param.6) | copy-start | bytes 49156
  41.8 59.5 %all-to-all-start = ((bf16[32,8,4096]{2,1,0:T(8,128)(2,1)}), bf16[32,8,4096]{2,1,0:T(8,128)(2,1)S(1)}, u32[]{:S(2)}, u32[]{:S(2)}) async-start(bf16[32,8,4096]{2,1,0:T(8,128)(2,1)} %fusion), calls=%async_computation.1 | async-start | bytes 4194304 | tf_op jit(solution)/shard_map/all_to_all | solution.py:93
  53.4 125.9 %all-gather.5.cloned.1.call-start = ((), (), s32[]{:S(2)}) async-start(), calls=%async_computation.2 | async-start | bytes 2162688 | tf_op jit(solution)/shard_map/all_gather | solution.py:62
  54.5 5.4 %collective-permute-start = (f32[8,4096]{1,0:T(8,128)S(1)}, f32[8,4096]{1,0:T(8,128)S(1)}, u32[]{:S(2)}, u32[]{:S(2)}) collective-permute-start(f32[8,4096]{1,0:T(8,128)S(1)} %mul.67), channel_id=1, source_target_pairs={{0,1},{1,0},{2,3},{3,2},{4,5},{5,4},{6,7},{7,6},{8,9},{9,8},{10,11... | collective-permute-start | bytes 393224 | tf_op jit(solution)/shard_map/ppermute | solution.py:16
  60.0 41.6 %collective-permute-start.1 = (f32[8,4096]{1,0:T(8,128)S(1)}, f32[8,4096]{1,0:T(8,128)S(1)}, u32[]{:S(2)}, u32[]{:S(2)}) collective-permute-start(f32[8,4096]{1,0:T(8,128)S(1)} %add_select_fusion.1), channel_id=1, source_target_pairs={{0,2},{2,0},{1,3},{3,1},{4,6},{6,4},{5,7},{7,5},{8,10},{10,8},{9,1... | collective-permute-start | bytes 393224 | tf_op jit(solution)/shard_map/ppermute | solution.py:16
  102.4 136.5 %all-gather.7.cloned.1.call-start = ((), (), s32[]{:S(2)}) async-start(), calls=%async_computation.4 | async-start | bytes 6291456 | tf_op jit(solution)/shard_map/all_gather | solution.py:63
  179.4 64.0 %slice-start = ((s8[6291456]{0:T(1024)(128)(4,1)}), s8[2097152]{0:T(1024)(128)(4,1)S(1)}, s32[]{:S(2)}) async-start(s8[6291456]{0:T(1024)(128)(4,1)} %bitcast.40), calls=%async_computation.5 | async-start | bytes 4194304
  179.4 94.2 %reduce-scatter.2.cloned.1.call-start = ((), (), s32[]{:S(2)}) async-start(), calls=%async_computation.3 | async-start | bytes 1966080 | tf_op jit(solution)/shard_map/reduce_scatter | solution.py:71
  180.5 54.5 %collective-permute-start.3 = (f32[8,4096]{1,0:T(8,128)S(1)}, f32[8,4096]{1,0:T(8,128)}, u32[]{:S(2)}, u32[]{:S(2)}) collective-permute-start(f32[8,4096]{1,0:T(8,128)S(1)} %mul.74), channel_id=1, source_target_pairs={{0,1},{1,0},{2,3},{3,2},{4,5},{5,4},{6,7},{7,6},{8,9},{9,8},{10,11... | collective-permute-start | bytes 393224 | tf_op jit(solution)/shard_map/ppermute | solution.py:16
  235.9 12.2 %collective-permute-start.4 = (f32[8,4096]{1,0:T(8,128)S(1)}, f32[8,4096]{1,0:T(8,128)S(1)}, u32[]{:S(2)}, u32[]{:S(2)}) collective-permute-start(f32[8,4096]{1,0:T(8,128)S(1)} %add_select_fusion), channel_id=1, source_target_pairs={{0,2},{2,0},{1,3},{3,1},{4,6},{6,4},{5,7},{7,5},{8,10},{10,8},{9,1... | collective-permute-start | bytes 393224 | tf_op jit(solution)/shard_map/ppermute | solution.py:16
  238.9 4.6 %slice-start.1 = ((s8[6291456]{0:T(1024)(128)(4,1)}), s8[4194304]{0:T(1024)(128)(4,1)S(1)}, s32[]{:S(2)}) async-start(s8[6291456]{0:T(1024)(128)(4,1)} %bitcast.40), calls=%async_computation.6 | async-start | bytes 8388608
  241.5 1.9 copy-start.2
  243.4 5.3 %copy-start.5 = (f32[768]{0:T(1024)S(1)}, f32[768]{0:T(1024)}, u32[]{:S(2)}) copy-start(f32[768]{0:T(1024)} %param.8) | copy-start | bytes 9220
Sparse Core Ops, SparseCore 0:
  102.5 76.8 all-gather.4
  181.1 17.4 all-gather.6
  248.2 25.3 reduce-scatter.1

commit v3 on v2

--- a/solution.py
+++ b/solution.py
@@ -59,14 +59,23 @@
     chips = lax.axis_size("dx") * lax.axis_size("dz")
     cores = lax.axis_size("dc")
     core = lax.axis_index("dc")
+    ratio_weight = weight.astype(jnp.float32) / clip_weight
+    tanh_weight = jnp.tanh(ratio_weight)
+    quant_weight = (clip_weight * tanh_weight).astype(jnp.bfloat16)
+    all_cot = lax.all_gather(cotangent, "tensor", axis=0, tiled=True)
+    partial = lax.dot_general(
+        all_cot, quant_weight, (((1,), (1,)), ((), ())), preferred_element_type=jnp.float32
+    ).reshape(chips, cores, rows, width)
+    quant_act, partial = lax.optimization_barrier((quant_act, partial))
     half_act = lax.all_gather(quant_act, CHIPS, axis=0, tiled=True)
-    both_act = lax.all_gather(half_act, "dc", axis=0, tiled=False)
+    pair = [(0, 1), (1, 0)]
+    partner_act = lax.ppermute(half_act, "dc", pair)
+    both_act = jnp.where(
+        core == 0, jnp.stack([half_act, partner_act]), jnp.stack([partner_act, half_act])
+    )
     all_act = (
         both_act.reshape(cores, chips, rows, width).transpose(1, 0, 2, 3).reshape(-1, width)
     )
-    ratio_weight = weight.astype(jnp.float32) / clip_weight
-    tanh_weight = jnp.tanh(ratio_weight)
-    quant_weight = (clip_weight * tanh_weight).astype(jnp.bfloat16)
     block = all_act
     projected = lax.psum_scatter(
         jnp.dot(block, quant_weight, preferred_element_type=jnp.float32),
@@ -74,7 +83,6 @@
         scatter_dimension=0,
         tiled=True,
     ).astype(jnp.bfloat16)
-    all_cot = lax.all_gather(cotangent, "tensor", axis=0, tiled=True)
     weight_prod = lax.dot_general(
         all_act, all_cot, (((0,), (0,)), ((), ())), preferred_element_type=jnp.float32
     )
@@ -82,18 +90,17 @@
     weight_grad = (weight_prod * slope_weight).astype(jnp.bfloat16)
     weight_terms = jnp.sum(weight_prod * (tanh_weight - ratio_weight * slope_weight), axis=0)
     clip_weight_grad = lax.psum(weight_terms, "tensor")
-    block = all_cot
-    partial = lax.dot_general(
-        block, quant_weight, (((1,), (1,)), ((), ())), preferred_element_type=jnp.float32
-    ).reshape(chips, cores, rows, width)
     mine = lax.dynamic_index_in_dim(partial, core, axis=1, keepdims=False)
     other = lax.dynamic_index_in_dim(partial, cores - 1 - core, axis=1, keepdims=False)
-    pair = [(0, 1), (1, 0)]
     chip_sum = mine + lax.ppermute(other.astype(jnp.bfloat16), "dc", pair).astype(jnp.float32)
     pieces = lax.all_to_all(chip_sum.astype(jnp.bfloat16), CHIPS, 0, 0, tiled=True)
     act_prod = jnp.sum(pieces.astype(jnp.float32), axis=0)
-    act_terms = lax.psum(jnp.sum(act_prod * edge_act, axis=0), "dc")
-    clip_act_grad = jnp.sum(lax.all_gather(act_terms, CHIPS, axis=0, tiled=False), axis=0)
+    act_terms = jnp.sum(act_prod * edge_act, axis=0)
+    groups = lax.axis_size("tensor")
+    slots = jnp.zeros((groups,) + act_terms.shape, act_terms.dtype)
+    slots = lax.dynamic_update_index_in_dim(slots, act_terms, lax.axis_index("tensor"), 0)
+    slots = lax.psum(slots, DP + ("tensor",))
+    clip_act_grad = lax.dynamic_index_in_dim(slots, lax.axis_index("tensor"), 0, keepdims=False)
     pre_rotation = act_prod * slope_act
     token_grad = rotate(pre_rotation).astype(jnp.bfloat16)
     return (projected, token_grad, weight_grad, clip_act_grad, clip_weight_grad)

time: 282 us -> 392 us (1.39)
  waiting for transfers between devices: 127 us -> 275 us
  blocking collectives: 74.7 us -> 24.6 us
  matrix products: 22 us -> 29.1 us
  other arithmetic: 14.5 us -> 19.5 us
    psum x0 -> x1, waiting for transfers between devices: none -> 202 us  [body(): slots = lax.psum(slots, DP + ('tensor',))]
    all_gather x1 -> x0, blocking collectives: 48 us -> none  [body(): lax.all_gather(act_terms, CHIPS, axis=0, tiled=False)]
    all_to_all x1, waiting for transfers between devices: 38.5 us -> 0.01 us  [body(): lax.all_to_all(chip_sum.astype(jnp.bfloat16), CHIPS, 0, 0, tiled=True)]
    all_gather x1, waiting for transfers between devices: 76.9 us -> 68.4 us  [body(): half_act = lax.all_gather(quant_act, CHIPS, axis=0, tiled=True)]
    dot_general x1, matrix products: 3.45 us -> 8.43 us  [body(): lax.dot_general(all_cot, quant_weight, (((1,), (1,)), ((), ())), preferre...]
    select_n x0 -> x1, other arithmetic: none -> 4.07 us  [body(): jnp.where(core == 0, jnp.stack([half_act, partner_act]), jnp.stack([partn...]
    psum x1 -> x0, blocking collectives: 3.94 us -> none  [body(): act_terms = lax.psum(jnp.sum(act_prod * edge_act, axis=0), 'dc')]
  transfers between devices with their start and end apart: 9 -> 10, of which waited for: 5 -> 4; matrix products, arithmetic and copies ran while one was open for 9% -> 12% of each run, Pallas kernels for 0% -> 0%
where the time goes in v3:
time: 392 us; the launch traced here: 390 us
  waiting for transfers between devices  275 us (70%)
  matrix products  29.1 us (7%)
  blocking collectives  24.6 us (6%)
  other arithmetic  19.5 us (5%)
  starting transfers between devices  17.7 us (5%)
  between operations  15.6 us (4%)
  local copies, waits for them, and re-layouts  8.11 us (2%)
    psum x1, waiting for transfers between devices, body(): slots = lax.psum(slots, DP + ('tensor',))  202 us
    all_gather x1, waiting for transfers between devices, body(): half_act = lax.all_gather(quant_act, CHIPS, axis=0, tiled=True)  68.4 us
    all_gather x1, blocking collectives, body(): all_cot = lax.all_gather(cotangent, 'tensor', axis=0, tiled=True)  14 us
    dot_general x1, matrix products, body(): lax.dot_general(all_act, all_cot, (((0,), (0,)), ((), ())), preferred_ele...  12.5 us
    all_to_all x1, starting transfers between devices, body(): lax.all_to_all(chip_sum.astype(jnp.bfloat16), CHIPS, 0, 0, tiled=True)  11.6 us
    psum x1, blocking collectives, body(): clip_weight_grad = lax.psum(weight_terms, 'tensor')  10.6 us
    dot_general x1, matrix products, body(): lax.dot_general(all_cot, quant_weight, (((1,), (1,)), ((), ())), preferre...  8.43 us
  transfers between devices with their start and end apart: 10, of which 4 were waited for; matrix products, arithmetic and copies ran while one was open for 12% of the time, Pallas kernels for 0%

profile of v3, /device:TPU:2, one launch (start us, length us, event | category | flops | bytes accessed | tf_op | source)
XLA Modules:
  0.0 389.7 jit_solution(14210989227953233177)
XLA Ops:
  8.0 1.0 reshape.40
  9.1 0.3 convolution_bitcast_fusion.1
  9.4 0.4 convolution_multiply_fusion.1
  9.9 1.7 collective-permute-start
  11.6 7.3 %multiply_convert_fusion.1 = bf16[4096,768]{1,0:T(8,128)(2,1)} fusion(f32[768]{0:T(1024)} %param.8, bf16[4096,768]{1,0:T(8,128)(2,1)} %param.7), kind=kLoop, calls=%fused_computation.3 | loop fusion | flops 12582912 | bytes 12585984 | tf_op jit(solution)/shard_map/convert_element_type | solution.py:64
  18.9 14.0 %all_gather.6 = bf16[512,768]{1,0:T(8,128)(2,1)S(1)} all-gather(bf16[128,768]{1,0:T(8,128)(2,1)S(1)} %copy-done.2), channel_id=1, replica_groups=mesh['dx'=4,'dz'=8,'dc'=2,'tensor'=4] {'tensor'}, dimensions={0}, use_global_device_ids=true | all-gather | bytes 983040 | tf_op jit(solution)/shard_map/all_gather | solution.py:65
  32.9 1.5 collective-permute-start.1
  34.5 8.4 %fusion.35 = f32[4096,512]{0,1:T(8,128)} fusion(bf16[4096,768]{1,0:T(8,128)(2,1)} %multiply_convert_fusion.1, bf16[512,768]{1,0:T(8,128)(2,1)S(1)} %all_gather.6), kind=kOutput, calls=%fused_computation.57 | convolution fusion | flops 3221225472 | bytes 15466496 | tf_op jit(solution)/shard_map/dot_general | solution.py:66
  42.9 0.7 multiply_convert_fusion.2
  43.6 2.5 fusion.1
  46.2 4.3 %collective-permute-done.3 = bf16[32,8,4096]{2,1,0:T(8,128)(2,1)} collective-permute-done((bf16[32,8,4096]{2,1,0:T(8,128)(2,1)S(1)}, bf16[32,8,4096]{2,1,0:T(8,128)(2,1)}, u32[]{:S(2)}, u32[]{:S(2)}) %collective-permute-start.3) | collective-permute-done | bytes 2097184 | tf_op jit(solution)/shard_map/ppermute | solution.py:95
  50.4 4.7 %fusion = bf16[32,8,4096]{2,1,0:T(8,128)(2,1)} fusion(bf16[32,8,4096]{2,1,0:T(8,128)(2,1)} %collective-permute-done.3, f32[32,2,8,4096]{3,2,1,0:T(8,128)} %bitcast.40, s32[]{:T(128)S(6)} %select_n.50), kind=kLoop, calls=%fused_computation.7 | loop fusion | flops 3145728 | bytes 8388612 | tf_op jit(solution)/shard_map/convert_element_type | solution.py:96
  55.2 11.6 %all-to-all-start = ((bf16[32,8,4096]{2,1,0:T(8,128)(2,1)}), bf16[32,8,4096]{2,1,0:T(8,128)(2,1)S(1)}, u32[]{:S(2)}, u32[]{:S(2)}) async-start(bf16[32,8,4096]{2,1,0:T(8,128)(2,1)} %fusion), calls=%async_computation.1 | async-start | bytes 4194304 | tf_op jit(solution)/shard_map/all_to_all | solution.py:96
  66.8 68.4 %all-gather.2.cloned.1.call-done = bf16[256,4096]{1,0:T(8,128)(2,1)} async-done(((bf16[8,4096]{1,0:T(8,128)(2,1)}), bf16[256,4096]{1,0:T(8,128)(2,1)}) %all-gather.2.cloned.1.call-update) | async-done | bytes 2097168 | tf_op jit(solution)/shard_map/all_gather | solution.py:70
  135.3 0.3 convert_reduce_fusion
  135.7 0.4 convolution_bitcast_fusion
  136.2 0.4 convolution_multiply_fusion
  136.7 1.6 collective-permute-start.4
  138.3 0.2 dynamic_update_slice.4
  138.5 0.6 copy-done.1
  139.2 0.2 reduce-scatter.2.cloned.1.call-start
  139.4 0.4 collective-permute-done.2
  139.8 4.1 %maximum_select_fusion = bf16[2,32,8,4096]{3,2,0,1:T(8,128)(2,1)S(1)} fusion(bf16[1,32,8,4096]{3,2,0,1:T(8,128)(2,1)} %bitcast.5, bf16[1,32,8,4096]{3,2,0,1:T(8,128)(2,1)} %bitcast.43, pred[]{:T(512)S(6)} %eq.11), kind=kLoop, calls=%fused_computation.5 | loop fusion | flops 6291456 | bytes 8388609 | tf_op jit(solution)/shard_map/jit(_where)/select_n | solution.py:73
  143.9 1.9 copy-done
  145.8 6.7 %fusion.36 = f32[512,768]{1,0:T(8,128)} fusion(bf16[512,4096]{1,0:T(8,128)(2,1)S(1)} %bitcast.41, bf16[4096,768]{1,0:T(8,128)(2,1)} %multiply_convert_fusion.1), kind=kOutput, calls=%fused_computation.58 | convolution fusion | flops 3221225472 | bytes 12058624 | tf_op jit(solution)/shard_map/dot_general | solution.py:81
  152.5 12.5 %multiply_reduce_fusion = (f32[768]{0:T(1024)S(1)}, bf16[4096,768]{1,0:T(8,128)(2,1)}) fusion(f32[768]{0:T(1024)S(1)} %copy-done.4, bf16[4096,768]{1,0:T(8,128)(2,1)} %param.7, bf16[512,4096]{1,0:T(8,128)(2,1)} %bitcast.42, bf16[512,768]{1,0:T(8,128)(2,1)S(1)} %all_gather.6), kind=kOutput, calls=%fused_computation | convolution fusion | flops 3252681984 | bytes 17569792 | tf_op jit(solution)/shard_map/dot_general | solution.py:86
  164.9 10.6 %psum.15 = f32[768]{0:T(1024)} all-reduce(f32[768]{0:T(1024)S(1)} %get-tuple-element.11), channel_id=1, replica_groups=mesh['dx'=4,'dz'=8,'dc'=2,'tensor'=4] {'tensor'}, use_global_device_ids=true, to_apply=%region_5.6 | all-reduce | flops 768 | bytes 6144 | tf_op jit(solution)/shard_map/psum | solution.py:92
  175.6 1.0 collective-permute-start.5
  176.6 201.9 %all-reduce.2.cloned.1.call-done = f32[4,4096]{1,0:T(4,128)} async-done(((f32[4,4096]{1,0:T(4,128)}), f32[4,4096]{1,0:T(4,128)}) %all-reduce.2.cloned.1.call-update) | async-done | bytes 65552 | tf_op jit(solution)/shard_map/psum | solution.py:102
  378.5 1.5 constant_dynamic-slice_fusion
  380.0 0.6 select_convert_fusion
  380.6 1.7 convert_element_type.50
  (28 shorter events, 0.7 us)
Async XLA Ops:
  8.0 127.3 %all-gather.2.cloned.1.call-start = ((), (), s32[]{:S(2)}) async-start(), calls=%async_computation.2 | async-start | bytes 2162688 | tf_op jit(solution)/shard_map/all_gather | solution.py:70
  9.9 9.0 %copy-start.2 = (bf16[128,768]{1,0:T(8,128)(2,1)S(1)}, bf16[128,768]{1,0:T(8,128)(2,1)}, u32[]{:S(2)}) copy-start(bf16[128,768]{1,0:T(8,128)(2,1)} %param.9) | copy-start | bytes 589828
  9.9 23.0 %collective-permute-start = (f32[8,4096]{1,0:T(8,128)S(1)}, f32[8,4096]{1,0:T(8,128)S(1)}, u32[]{:S(2)}, u32[]{:S(2)}) collective-permute-start(f32[8,4096]{1,0:T(8,128)S(1)} %mul.67), channel_id=1, source_target_pairs={{0,1},{1,0},{2,3},{3,2},{4,5},{5,4},{6,7},{7,6},{8,9},{9,8},{10,11... | collective-permute-start | bytes 393224 | tf_op jit(solution)/shard_map/ppermute | solution.py:16
  32.9 10.0 %copy-start.3 = (f32[4096]{0:T(1024)S(1)}, f32[4096]{0:T(1024)}, u32[]{:S(2)}) copy-start(f32[4096]{0:T(1024)} %param.6) | copy-start | bytes 49156
  32.9 10.0 %collective-permute-start.1 = (f32[8,4096]{1,0:T(8,128)S(1)}, f32[8,4096]{1,0:T(8,128)S(1)}, u32[]{:S(2)}, u32[]{:S(2)}) collective-permute-start(f32[8,4096]{1,0:T(8,128)S(1)} %add_select_fusion.1), channel_id=1, source_target_pairs={{0,2},{2,0},{1,3},{3,1},{4,6},{6,4},{5,7},{7,5},{8,10},{10,8},{9,1... | collective-permute-start | bytes 393224 | tf_op jit(solution)/shard_map/ppermute | solution.py:16
  46.1 4.4 %collective-permute-start.3 = (bf16[32,8,4096]{2,1,0:T(8,128)(2,1)S(1)}, bf16[32,8,4096]{2,1,0:T(8,128)(2,1)}, u32[]{:S(2)}, u32[]{:S(2)}) collective-permute-start(bf16[32,8,4096]{2,1,0:T(8,128)(2,1)S(1)} %fusion.1), channel_id=1, source_target_pairs={{0,4},{4,0},{1,5},{5,1},{2,6},{6,2},{3,7},{7,3},{8,12},{12,8},{9,1... | collective-permute-start | bytes 6291464 | tf_op jit(solution)/shard_map/ppermute | solution.py:95
  55.2 80.1 %all-to-all-start = ((bf16[32,8,4096]{2,1,0:T(8,128)(2,1)}), bf16[32,8,4096]{2,1,0:T(8,128)(2,1)S(1)}, u32[]{:S(2)}, u32[]{:S(2)}) async-start(bf16[32,8,4096]{2,1,0:T(8,128)(2,1)} %fusion), calls=%async_computation.1 | async-start | bytes 4194304 | tf_op jit(solution)/shard_map/all_to_all | solution.py:96
  66.8 311.7 %all-reduce.2.cloned.1.call-start = ((), (), s32[]{:S(2)}) async-start(), calls=%async_computation.4 | async-start | bytes 131072 | tf_op jit(solution)/shard_map/psum | solution.py:102
  135.3 4.5 %collective-permute-start.2 = (bf16[256,4096]{1,0:T(8,128)(2,1)}, bf16[256,4096]{1,0:T(8,128)(2,1)}, u32[]{:S(2)}, u32[]{:S(2)}) collective-permute-start(bf16[256,4096]{1,0:T(8,128)(2,1)} %all-gather.2.cloned.1.call-done), channel_id=1, source_target_pairs={{0,4},{4,0},{1,5},{5,1},{2,6},{6,2},{3,7},{7,3},{8,12},{12,8},{9,1... | collective-permute-start | bytes 6291464 | tf_op jit(solution)/shard_map/ppermute | solution.py:72
  136.7 38.9 %collective-permute-start.4 = (f32[8,4096]{1,0:T(8,128)S(1)}, f32[8,4096]{1,0:T(8,128)S(1)}, u32[]{:S(2)}, u32[]{:S(2)}) collective-permute-start(f32[8,4096]{1,0:T(8,128)S(1)} %mul.74), channel_id=1, source_target_pairs={{0,1},{1,0},{2,3},{3,2},{4,5},{5,4},{6,7},{7,6},{8,9},{9,8},{10,11... | collective-permute-start | bytes 393224 | tf_op jit(solution)/shard_map/ppermute | solution.py:16
  138.5 0.6 copy-start.1
  139.2 241.4 %reduce-scatter.2.cloned.1.call-start = ((), (), s32[]{:S(2)}) async-start(), calls=%async_computation.3 | async-start | bytes 1966080 | tf_op jit(solution)/shard_map/reduce_scatter | solution.py:80
  143.8 1.9 copy-start
  145.8 6.7 %copy-start.4 = (f32[768]{0:T(1024)S(1)}, f32[768]{0:T(1024)}, u32[]{:S(2)}) copy-start(f32[768]{0:T(1024)} %param.8) | copy-start | bytes 9220
  175.6 204.4 %collective-permute-start.5 = (f32[8,4096]{1,0:T(8,128)S(1)}, f32[8,4096]{1,0:T(8,128)S(1)}, u32[]{:S(2)}, u32[]{:S(2)}) collective-permute-start(f32[8,4096]{1,0:T(8,128)S(1)} %add_select_fusion), channel_id=1, source_target_pairs={{0,2},{2,0},{1,3},{3,1},{4,6},{6,4},{5,7},{7,5},{8,10},{10,8},{9,1... | collective-permute-start | bytes 393224 | tf_op jit(solution)/shard_map/ppermute | solution.py:16
Sparse Core Ops, SparseCore 0:
  46.3 88.8 all-gather.1
  152.6 27.1 reduce-scatter.1
Sparse Core Ops, SparseCore 1:
  139.3 239.2 all-reduce.1

commit v4 on v3

--- a/solution.py
+++ b/solution.py
@@ -14,6 +14,12 @@
         if high != low and high < count:
             route += [(low, high), (high, low)]
     return lax.ppermute(block, axis, route)
+
+
+def butterfly_sum(values, axis):
+    for bit_number in range(lax.axis_size(axis).bit_length() - 1):
+        values = values + swapped(values, axis, bit_number)
+    return values
 
 
 def sylvester(order):
@@ -89,18 +95,16 @@
     slope_weight = 1.0 - tanh_weight * tanh_weight
     weight_grad = (weight_prod * slope_weight).astype(jnp.bfloat16)
     weight_terms = jnp.sum(weight_prod * (tanh_weight - ratio_weight * slope_weight), axis=0)
-    clip_weight_grad = lax.psum(weight_terms, "tensor")
+    clip_weight_grad = butterfly_sum(weight_terms, "tensor")
     mine = lax.dynamic_index_in_dim(partial, core, axis=1, keepdims=False)
     other = lax.dynamic_index_in_dim(partial, cores - 1 - core, axis=1, keepdims=False)
     chip_sum = mine + lax.ppermute(other.astype(jnp.bfloat16), "dc", pair).astype(jnp.float32)
     pieces = lax.all_to_all(chip_sum.astype(jnp.bfloat16), CHIPS, 0, 0, tiled=True)
     act_prod = jnp.sum(pieces.astype(jnp.float32), axis=0)
     act_terms = jnp.sum(act_prod * edge_act, axis=0)
-    groups = lax.axis_size("tensor")
-    slots = jnp.zeros((groups,) + act_terms.shape, act_terms.dtype)
-    slots = lax.dynamic_update_index_in_dim(slots, act_terms, lax.axis_index("tensor"), 0)
-    slots = lax.psum(slots, DP + ("tensor",))
-    clip_act_grad = lax.dynamic_index_in_dim(slots, lax.axis_index("tensor"), 0, keepdims=False)
+    for axis in DP:
+        act_terms = butterfly_sum(act_terms, axis)
+    clip_act_grad = act_terms
     pre_rotation = act_prod * slope_act
     token_grad = rotate(pre_rotation).astype(jnp.bfloat16)
     return (projected, token_grad, weight_grad, clip_act_grad, clip_weight_grad)

time: 392 us -> 199 us (0.51)
  waiting for transfers between devices: 275 us -> 87.1 us
  starting transfers between devices: 17.7 us -> 29.4 us
  blocking collectives: 24.6 us -> 14 us
  local copies, waits for them, and re-layouts: 8.11 us -> 3.84 us
    psum x1 -> x0, waiting for transfers between devices: 202 us -> none  [body(): slots = lax.psum(slots, DP + ('tensor',))]
    ppermute x4 -> x12, waiting for transfers between devices: 0.01 us -> 13.7 us  [swapped(): return lax.ppermute(block, axis, route)]
    ppermute x4 -> x12, starting transfers between devices: 5.75 us -> 17.7 us  [swapped(): return lax.ppermute(block, axis, route)]
    psum x1 -> x0, blocking collectives: 10.6 us -> none  [body(): clip_weight_grad = lax.psum(weight_terms, 'tensor')]
  transfers between devices with their start and end apart: 10 -> 17, of which waited for: 4 -> 8; matrix products, arithmetic and copies ran while one was open for 12% -> 24% of each run, Pallas kernels for 0% -> 0%
where the time goes in v4:
time: 199 us
  waiting for transfers between devices  87.1 us (44%)
  starting transfers between devices  29.4 us (15%)
  matrix products  29.1 us (15%)
  other arithmetic  21 us (11%)
  between operations  14.2 us (7%)
  blocking collectives  14 us (7%)
  local copies, waits for them, and re-layouts  3.84 us (2%)
    all_gather x1, waiting for transfers between devices, body(): half_act = lax.all_gather(quant_act, CHIPS, axis=0, tiled=True)  68.5 us
    ppermute x12, starting transfers between devices, swapped(): return lax.ppermute(block, axis, route)  17.7 us
    all_gather x1, blocking collectives, body(): all_cot = lax.all_gather(cotangent, 'tensor', axis=0, tiled=True)  14 us
    ppermute x12, waiting for transfers between devices, swapped(): return lax.ppermute(block, axis, route)  13.7 us
    dot_general x1, matrix products, body(): lax.dot_general(all_act, all_cot, (((0,), (0,)), ((), ())), preferred_ele...  12.4 us
    all_to_all x1, starting transfers between devices, body(): lax.all_to_all(chip_sum.astype(jnp.bfloat16), CHIPS, 0, 0, tiled=True)  11.6 us
    dot_general x1, matrix products, body(): lax.dot_general(all_cot, quant_weight, (((1,), (1,)), ((), ())), preferre...  8.42 us
    convert_element_type x1, other arithmetic, body(): quant_weight = (clip_weight * tanh_weight).astype(jnp.bfloat16)  7.31 us
  transfers between devices with their start and end apart: 17, of which 8 were waited for; matrix products, arithmetic and copies ran while one was open for 24% of the time, Pallas kernels for 0%

profile of v4, /device:TPU:2, one launch (start us, length us, event | category | flops | bytes accessed | tf_op | source)
XLA Modules:
  0.0 198.7 jit_solution(12962387192150915478)
XLA Ops:
  7.2 1.0 reshape.40
  9.1 1.7 collective-permute-start
  10.8 7.3 %multiply_convert_fusion.1 = bf16[4096,768]{1,0:T(8,128)(2,1)} fusion(f32[768]{0:T(1024)} %param.8, bf16[4096,768]{1,0:T(8,128)(2,1)} %param.7), kind=kLoop, calls=%fused_computation.3 | loop fusion | flops 12582912 | bytes 12585984 | tf_op jit(solution)/shard_map/convert_element_type | solution.py:70
  18.1 14.0 %all_gather.6 = bf16[512,768]{1,0:T(8,128)(2,1)S(1)} all-gather(bf16[128,768]{1,0:T(8,128)(2,1)S(1)} %copy-done.1), channel_id=1, replica_groups=mesh['dx'=4,'dz'=8,'dc'=2,'tensor'=4] {'tensor'}, dimensions={0}, use_global_device_ids=true | all-gather | bytes 983040 | tf_op jit(solution)/shard_map/all_gather | solution.py:71
  32.1 1.5 collective-permute-start.1
  33.6 8.4 %fusion.35 = f32[4096,512]{0,1:T(8,128)} fusion(bf16[4096,768]{1,0:T(8,128)(2,1)} %multiply_convert_fusion.1, bf16[512,768]{1,0:T(8,128)(2,1)S(1)} %all_gather.6), kind=kOutput, calls=%fused_computation.56 | convolution fusion | flops 3221225472 | bytes 15466496 | tf_op jit(solution)/shard_map/dot_general | solution.py:72
  42.1 0.7 multiply_convert_fusion.2
  42.7 2.5 %fusion.1 = bf16[32,8,4096]{2,1,0:T(8,128)(2,1)S(1)} fusion(f32[32,2,8,4096]{3,2,1,0:T(8,128)} %bitcast.37, s32[]{:T(128)S(6)} %select_n.45), kind=kLoop, calls=%fused_computation.10 | loop fusion | bytes 4194308 | tf_op jit(solution)/shard_map/convert_element_type | solution.py:101
  45.3 4.3 %collective-permute-done.3 = bf16[32,8,4096]{2,1,0:T(8,128)(2,1)} collective-permute-done((bf16[32,8,4096]{2,1,0:T(8,128)(2,1)S(1)}, bf16[32,8,4096]{2,1,0:T(8,128)(2,1)}, u32[]{:S(2)}, u32[]{:S(2)}) %collective-permute-start.3) | collective-permute-done | bytes 2097184 | tf_op jit(solution)/shard_map/ppermute | solution.py:101
  49.6 4.7 %fusion = bf16[32,8,4096]{2,1,0:T(8,128)(2,1)} fusion(bf16[32,8,4096]{2,1,0:T(8,128)(2,1)} %collective-permute-done.3, f32[32,2,8,4096]{3,2,1,0:T(8,128)} %bitcast.38, s32[]{:T(128)S(6)} %select_n.44), kind=kLoop, calls=%fused_computation.7 | loop fusion | flops 3145728 | bytes 8388612 | tf_op jit(solution)/shard_map/convert_element_type | solution.py:102
  54.3 11.6 %all-to-all-start = ((bf16[32,8,4096]{2,1,0:T(8,128)(2,1)}), bf16[32,8,4096]{2,1,0:T(8,128)(2,1)S(1)}, u32[]{:S(2)}, u32[]{:S(2)}) async-start(bf16[32,8,4096]{2,1,0:T(8,128)(2,1)} %fusion), calls=%async_computation.1 | async-start | bytes 4194304 | tf_op jit(solution)/shard_map/all_to_all | solution.py:102
  66.0 68.5 %all-gather.2.cloned.1.call-done = bf16[256,4096]{1,0:T(8,128)(2,1)} async-done(((bf16[8,4096]{1,0:T(8,128)(2,1)}), bf16[256,4096]{1,0:T(8,128)(2,1)}) %all-gather.2.cloned.1.call-update) | async-done | bytes 2097168 | tf_op jit(solution)/shard_map/all_gather | solution.py:76
  134.9 0.8 collective-permute-start.6
  135.8 2.9 %collective-permute-done.6 = f32[4096]{0:T(1024)S(1)} collective-permute-done((f32[4096]{0:T(1024)S(1)}, f32[4096]{0:T(1024)S(1)}, u32[]{:S(2)}, u32[]{:S(2)}) %collective-permute-start.6) | collective-permute-done | bytes 16416 | tf_op jit(solution)/shard_map/ppermute | solution.py:16
  138.7 2.2 %collective-permute-start.7 = (f32[4096]{0:T(1024)S(1)}, f32[4096]{0:T(1024)S(1)}, u32[]{:S(2)}, u32[]{:S(2)}) collective-permute-start(f32[4096]{0:T(1024)S(1)} %add.121), channel_id=1, source_target_pairs={{0,128},{128,0},{64,192},{192,64},{1,129},{129,1},{65,193},{193,65... | collective-permute-start | bytes 49160 | tf_op jit(solution)/shard_map/ppermute | solution.py:16
  141.3 2.6 %collective-permute-done.7 = f32[4096]{0:T(1024)S(1)} collective-permute-done((f32[4096]{0:T(1024)S(1)}, f32[4096]{0:T(1024)S(1)}, u32[]{:S(2)}, u32[]{:S(2)}) %collective-permute-start.7) | collective-permute-done | bytes 16416 | tf_op jit(solution)/shard_map/ppermute | solution.py:16
  143.9 0.9 collective-permute-start.8
  145.3 1.6 collective-permute-start.4
  146.9 0.8 collective-permute-done.8
  147.7 2.0 collective-permute-start.9
  149.6 4.3 %maximum_select_fusion = bf16[2,32,8,4096]{3,2,0,1:T(8,128)(2,1)S(1)} fusion(bf16[1,32,8,4096]{3,2,0,1:T(8,128)(2,1)} %bitcast.5, bf16[1,32,8,4096]{3,2,0,1:T(8,128)(2,1)} %bitcast.41, pred[]{:T(512)S(6)} %eq.11), kind=kLoop, calls=%fused_computation.5 | loop fusion | flops 6291456 | bytes 8388609 | tf_op jit(solution)/shard_map/jit(_where)/select_n | solution.py:79
  154.0 2.7 %collective-permute-start.10 = (f32[4096]{0:T(1024)S(1)}, f32[4096]{0:T(1024)S(1)}, u32[]{:S(2)}, u32[]{:S(2)}) collective-permute-start(f32[4096]{0:T(1024)S(1)} %add.124), channel_id=1, source_target_pairs={{0,32},{32,0},{8,40},{40,8},{16,48},{48,16},{24,56},{56,24},{1,33}... | collective-permute-start | bytes 49160 | tf_op jit(solution)/shard_map/ppermute | solution.py:16
  156.7 6.7 %fusion.36 = f32[512,768]{1,0:T(8,128)} fusion(bf16[512,4096]{1,0:T(8,128)(2,1)S(1)} %bitcast.39, bf16[4096,768]{1,0:T(8,128)(2,1)} %multiply_convert_fusion.1), kind=kOutput, calls=%fused_computation.57 | convolution fusion | flops 3221225472 | bytes 12058624 | tf_op jit(solution)/shard_map/dot_general | solution.py:87
  163.5 2.6 %collective-permute-start.5 = (f32[8,4096]{1,0:T(8,128)S(1)}, f32[8,4096]{1,0:T(8,128)S(1)}, u32[]{:S(2)}, u32[]{:S(2)}) collective-permute-start(f32[8,4096]{1,0:T(8,128)S(1)} %add_select_fusion), channel_id=1, source_target_pairs={{0,2},{2,0},{1,3},{3,1},{4,6},{6,4},{5,7},{7,5},{8,10},{10,8},{9,1... | collective-permute-start | bytes 393224 | tf_op jit(solution)/shard_map/ppermute | solution.py:16
  166.2 12.4 %multiply_reduce_fusion = (f32[768]{0:T(1024)S(1)}, bf16[4096,768]{1,0:T(8,128)(2,1)}) fusion(f32[768]{0:T(1024)S(1)} %copy-done.3, bf16[4096,768]{1,0:T(8,128)(2,1)} %param.7, bf16[512,4096]{1,0:T(8,128)(2,1)} %bitcast.40, bf16[512,768]{1,0:T(8,128)(2,1)S(1)} %all_gather.6), kind=kOutput, calls=%fused_computation | convolution fusion | flops 3252681984 | bytes 17569792 | tf_op jit(solution)/shard_map/dot_general | solution.py:92
  179.2 3.2 %collective-permute-done.12 = f32[768]{0:T(1024)S(1)} collective-permute-done((f32[768]{0:T(1024)S(1)}, f32[768]{0:T(1024)S(1)}, u32[]{:S(2)}, u32[]{:S(2)}) %collective-permute-start.12) | collective-permute-done | bytes 3104 | tf_op jit(solution)/shard_map/ppermute | solution.py:16
  182.4 1.1 collective-permute-start.13
  183.5 4.2 %collective-permute-done.13 = f32[768]{0:T(1024)S(1)} collective-permute-done((f32[768]{0:T(1024)S(1)}, f32[768]{0:T(1024)S(1)}, u32[]{:S(2)}, u32[]{:S(2)}) %collective-permute-start.13) | collective-permute-done | bytes 3104 | tf_op jit(solution)/shard_map/ppermute | solution.py:16
  188.3 0.6 add.126
  188.9 0.6 select_convert_fusion
  189.6 0.6 reduce-scatter.2.cloned.1.call-done
  190.2 1.7 convert_element_type.50
  (43 shorter events, 3.8 us)
Async XLA Ops:
  7.2 127.3 %all-gather.2.cloned.1.call-start = ((), (), s32[]{:S(2)}) async-start(), calls=%async_computation.2 | async-start | bytes 2162688 | tf_op jit(solution)/shard_map/all_gather | solution.py:76
  9.1 9.0 %copy-start.1 = (bf16[128,768]{1,0:T(8,128)(2,1)S(1)}, bf16[128,768]{1,0:T(8,128)(2,1)}, u32[]{:S(2)}) copy-start(bf16[128,768]{1,0:T(8,128)(2,1)} %param.9) | copy-start | bytes 589828
  9.1 22.9 %collective-permute-start = (f32[8,4096]{1,0:T(8,128)S(1)}, f32[8,4096]{1,0:T(8,128)S(1)}, u32[]{:S(2)}, u32[]{:S(2)}) collective-permute-start(f32[8,4096]{1,0:T(8,128)S(1)} %mul.67), channel_id=1, source_target_pairs={{0,1},{1,0},{2,3},{3,2},{4,5},{5,4},{6,7},{7,6},{8,9},{9,8},{10,11... | collective-permute-start | bytes 393224 | tf_op jit(solution)/shard_map/ppermute | solution.py:16
  32.1 10.0 %copy-start.2 = (f32[4096]{0:T(1024)S(1)}, f32[4096]{0:T(1024)}, u32[]{:S(2)}) copy-start(f32[4096]{0:T(1024)} %param.6) | copy-start | bytes 49156
  32.1 10.0 %collective-permute-start.1 = (f32[8,4096]{1,0:T(8,128)S(1)}, f32[8,4096]{1,0:T(8,128)S(1)}, u32[]{:S(2)}, u32[]{:S(2)}) collective-permute-start(f32[8,4096]{1,0:T(8,128)S(1)} %add_select_fusion.1), channel_id=1, source_target_pairs={{0,2},{2,0},{1,3},{3,1},{4,6},{6,4},{5,7},{7,5},{8,10},{10,8},{9,1... | collective-permute-start | bytes 393224 | tf_op jit(solution)/shard_map/ppermute | solution.py:16
  45.2 4.4 %collective-permute-start.3 = (bf16[32,8,4096]{2,1,0:T(8,128)(2,1)S(1)}, bf16[32,8,4096]{2,1,0:T(8,128)(2,1)}, u32[]{:S(2)}, u32[]{:S(2)}) collective-permute-start(bf16[32,8,4096]{2,1,0:T(8,128)(2,1)S(1)} %fusion.1), channel_id=1, source_target_pairs={{0,4},{4,0},{1,5},{5,1},{2,6},{6,2},{3,7},{7,3},{8,12},{12,8},{9,1... | collective-permute-start | bytes 6291464 | tf_op jit(solution)/shard_map/ppermute | solution.py:101
  54.3 80.2 %all-to-all-start = ((bf16[32,8,4096]{2,1,0:T(8,128)(2,1)}), bf16[32,8,4096]{2,1,0:T(8,128)(2,1)S(1)}, u32[]{:S(2)}, u32[]{:S(2)}) async-start(bf16[32,8,4096]{2,1,0:T(8,128)(2,1)} %fusion), calls=%async_computation.1 | async-start | bytes 4194304 | tf_op jit(solution)/shard_map/all_to_all | solution.py:102
  65.9 124.2 %reduce-scatter.2.cloned.1.call-start = ((), (), s32[]{:S(2)}) async-start(), calls=%async_computation.3 | async-start | bytes 1966080 | tf_op jit(solution)/shard_map/reduce_scatter | solution.py:86
  134.5 15.2 %collective-permute-start.2 = (bf16[256,4096]{1,0:T(8,128)(2,1)}, bf16[256,4096]{1,0:T(8,128)(2,1)}, u32[]{:S(2)}, u32[]{:S(2)}) collective-permute-start(bf16[256,4096]{1,0:T(8,128)(2,1)} %all-gather.2.cloned.1.call-done), channel_id=1, source_target_pairs={{0,4},{4,0},{1,5},{5,1},{2,6},{6,2},{3,7},{7,3},{8,12},{12,8},{9,1... | collective-permute-start | bytes 6291464 | tf_op jit(solution)/shard_map/ppermute | solution.py:78
  134.9 3.8 %collective-permute-start.6 = (f32[4096]{0:T(1024)S(1)}, f32[4096]{0:T(1024)S(1)}, u32[]{:S(2)}, u32[]{:S(2)}) collective-permute-start(f32[4096]{0:T(1024)S(1)} %get-tuple-element.13), channel_id=1, source_target_pairs={{0,64},{64,0},{128,192},{192,128},{1,65},{65,1},{129,193},{193,129... | collective-permute-start | bytes 49160 | tf_op jit(solution)/shard_map/ppermute | solution.py:16
  138.7 5.2 %collective-permute-start.7 = (f32[4096]{0:T(1024)S(1)}, f32[4096]{0:T(1024)S(1)}, u32[]{:S(2)}, u32[]{:S(2)}) collective-permute-start(f32[4096]{0:T(1024)S(1)} %add.121), channel_id=1, source_target_pairs={{0,128},{128,0},{64,192},{192,64},{1,129},{129,1},{65,193},{193,65... | collective-permute-start | bytes 49160 | tf_op jit(solution)/shard_map/ppermute | solution.py:16
  143.9 3.7 %collective-permute-start.8 = (f32[4096]{0:T(1024)S(1)}, f32[4096]{0:T(1024)S(1)}, u32[]{:S(2)}, u32[]{:S(2)}) collective-permute-start(f32[4096]{0:T(1024)S(1)} %add.122), channel_id=1, source_target_pairs={{0,8},{8,0},{16,24},{24,16},{32,40},{40,32},{48,56},{56,48},{1,9},... | collective-permute-start | bytes 49160 | tf_op jit(solution)/shard_map/ppermute | solution.py:16
  145.3 18.2 %collective-permute-start.4 = (f32[8,4096]{1,0:T(8,128)S(1)}, f32[8,4096]{1,0:T(8,128)S(1)}, u32[]{:S(2)}, u32[]{:S(2)}) collective-permute-start(f32[8,4096]{1,0:T(8,128)S(1)} %mul.74), channel_id=1, source_target_pairs={{0,1},{1,0},{2,3},{3,2},{4,5},{5,4},{6,7},{7,6},{8,9},{9,8},{10,11... | collective-permute-start | bytes 393224 | tf_op jit(solution)/shard_map/ppermute | solution.py:16
  147.7 6.3 %collective-permute-start.9 = (f32[4096]{0:T(1024)S(1)}, f32[4096]{0:T(1024)S(1)}, u32[]{:S(2)}, u32[]{:S(2)}) collective-permute-start(f32[4096]{0:T(1024)S(1)} %add.123), channel_id=1, source_target_pairs={{0,16},{16,0},{8,24},{24,8},{32,48},{48,32},{40,56},{56,40},{1,17}... | collective-permute-start | bytes 49160 | tf_op jit(solution)/shard_map/ppermute | solution.py:16
  154.0 2.7 %copy-start = (bf16[2,32,8,4096]{3,2,0,1:T(8,128)(2,1)}, bf16[2,32,8,4096]{3,2,0,1:T(8,128)(2,1)S(1)}, u32[]{:S(2)}) copy-start(bf16[2,32,8,4096]{3,2,0,1:T(8,128)(2,1)S(1)} %maximum_select_fusion) | copy-start | bytes 12582916
  154.0 9.4 %collective-permute-start.10 = (f32[4096]{0:T(1024)S(1)}, f32[4096]{0:T(1024)S(1)}, u32[]{:S(2)}, u32[]{:S(2)}) collective-permute-start(f32[4096]{0:T(1024)S(1)} %add.124), channel_id=1, source_target_pairs={{0,32},{32,0},{8,40},{40,8},{16,48},{48,16},{24,56},{56,24},{1,33}... | collective-permute-start | bytes 49160 | tf_op jit(solution)/shard_map/ppermute | solution.py:16
  156.7 9.5 %copy-start.3 = (f32[768]{0:T(1024)S(1)}, f32[768]{0:T(1024)}, u32[]{:S(2)}) copy-start(f32[768]{0:T(1024)} %param.8) | copy-start | bytes 9220
  163.4 24.9 %collective-permute-start.11 = (f32[4096]{0:T(1024)S(1)}, f32[4096]{0:T(1024)S(1)}, u32[]{:S(2)}, u32[]{:S(2)}) collective-permute-start(f32[4096]{0:T(1024)S(1)} %add.125), channel_id=1, source_target_pairs={{0,4},{4,0},{1,5},{5,1},{2,6},{6,2},{3,7},{7,3},{8,12},{12,8},{9,1... | collective-permute-start | bytes 49160 | tf_op jit(solution)/shard_map/ppermute | solution.py:16
  163.5 25.4 %collective-permute-start.5 = (f32[8,4096]{1,0:T(8,128)S(1)}, f32[8,4096]{1,0:T(8,128)S(1)}, u32[]{:S(2)}, u32[]{:S(2)}) collective-permute-start(f32[8,4096]{1,0:T(8,128)S(1)} %add_select_fusion), channel_id=1, source_target_pairs={{0,2},{2,0},{1,3},{3,1},{4,6},{6,4},{5,7},{7,5},{8,10},{10,8},{9,1... | collective-permute-start | bytes 393224 | tf_op jit(solution)/shard_map/ppermute | solution.py:16
  178.6 3.8 %collective-permute-start.12 = (f32[768]{0:T(1024)S(1)}, f32[768]{0:T(1024)S(1)}, u32[]{:S(2)}, u32[]{:S(2)}) collective-permute-start(f32[768]{0:T(1024)S(1)} %get-tuple-element.11), channel_id=1, source_target_pairs={{0,1},{1,0},{2,3},{3,2},{4,5},{5,4},{6,7},{7,6},{8,9},{9,8},{10,11... | collective-permute-start | bytes 9224 | tf_op jit(solution)/shard_map/ppermute | solution.py:16
  182.4 5.3 %collective-permute-start.13 = (f32[768]{0:T(1024)S(1)}, f32[768]{0:T(1024)S(1)}, u32[]{:S(2)}, u32[]{:S(2)}) collective-permute-start(f32[768]{0:T(1024)S(1)} %add.127), channel_id=1, source_target_pairs={{0,2},{2,0},{1,3},{3,1},{4,6},{6,4},{5,7},{7,5},{8,10},{10,8},{9,1... | collective-permute-start | bytes 9224 | tf_op jit(solution)/shard_map/ppermute | solution.py:16
Sparse Core Ops, SparseCore 0:
  45.5 88.9 all-gather.1
  163.5 26.6 reduce-scatter.1

commit v5 on v4

--- a/solution.py
+++ b/solution.py
@@ -76,21 +76,27 @@
     half_act = lax.all_gather(quant_act, CHIPS, axis=0, tiled=True)
     pair = [(0, 1), (1, 0)]
     partner_act = lax.ppermute(half_act, "dc", pair)
-    both_act = jnp.where(
-        core == 0, jnp.stack([half_act, partner_act]), jnp.stack([partner_act, half_act])
-    )
-    all_act = (
-        both_act.reshape(cores, chips, rows, width).transpose(1, 0, 2, 3).reshape(-1, width)
-    )
-    block = all_act
+    hidden = all_cot.shape[1]
+    cot_split = all_cot.reshape(chips, cores, rows, hidden)
+    cot_own = lax.dynamic_index_in_dim(cot_split, core, axis=1, keepdims=False)
+    cot_partner = lax.dynamic_index_in_dim(cot_split, cores - 1 - core, axis=1, keepdims=False)
+    proj_own = jnp.dot(half_act, quant_weight, preferred_element_type=jnp.float32)
+    proj_partner = jnp.dot(partner_act, quant_weight, preferred_element_type=jnp.float32)
+    proj_own = proj_own.reshape(chips, rows, hidden)
+    proj_partner = proj_partner.reshape(chips, rows, hidden)
+    proj_all = jnp.where(
+        core == 0,
+        jnp.stack([proj_own, proj_partner], axis=1),
+        jnp.stack([proj_partner, proj_own], axis=1),
+    ).reshape(-1, hidden)
     projected = lax.psum_scatter(
-        jnp.dot(block, quant_weight, preferred_element_type=jnp.float32),
-        "tensor",
-        scatter_dimension=0,
-        tiled=True,
+        proj_all, "tensor", scatter_dimension=0, tiled=True
     ).astype(jnp.bfloat16)
+    contract = (((0,), (0,)), ((), ()))
     weight_prod = lax.dot_general(
-        all_act, all_cot, (((0,), (0,)), ((), ())), preferred_element_type=jnp.float32
+        half_act, cot_own.reshape(-1, hidden), contract, preferred_element_type=jnp.float32
+    ) + lax.dot_general(
+        partner_act, cot_partner.reshape(-1, hidden), contract, preferred_element_type=jnp.float32
     )
     slope_weight = 1.0 - tanh_weight * tanh_weight
     weight_grad = (weight_prod * slope_weight).astype(jnp.bfloat16)

time: 199 us -> 209 us (1.050)
  matrix products: 29.1 us -> 42.2 us
  other arithmetic: 21 us -> 16.8 us
  waiting for transfers between devices: 87.1 us -> 84.8 us
    dot_general x2 -> x4, matrix products: 19.1 us -> 32.2 us  [the longest x1 12.9 us: body(): lax.dot_general(partner_act, cot_partner.reshape(-1, hidden), contract, p...]
    select_n x1, other arithmetic: 4.33 us -> 0.1 us  [body(): jnp.where(core == 0, jnp.stack([proj_own, proj_partner], axis=1), jnp.sta...]
  transfers between devices with their start and end apart: 17 -> 17, of which waited for: 8 -> 7; matrix products, arithmetic and copies ran while one was open for 24% -> 28% of each run, Pallas kernels for 0% -> 0%
where the time goes in v5:
time: 209 us; the launch traced here: 208 us
  waiting for transfers between devices  84.8 us (41%)
  matrix products  42.2 us (20%)
  starting transfers between devices  30.7 us (15%)
  other arithmetic  16.8 us (8%)
  between operations  14.2 us (7%)
  blocking collectives  14 us (7%)
  local copies, waits for them, and re-layouts  5.21 us (2%)
    all_gather x1, waiting for transfers between devices, body(): half_act = lax.all_gather(quant_act, CHIPS, axis=0, tiled=True)  67 us
    ppermute x12, starting transfers between devices, swapped(): return lax.ppermute(block, axis, route)  19 us
    all_gather x1, blocking collectives, body(): all_cot = lax.all_gather(cotangent, 'tensor', axis=0, tiled=True)  14 us
    ppermute x12, waiting for transfers between devices, swapped(): return lax.ppermute(block, axis, route)  13.5 us
    dot_general x1, matrix products, body(): lax.dot_general(partner_act, cot_partner.reshape(-1, hidden), contract, p...  12.9 us
    all_to_all x1, starting transfers between devices, body(): lax.all_to_all(chip_sum.astype(jnp.bfloat16), CHIPS, 0, 0, tiled=True)  11.6 us
    dot_general x1, matrix products, body(): lax.dot_general(all_cot, quant_weight, (((1,), (1,)), ((), ())), preferre...  8.42 us
    dot_general x1, matrix products, body(): lax.dot_general(half_act, cot_own.reshape(-1, hidden), contract, preferre...  8 us
  transfers between devices with their start and end apart: 17, of which 7 were waited for; matrix products, arithmetic and copies ran while one was open for 28% of the time, Pallas kernels for 0%

profile of v5, /device:TPU:2, one launch (start us, length us, event | category | flops | bytes accessed | tf_op | source)
XLA Modules:
  0.0 207.9 jit_solution(4741345571837076026)
XLA Ops:
  7.2 1.0 reshape.44
  9.1 1.7 collective-permute-start
  10.8 7.3 %multiply_convert_fusion.1 = bf16[4096,768]{1,0:T(8,128)(2,1)} fusion(f32[768]{0:T(1024)} %param.8, bf16[4096,768]{1,0:T(8,128)(2,1)} %param.7), kind=kLoop, calls=%fused_computation.3 | loop fusion | flops 12582912 | bytes 12585984 | tf_op jit(solution)/shard_map/convert_element_type | solution.py:70
  18.1 14.0 %all_gather.6 = bf16[512,768]{1,0:T(8,128)(2,1)S(1)} all-gather(bf16[128,768]{1,0:T(8,128)(2,1)S(1)} %copy-done.1), channel_id=1, replica_groups=mesh['dx'=4,'dz'=8,'dc'=2,'tensor'=4] {'tensor'}, dimensions={0}, use_global_device_ids=true | all-gather | bytes 983040 | tf_op jit(solution)/shard_map/all_gather | solution.py:71
  32.1 1.5 collective-permute-start.1
  33.6 8.4 %fusion.42 = f32[4096,512]{0,1:T(8,128)} fusion(bf16[4096,768]{1,0:T(8,128)(2,1)} %multiply_convert_fusion.1, bf16[512,768]{1,0:T(8,128)(2,1)S(1)} %all_gather.6), kind=kOutput, calls=%fused_computation.66 | convolution fusion | flops 3221225472 | bytes 15466496 | tf_op jit(solution)/shard_map/dot_general | solution.py:72
  42.1 0.7 multiply_convert_fusion.2
  42.7 2.5 %fusion.1 = bf16[32,8,4096]{2,1,0:T(8,128)(2,1)S(1)} fusion(f32[32,2,8,4096]{3,2,1,0:T(8,128)} %bitcast.49, s32[]{:T(128)S(6)} %select_n.52), kind=kLoop, calls=%fused_computation.10 | loop fusion | bytes 4194308 | tf_op jit(solution)/shard_map/convert_element_type | solution.py:107
  45.3 4.3 %collective-permute-done.3 = bf16[32,8,4096]{2,1,0:T(8,128)(2,1)} collective-permute-done((bf16[32,8,4096]{2,1,0:T(8,128)(2,1)S(1)}, bf16[32,8,4096]{2,1,0:T(8,128)(2,1)}, u32[]{:S(2)}, u32[]{:S(2)}) %collective-permute-start.3) | collective-permute-done | bytes 2097184 | tf_op jit(solution)/shard_map/ppermute | solution.py:107
  49.6 4.8 %fusion = bf16[32,8,4096]{2,1,0:T(8,128)(2,1)} fusion(bf16[32,8,4096]{2,1,0:T(8,128)(2,1)} %collective-permute-done.3, f32[32,2,8,4096]{3,2,1,0:T(8,128)} %bitcast.50, s32[]{:T(128)S(6)} %select_n.51), kind=kLoop, calls=%fused_computation.7 | loop fusion | flops 3145728 | bytes 8388612 | tf_op jit(solution)/shard_map/convert_element_type | solution.py:108
  54.4 11.6 %all-to-all-start = ((bf16[32,8,4096]{2,1,0:T(8,128)(2,1)}), bf16[32,8,4096]{2,1,0:T(8,128)(2,1)S(1)}, u32[]{:S(2)}, u32[]{:S(2)}) async-start(bf16[32,8,4096]{2,1,0:T(8,128)(2,1)} %fusion), calls=%async_computation.1 | async-start | bytes 4194304 | tf_op jit(solution)/shard_map/all_to_all | solution.py:108
  66.0 67.0 %all-gather.2.cloned.1.call-done = bf16[256,4096]{1,0:T(8,128)(2,1)} async-done(((bf16[8,4096]{1,0:T(8,128)(2,1)}), bf16[256,4096]{1,0:T(8,128)(2,1)}) %all-gather.2.cloned.1.call-update) | async-done | bytes 2097168 | tf_op jit(solution)/shard_map/all_gather | solution.py:76
  133.1 6.1 %convolution_bitcast_fusion.1 = f32[32,1,8,768]{3,2,0,1:T(8,128)} fusion(bf16[256,4096]{1,0:T(8,128)(2,1)} %all-gather.2.cloned.1.call-done, bf16[4096,768]{1,0:T(8,128)(2,1)} %multiply_convert_fusion.1), kind=kOutput, calls=%fused_computation.13 | convolution fusion | flops 1610612736 | bytes 9175040 | tf_op jit(solution)/shard_map/dot_general | solution.py:83
  139.5 1.0 collective-permute-start.6
  140.5 8.0 %fusion.3 = f32[4096,768]{1,0:T(8,128)} fusion(bf16[256,4096]{1,0:T(8,128)(2,1)} %all-gather.2.cloned.1.call-done, bf16[32,2,8,768]{3,2,1,0:T(8,128)(2,1)S(1)} %bitcast.51, s32[]{:T(128)S(6)} %select_n.51), kind=kOutput, calls=%fused_computation.19 | convolution fusion | flops 1610612736 | bytes 15073284 | tf_op jit(solution)/shard_map/dot_general | solution.py:96
  148.6 3.2 %collective-permute-start.7 = (f32[4096]{0:T(1024)S(1)}, f32[4096]{0:T(1024)S(1)}, u32[]{:S(2)}, u32[]{:S(2)}) collective-permute-start(f32[4096]{0:T(1024)S(1)} %add.128), channel_id=1, source_target_pairs={{0,128},{128,0},{64,192},{192,64},{1,129},{129,1},{65,193},{193,65... | collective-permute-start | bytes 49160 | tf_op jit(solution)/shard_map/ppermute | solution.py:16
  152.3 1.8 collective-permute-done.7
  155.3 1.6 collective-permute-start.4
  156.9 1.0 collective-permute-done.8
  157.9 1.6 collective-permute-start.9
  159.5 5.2 %convolution_bitcast_fusion = f32[32,1,8,768]{3,2,0,1:T(8,128)S(1)} fusion(bf16[256,4096]{1,0:T(8,128)(2,1)} %collective-permute-done.2, bf16[4096,768]{1,0:T(8,128)(2,1)} %multiply_convert_fusion.1), kind=kOutput, calls=%fused_computation.12 | convolution fusion | flops 1610612736 | bytes 9175040 | tf_op jit(solution)/shard_map/dot_general | solution.py:84
  164.8 3.3 %collective-permute-start.10 = (f32[4096]{0:T(1024)S(1)}, f32[4096]{0:T(1024)S(1)}, u32[]{:S(2)}, u32[]{:S(2)}) collective-permute-start(f32[4096]{0:T(1024)S(1)} %add.131), channel_id=1, source_target_pairs={{0,32},{32,0},{8,40},{40,8},{16,48},{48,16},{24,56},{56,24},{1,33}... | collective-permute-start | bytes 49160 | tf_op jit(solution)/shard_map/ppermute | solution.py:16
  168.2 1.4 copy.10
  169.6 2.9 %collective-permute-done.10 = f32[4096]{0:T(1024)S(1)} collective-permute-done((f32[4096]{0:T(1024)S(1)}, f32[4096]{0:T(1024)S(1)}, u32[]{:S(2)}, u32[]{:S(2)}) %collective-permute-start.10) | collective-permute-done | bytes 16416 | tf_op jit(solution)/shard_map/ppermute | solution.py:16
  172.5 3.3 %collective-permute-start.5 = (f32[8,4096]{1,0:T(8,128)S(1)}, f32[8,4096]{1,0:T(8,128)S(1)}, u32[]{:S(2)}, u32[]{:S(2)}) collective-permute-start(f32[8,4096]{1,0:T(8,128)S(1)} %add_select_fusion), channel_id=1, source_target_pairs={{0,2},{2,0},{1,3},{3,1},{4,6},{6,4},{5,7},{7,5},{8,10},{10,8},{9,1... | collective-permute-start | bytes 393224 | tf_op jit(solution)/shard_map/ppermute | solution.py:16
  175.9 12.9 %multiply_reduce_fusion = (f32[768]{0:T(1024)S(1)}, bf16[4096,768]{1,0:T(8,128)(2,1)}) fusion(f32[768]{0:T(1024)S(1)} %copy-done.3, bf16[4096,768]{1,0:T(8,128)(2,1)} %param.7, f32[4096,768]{1,0:T(8,128)} %fusion.3, bf16[256,4096]{1,0:T(8,128)(2,1)} %collective-permute-done.2, bf16[32,2,8,768]{3,2,1,0:T(8,128)(2,1)S(1)} %bitcast.52, s32[]{:T(128)S(6)} %select_n.52), kind=kOutput, calls=%fused_computation | convolution fusion | flops 1645214976 | bytes 27663364 | tf_op jit(solution)/shard_map/dot_general | solution.py:98
  189.1 3.3 %collective-permute-done.12 = f32[768]{0:T(1024)S(1)} collective-permute-done((f32[768]{0:T(1024)S(1)}, f32[768]{0:T(1024)S(1)}, u32[]{:S(2)}, u32[]{:S(2)}) %collective-permute-start.12) | collective-permute-done | bytes 3104 | tf_op jit(solution)/shard_map/ppermute | solution.py:16
  192.4 0.8 collective-permute-start.13
  193.2 4.3 %collective-permute-done.13 = f32[768]{0:T(1024)S(1)} collective-permute-done((f32[768]{0:T(1024)S(1)}, f32[768]{0:T(1024)S(1)}, u32[]{:S(2)}, u32[]{:S(2)}) %collective-permute-start.13) | collective-permute-done | bytes 3104 | tf_op jit(solution)/shard_map/ppermute | solution.py:16
  198.1 0.6 add.133
  198.7 0.6 select_convert_fusion
  199.4 1.7 convert_element_type.50
  (46 shorter events, 4.2 us)
Async XLA Ops:
  7.2 125.9 %all-gather.2.cloned.1.call-start = ((), (), s32[]{:S(2)}) async-start(), calls=%async_computation.2 | async-start | bytes 2162688 | tf_op jit(solution)/shard_map/all_gather | solution.py:76
  9.1 9.0 %copy-start.1 = (bf16[128,768]{1,0:T(8,128)(2,1)S(1)}, bf16[128,768]{1,0:T(8,128)(2,1)}, u32[]{:S(2)}) copy-start(bf16[128,768]{1,0:T(8,128)(2,1)} %param.9) | copy-start | bytes 589828
  9.1 22.9 %collective-permute-start = (f32[8,4096]{1,0:T(8,128)S(1)}, f32[8,4096]{1,0:T(8,128)S(1)}, u32[]{:S(2)}, u32[]{:S(2)}) collective-permute-start(f32[8,4096]{1,0:T(8,128)S(1)} %mul.67), channel_id=1, source_target_pairs={{0,1},{1,0},{2,3},{3,2},{4,5},{5,4},{6,7},{7,6},{8,9},{9,8},{10,11... | collective-permute-start | bytes 393224 | tf_op jit(solution)/shard_map/ppermute | solution.py:16
  32.1 10.0 %copy-start.2 = (f32[4096]{0:T(1024)S(1)}, f32[4096]{0:T(1024)}, u32[]{:S(2)}) copy-start(f32[4096]{0:T(1024)} %param.6) | copy-start | bytes 49156
  32.1 10.0 %collective-permute-start.1 = (f32[8,4096]{1,0:T(8,128)S(1)}, f32[8,4096]{1,0:T(8,128)S(1)}, u32[]{:S(2)}, u32[]{:S(2)}) collective-permute-start(f32[8,4096]{1,0:T(8,128)S(1)} %add_select_fusion.1), channel_id=1, source_target_pairs={{0,2},{2,0},{1,3},{3,1},{4,6},{6,4},{5,7},{7,5},{8,10},{10,8},{9,1... | collective-permute-start | bytes 393224 | tf_op jit(solution)/shard_map/ppermute | solution.py:16
  45.2 4.4 %collective-permute-start.3 = (bf16[32,8,4096]{2,1,0:T(8,128)(2,1)S(1)}, bf16[32,8,4096]{2,1,0:T(8,128)(2,1)}, u32[]{:S(2)}, u32[]{:S(2)}) collective-permute-start(bf16[32,8,4096]{2,1,0:T(8,128)(2,1)S(1)} %fusion.1), channel_id=1, source_target_pairs={{0,4},{4,0},{1,5},{5,1},{2,6},{6,2},{3,7},{7,3},{8,12},{12,8},{9,1... | collective-permute-start | bytes 6291464 | tf_op jit(solution)/shard_map/ppermute | solution.py:107
  54.4 84.8 %all-to-all-start = ((bf16[32,8,4096]{2,1,0:T(8,128)(2,1)}), bf16[32,8,4096]{2,1,0:T(8,128)(2,1)S(1)}, u32[]{:S(2)}, u32[]{:S(2)}) async-start(bf16[32,8,4096]{2,1,0:T(8,128)(2,1)} %fusion), calls=%async_computation.1 | async-start | bytes 4194304 | tf_op jit(solution)/shard_map/all_to_all | solution.py:108
  66.0 133.4 %reduce-scatter.2.cloned.1.call-start = ((), (), s32[]{:S(2)}) async-start(), calls=%async_computation.3 | async-start | bytes 1966080 | tf_op jit(solution)/shard_map/reduce_scatter | solution.py:92
  133.1 26.5 %collective-permute-start.2 = (bf16[256,4096]{1,0:T(8,128)(2,1)}, bf16[256,4096]{1,0:T(8,128)(2,1)}, u32[]{:S(2)}, u32[]{:S(2)}) collective-permute-start(bf16[256,4096]{1,0:T(8,128)(2,1)} %all-gather.2.cloned.1.call-done), channel_id=1, source_target_pairs={{0,4},{4,0},{1,5},{5,1},{2,6},{6,2},{3,7},{7,3},{8,12},{12,8},{9,1... | collective-permute-start | bytes 6291464 | tf_op jit(solution)/shard_map/ppermute | solution.py:78
  139.5 9.1 %collective-permute-start.6 = (f32[4096]{0:T(1024)S(1)}, f32[4096]{0:T(1024)S(1)}, u32[]{:S(2)}, u32[]{:S(2)}) collective-permute-start(f32[4096]{0:T(1024)S(1)} %get-tuple-element.13), channel_id=1, source_target_pairs={{0,64},{64,0},{128,192},{192,128},{1,65},{65,1},{129,193},{193,129... | collective-permute-start | bytes 49160 | tf_op jit(solution)/shard_map/ppermute | solution.py:16
  148.6 5.5 %collective-permute-start.7 = (f32[4096]{0:T(1024)S(1)}, f32[4096]{0:T(1024)S(1)}, u32[]{:S(2)}, u32[]{:S(2)}) collective-permute-start(f32[4096]{0:T(1024)S(1)} %add.128), channel_id=1, source_target_pairs={{0,128},{128,0},{64,192},{192,64},{1,129},{129,1},{65,193},{193,65... | collective-permute-start | bytes 49160 | tf_op jit(solution)/shard_map/ppermute | solution.py:16
  154.2 3.7 %collective-permute-start.8 = (f32[4096]{0:T(1024)S(1)}, f32[4096]{0:T(1024)S(1)}, u32[]{:S(2)}, u32[]{:S(2)}) collective-permute-start(f32[4096]{0:T(1024)S(1)} %add.129), channel_id=1, source_target_pairs={{0,8},{8,0},{16,24},{24,16},{32,40},{40,32},{48,56},{56,48},{1,9},... | collective-permute-start | bytes 49160 | tf_op jit(solution)/shard_map/ppermute | solution.py:16
  155.3 17.3 %collective-permute-start.4 = (f32[8,4096]{1,0:T(8,128)S(1)}, f32[8,4096]{1,0:T(8,128)S(1)}, u32[]{:S(2)}, u32[]{:S(2)}) collective-permute-start(f32[8,4096]{1,0:T(8,128)S(1)} %mul.74), channel_id=1, source_target_pairs={{0,1},{1,0},{2,3},{3,2},{4,5},{5,4},{6,7},{7,6},{8,9},{9,8},{10,11... | collective-permute-start | bytes 393224 | tf_op jit(solution)/shard_map/ppermute | solution.py:16
  157.9 10.2 %copy-start = (f32[32,1,8,768]{3,2,0,1:T(8,128)S(1)}, f32[32,1,8,768]{3,2,0,1:T(8,128)}, u32[]{:S(2)}) copy-start(f32[32,1,8,768]{3,2,0,1:T(8,128)} %convolution_bitcast_fusion.1) | copy-start | bytes 2359300
  157.9 6.8 %collective-permute-start.9 = (f32[4096]{0:T(1024)S(1)}, f32[4096]{0:T(1024)S(1)}, u32[]{:S(2)}, u32[]{:S(2)}) collective-permute-start(f32[4096]{0:T(1024)S(1)} %add.130), channel_id=1, source_target_pairs={{0,16},{16,0},{8,24},{24,8},{32,48},{48,32},{40,56},{56,40},{1,17}... | collective-permute-start | bytes 49160 | tf_op jit(solution)/shard_map/ppermute | solution.py:16
  164.7 11.1 %copy-start.3 = (f32[768]{0:T(1024)S(1)}, f32[768]{0:T(1024)}, u32[]{:S(2)}) copy-start(f32[768]{0:T(1024)} %param.8) | copy-start | bytes 9220
  164.8 7.7 %collective-permute-start.10 = (f32[4096]{0:T(1024)S(1)}, f32[4096]{0:T(1024)S(1)}, u32[]{:S(2)}, u32[]{:S(2)}) collective-permute-start(f32[4096]{0:T(1024)S(1)} %add.131), channel_id=1, source_target_pairs={{0,32},{32,0},{8,40},{40,8},{16,48},{48,16},{24,56},{56,24},{1,33}... | collective-permute-start | bytes 49160 | tf_op jit(solution)/shard_map/ppermute | solution.py:16
  172.5 25.6 %collective-permute-start.11 = (f32[4096]{0:T(1024)S(1)}, f32[4096]{0:T(1024)S(1)}, u32[]{:S(2)}, u32[]{:S(2)}) collective-permute-start(f32[4096]{0:T(1024)S(1)} %add.132), channel_id=1, source_target_pairs={{0,4},{4,0},{1,5},{5,1},{2,6},{6,2},{3,7},{7,3},{8,12},{12,8},{9,1... | collective-permute-start | bytes 49160 | tf_op jit(solution)/shard_map/ppermute | solution.py:16
  172.5 26.2 %collective-permute-start.5 = (f32[8,4096]{1,0:T(8,128)S(1)}, f32[8,4096]{1,0:T(8,128)S(1)}, u32[]{:S(2)}, u32[]{:S(2)}) collective-permute-start(f32[8,4096]{1,0:T(8,128)S(1)} %add_select_fusion), channel_id=1, source_target_pairs={{0,2},{2,0},{1,3},{3,1},{4,6},{6,4},{5,7},{7,5},{8,10},{10,8},{9,1... | collective-permute-start | bytes 393224 | tf_op jit(solution)/shard_map/ppermute | solution.py:16
  188.8 3.6 %collective-permute-start.12 = (f32[768]{0:T(1024)S(1)}, f32[768]{0:T(1024)S(1)}, u32[]{:S(2)}, u32[]{:S(2)}) collective-permute-start(f32[768]{0:T(1024)S(1)} %get-tuple-element.11), channel_id=1, source_target_pairs={{0,1},{1,0},{2,3},{3,2},{4,5},{5,4},{6,7},{7,6},{8,9},{9,8},{10,11... | collective-permute-start | bytes 9224 | tf_op jit(solution)/shard_map/ppermute | solution.py:16
  192.4 5.1 %collective-permute-start.13 = (f32[768]{0:T(1024)S(1)}, f32[768]{0:T(1024)S(1)}, u32[]{:S(2)}, u32[]{:S(2)}) collective-permute-start(f32[768]{0:T(1024)S(1)} %add.134), channel_id=1, source_target_pairs={{0,2},{2,0},{1,3},{3,1},{4,6},{6,4},{5,7},{7,5},{8,10},{10,8},{9,1... | collective-permute-start | bytes 9224 | tf_op jit(solution)/shard_map/ppermute | solution.py:16
Sparse Core Ops, SparseCore 0:
  45.5 87.5 all-gather.1
  169.7 27.5 reduce-scatter.1

commit v6 on v4

--- a/solution.py
+++ b/solution.py
@@ -73,15 +73,8 @@
         all_cot, quant_weight, (((1,), (1,)), ((), ())), preferred_element_type=jnp.float32
     ).reshape(chips, cores, rows, width)
     quant_act, partial = lax.optimization_barrier((quant_act, partial))
-    half_act = lax.all_gather(quant_act, CHIPS, axis=0, tiled=True)
+    all_act = lax.all_gather(quant_act, DP, axis=0, tiled=True)
     pair = [(0, 1), (1, 0)]
-    partner_act = lax.ppermute(half_act, "dc", pair)
-    both_act = jnp.where(
-        core == 0, jnp.stack([half_act, partner_act]), jnp.stack([partner_act, half_act])
-    )
-    all_act = (
-        both_act.reshape(cores, chips, rows, width).transpose(1, 0, 2, 3).reshape(-1, width)
-    )
     block = all_act
     projected = lax.psum_scatter(
         jnp.dot(block, quant_weight, preferred_element_type=jnp.float32),

time: 199 us -> 194 us (0.975)
  blocking collectives: 14 us -> 80.1 us
  waiting for transfers between devices: 87.1 us -> 28.7 us
  starting transfers between devices: 29.4 us -> 20.1 us
  other arithmetic: 21 us -> 15.3 us
    all_gather x1, waiting for transfers between devices: 68.5 us -> 0.01 us  [body(): all_act = lax.all_gather(quant_act, DP, axis=0, tiled=True)]
    all_to_all x0 -> x1, blocking collectives: none -> 66.2 us  [body(): lax.all_to_all(chip_sum.astype(jnp.bfloat16), CHIPS, 0, 0, tiled=True)]
    all_to_all x1 -> x0, starting transfers between devices: 11.6 us -> none  [body(): lax.all_to_all(chip_sum.astype(jnp.bfloat16), CHIPS, 0, 0, tiled=True)]
    ppermute x12, waiting for transfers between devices: 13.7 us -> 21.7 us  [swapped(): return lax.ppermute(block, axis, route)]
    select_n x1 -> x0, other arithmetic: 4.33 us -> none  [body(): jnp.where(core == 0, jnp.stack([half_act, partner_act]), jnp.stack([partn...]
    ppermute x12, starting transfers between devices: 17.7 us -> 20 us  [swapped(): return lax.ppermute(block, axis, route)]
    reduce_scatter x1, waiting for transfers between devices: 0.61 us -> 2.76 us  [body(): lax.psum_scatter(jnp.dot(block, quant_weight, preferred_element_type=jnp....]
  transfers between devices with their start and end apart: 17 -> 15, of which waited for: 8 -> 9; matrix products, arithmetic and copies ran while one was open for 24% -> 22% of each run, Pallas kernels for 0% -> 0%
where the time goes in v6:
time: 194 us; the launch traced here: 193 us
  blocking collectives  80.1 us (41%)
  matrix products  31 us (16%)
  waiting for transfers between devices  28.7 us (15%)
  starting transfers between devices  20.1 us (10%)
  other arithmetic  15.3 us (8%)
  between operations  14.2 us (7%)
  local copies, waits for them, and re-layouts  3.84 us (2%)
    all_to_all x1, blocking collectives, body(): lax.all_to_all(chip_sum.astype(jnp.bfloat16), CHIPS, 0, 0, tiled=True)  66.2 us
    ppermute x12, waiting for transfers between devices, swapped(): return lax.ppermute(block, axis, route)  21.7 us
    ppermute x12, starting transfers between devices, swapped(): return lax.ppermute(block, axis, route)  20 us
    all_gather x1, blocking collectives, body(): all_cot = lax.all_gather(cotangent, 'tensor', axis=0, tiled=True)  14 us
    dot_general x1, matrix products, body(): lax.dot_general(all_act, all_cot, (((0,), (0,)), ((), ())), preferred_ele...  12.5 us
    dot_general x1, matrix products, body(): jnp.dot(block, quant_weight, preferred_element_type=jnp.float32)  8.63 us
    dot_general x1, matrix products, body(): lax.dot_general(all_cot, quant_weight, (((1,), (1,)), ((), ())), preferre...  8.42 us
    convert_element_type x1, other arithmetic, body(): quant_weight = (clip_weight * tanh_weight).astype(jnp.bfloat16)  7.31 us
  transfers between devices with their start and end apart: 15, of which 9 were waited for; matrix products, arithmetic and copies ran while one was open for 22% of the time, Pallas kernels for 0%

profile of v6, /device:TPU:2, one launch (start us, length us, event | category | flops | bytes accessed | tf_op | source)
XLA Modules:
  0.0 193.4 jit_solution(18445984445501119298)
XLA Ops:
  7.2 1.0 reshape.28
  9.1 1.7 collective-permute-start
  10.8 7.3 %multiply_convert_fusion.1 = bf16[4096,768]{1,0:T(8,128)(2,1)} fusion(f32[768]{0:T(1024)} %param.8, bf16[4096,768]{1,0:T(8,128)(2,1)} %param.7), kind=kLoop, calls=%fused_computation.3 | loop fusion | flops 12582912 | bytes 12585984 | tf_op jit(solution)/shard_map/convert_element_type | solution.py:70
  18.1 14.0 %all_gather.6 = bf16[512,768]{1,0:T(8,128)(2,1)S(1)} all-gather(bf16[128,768]{1,0:T(8,128)(2,1)S(1)} %copy-done), channel_id=1, replica_groups=mesh['dx'=4,'dz'=8,'dc'=2,'tensor'=4] {'tensor'}, dimensions={0}, use_global_device_ids=true | all-gather | bytes 983040 | tf_op jit(solution)/shard_map/all_gather | solution.py:71
  32.1 1.5 collective-permute-start.1
  33.6 8.4 %fusion.35 = f32[4096,512]{0,1:T(8,128)} fusion(bf16[4096,768]{1,0:T(8,128)(2,1)} %multiply_convert_fusion.1, bf16[512,768]{1,0:T(8,128)(2,1)S(1)} %all_gather.6), kind=kOutput, calls=%fused_computation.55 | convolution fusion | flops 3221225472 | bytes 15466496 | tf_op jit(solution)/shard_map/dot_general | solution.py:72
  42.1 0.7 multiply_convert_fusion.2
  42.7 2.5 %fusion.1 = bf16[32,8,4096]{2,1,0:T(8,128)(2,1)S(1)} fusion(f32[32,2,8,4096]{3,2,1,0:T(8,128)} %bitcast.32, s32[]{:T(128)S(6)} %select_n.34), kind=kLoop, calls=%fused_computation.9 | loop fusion | bytes 4194308 | tf_op jit(solution)/shard_map/convert_element_type | solution.py:94
  45.4 4.2 %collective-permute-done.2 = bf16[32,8,4096]{2,1,0:T(8,128)(2,1)} collective-permute-done((bf16[32,8,4096]{2,1,0:T(8,128)(2,1)S(1)}, bf16[32,8,4096]{2,1,0:T(8,128)(2,1)}, u32[]{:S(2)}, u32[]{:S(2)}) %collective-permute-start.2) | collective-permute-done | bytes 2097184 | tf_op jit(solution)/shard_map/ppermute | solution.py:94
  49.6 3.4 %fusion = bf16[32,8,4096]{2,1,0:T(8,128)(2,1)S(1)} fusion(bf16[32,8,4096]{2,1,0:T(8,128)(2,1)} %collective-permute-done.2, f32[32,2,8,4096]{3,2,1,0:T(8,128)} %bitcast.33, s32[]{:T(128)S(6)} %select_n.33), kind=kLoop, calls=%fused_computation.6 | loop fusion | flops 3145728 | bytes 8388612 | tf_op jit(solution)/shard_map/convert_element_type | solution.py:95
  53.0 66.2 %all_to_all.5 = bf16[32,8,4096]{2,1,0:T(8,128)(2,1)S(1)} all-to-all(bf16[32,8,4096]{2,1,0:T(8,128)(2,1)S(1)} %fusion), channel_id=1, replica_groups=mesh['dx'=4,'dz'=8,'dc'=2,'tensor'=4] {'dx','dz'}, dimensions={0} | all-to-all | bytes 4194304 | tf_op jit(solution)/shard_map/all_to_all | solution.py:95
  120.5 1.6 collective-permute-start.3
  122.1 2.7 %collective-permute-start.5 = (f32[4096]{0:T(1024)S(1)}, f32[4096]{0:T(1024)S(1)}, u32[]{:S(2)}, u32[]{:S(2)}) collective-permute-start(f32[4096]{0:T(1024)S(1)} %get-tuple-element.13), channel_id=1, source_target_pairs={{0,64},{64,0},{128,192},{192,128},{1,65},{65,1},{129,193},{193,129... | collective-permute-start | bytes 49160 | tf_op jit(solution)/shard_map/ppermute | solution.py:16
  124.8 1.8 collective-permute-done.5
  126.6 1.2 collective-permute-start.6
  127.7 4.1 %collective-permute-done.6 = f32[4096]{0:T(1024)S(1)} collective-permute-done((f32[4096]{0:T(1024)S(1)}, f32[4096]{0:T(1024)S(1)}, u32[]{:S(2)}, u32[]{:S(2)}) %collective-permute-start.6) | collective-permute-done | bytes 16416 | tf_op jit(solution)/shard_map/ppermute | solution.py:16
  131.8 3.0 %collective-permute-start.7 = (f32[4096]{0:T(1024)S(1)}, f32[4096]{0:T(1024)S(1)}, u32[]{:S(2)}, u32[]{:S(2)}) collective-permute-start(f32[4096]{0:T(1024)S(1)} %add.122), channel_id=1, source_target_pairs={{0,8},{8,0},{16,24},{24,16},{32,40},{40,32},{48,56},{56,48},{1,9},... | collective-permute-start | bytes 49160 | tf_op jit(solution)/shard_map/ppermute | solution.py:16
  134.8 1.7 collective-permute-done.7
  136.5 2.7 %collective-permute-start.8 = (f32[4096]{0:T(1024)S(1)}, f32[4096]{0:T(1024)S(1)}, u32[]{:S(2)}, u32[]{:S(2)}) collective-permute-start(f32[4096]{0:T(1024)S(1)} %add.123), channel_id=1, source_target_pairs={{0,16},{16,0},{8,24},{24,8},{32,48},{48,32},{40,56},{56,40},{1,17}... | collective-permute-start | bytes 49160 | tf_op jit(solution)/shard_map/ppermute | solution.py:16
  139.3 1.9 collective-permute-done.8
  141.2 1.8 collective-permute-start.9
  142.9 5.9 %collective-permute-done.9 = f32[4096]{0:T(1024)S(1)} collective-permute-done((f32[4096]{0:T(1024)S(1)}, f32[4096]{0:T(1024)S(1)}, u32[]{:S(2)}, u32[]{:S(2)}) %collective-permute-start.9) | collective-permute-done | bytes 16416 | tf_op jit(solution)/shard_map/ppermute | solution.py:16
  148.9 2.3 %collective-permute-start.4 = (f32[8,4096]{1,0:T(8,128)S(1)}, f32[8,4096]{1,0:T(8,128)S(1)}, u32[]{:S(2)}, u32[]{:S(2)}) collective-permute-start(f32[8,4096]{1,0:T(8,128)S(1)} %add_select_fusion), channel_id=1, source_target_pairs={{0,2},{2,0},{1,3},{3,1},{4,6},{6,4},{5,7},{7,5},{8,10},{10,8},{9,1... | collective-permute-start | bytes 393224 | tf_op jit(solution)/shard_map/ppermute | solution.py:16
  151.2 8.6 %fusion.36 = f32[512,768]{1,0:T(8,128)} fusion(bf16[512,4096]{1,0:T(8,128)(2,1)} %all-gather.2.cloned.1.call-done, bf16[4096,768]{1,0:T(8,128)(2,1)} %multiply_convert_fusion.1), kind=kOutput, calls=%fused_computation.56 | convolution fusion | flops 3221225472 | bytes 12058624 | tf_op jit(solution)/shard_map/dot_general | solution.py:80
  159.9 12.5 %multiply_reduce_fusion = (f32[768]{0:T(1024)S(1)}, bf16[4096,768]{1,0:T(8,128)(2,1)}) fusion(f32[768]{0:T(1024)S(1)} %copy-done.2, bf16[4096,768]{1,0:T(8,128)(2,1)} %param.7, bf16[512,4096]{1,0:T(8,128)(2,1)} %all-gather.2.cloned.1.call-done, bf16[512,768]{1,0:T(8,128)(2,1)S(1)} %all_gather.6), kind=kOutput, calls=%fused_computation | convolution fusion | flops 3252681984 | bytes 17569792 | tf_op jit(solution)/shard_map/dot_general | solution.py:85
  172.4 0.6 add.126
  173.0 3.1 %collective-permute-done.11 = f32[768]{0:T(1024)S(1)} collective-permute-done((f32[768]{0:T(1024)S(1)}, f32[768]{0:T(1024)S(1)}, u32[]{:S(2)}, u32[]{:S(2)}) %collective-permute-start.11) | collective-permute-done | bytes 3104 | tf_op jit(solution)/shard_map/ppermute | solution.py:16
  176.2 1.5 collective-permute-start.12
  177.6 0.6 select_convert_fusion
  178.3 3.2 %collective-permute-done.12 = f32[768]{0:T(1024)S(1)} collective-permute-done((f32[768]{0:T(1024)S(1)}, f32[768]{0:T(1024)S(1)}, u32[]{:S(2)}, u32[]{:S(2)}) %collective-permute-start.12) | collective-permute-done | bytes 3104 | tf_op jit(solution)/shard_map/ppermute | solution.py:16
  182.1 2.8 %reduce-scatter.2.cloned.1.call-done = f32[128,768]{1,0:T(8,128)} async-done(((f32[512,768]{1,0:T(8,128)}), f32[128,768]{1,0:T(8,128)}) %reduce-scatter.2.cloned.1.call-update) | async-done | bytes 393232 | tf_op jit(solution)/shard_map/reduce_scatter | solution.py:79
  184.8 1.7 convert_element_type.50
  (37 shorter events, 3.2 us)
Async XLA Ops:
  7.2 144.1 %all-gather.2.cloned.1.call-start = ((), (), s32[]{:S(2)}) async-start(), calls=%async_computation.2 | async-start | bytes 4259840 | tf_op jit(solution)/shard_map/all_gather | solution.py:76
  9.1 9.0 %copy-start = (bf16[128,768]{1,0:T(8,128)(2,1)S(1)}, bf16[128,768]{1,0:T(8,128)(2,1)}, u32[]{:S(2)}) copy-start(bf16[128,768]{1,0:T(8,128)(2,1)} %param.9) | copy-start | bytes 589828
  9.1 23.0 %collective-permute-start = (f32[8,4096]{1,0:T(8,128)S(1)}, f32[8,4096]{1,0:T(8,128)S(1)}, u32[]{:S(2)}, u32[]{:S(2)}) collective-permute-start(f32[8,4096]{1,0:T(8,128)S(1)} %mul.67), channel_id=1, source_target_pairs={{0,1},{1,0},{2,3},{3,2},{4,5},{5,4},{6,7},{7,6},{8,9},{9,8},{10,11... | collective-permute-start | bytes 393224 | tf_op jit(solution)/shard_map/ppermute | solution.py:16
  32.1 10.0 %copy-start.1 = (f32[4096]{0:T(1024)S(1)}, f32[4096]{0:T(1024)}, u32[]{:S(2)}) copy-start(f32[4096]{0:T(1024)} %param.6) | copy-start | bytes 49156
  32.1 10.0 %collective-permute-start.1 = (f32[8,4096]{1,0:T(8,128)S(1)}, f32[8,4096]{1,0:T(8,128)S(1)}, u32[]{:S(2)}, u32[]{:S(2)}) collective-permute-start(f32[8,4096]{1,0:T(8,128)S(1)} %add_select_fusion.1), channel_id=1, source_target_pairs={{0,2},{2,0},{1,3},{3,1},{4,6},{6,4},{5,7},{7,5},{8,10},{10,8},{9,1... | collective-permute-start | bytes 393224 | tf_op jit(solution)/shard_map/ppermute | solution.py:16
  45.2 4.4 %collective-permute-start.2 = (bf16[32,8,4096]{2,1,0:T(8,128)(2,1)S(1)}, bf16[32,8,4096]{2,1,0:T(8,128)(2,1)}, u32[]{:S(2)}, u32[]{:S(2)}) collective-permute-start(bf16[32,8,4096]{2,1,0:T(8,128)(2,1)S(1)} %fusion.1), channel_id=1, source_target_pairs={{0,4},{4,0},{1,5},{5,1},{2,6},{6,2},{3,7},{7,3},{8,12},{12,8},{9,1... | collective-permute-start | bytes 6291464 | tf_op jit(solution)/shard_map/ppermute | solution.py:94
  45.3 139.5 %reduce-scatter.2.cloned.1.call-start = ((), (), s32[]{:S(2)}) async-start(), calls=%async_computation.3 | async-start | bytes 1966080 | tf_op jit(solution)/shard_map/reduce_scatter | solution.py:79
  120.5 28.3 %collective-permute-start.3 = (f32[8,4096]{1,0:T(8,128)S(1)}, f32[8,4096]{1,0:T(8,128)S(1)}, u32[]{:S(2)}, u32[]{:S(2)}) collective-permute-start(f32[8,4096]{1,0:T(8,128)S(1)} %mul.74), channel_id=1, source_target_pairs={{0,1},{1,0},{2,3},{3,2},{4,5},{5,4},{6,7},{7,6},{8,9},{9,8},{10,11... | collective-permute-start | bytes 393224 | tf_op jit(solution)/shard_map/ppermute | solution.py:16
  122.1 4.4 %collective-permute-start.5 = (f32[4096]{0:T(1024)S(1)}, f32[4096]{0:T(1024)S(1)}, u32[]{:S(2)}, u32[]{:S(2)}) collective-permute-start(f32[4096]{0:T(1024)S(1)} %get-tuple-element.13), channel_id=1, source_target_pairs={{0,64},{64,0},{128,192},{192,128},{1,65},{65,1},{129,193},{193,129... | collective-permute-start | bytes 49160 | tf_op jit(solution)/shard_map/ppermute | solution.py:16
  126.6 5.2 %collective-permute-start.6 = (f32[4096]{0:T(1024)S(1)}, f32[4096]{0:T(1024)S(1)}, u32[]{:S(2)}, u32[]{:S(2)}) collective-permute-start(f32[4096]{0:T(1024)S(1)} %add.121), channel_id=1, source_target_pairs={{0,128},{128,0},{64,192},{192,64},{1,129},{129,1},{65,193},{193,65... | collective-permute-start | bytes 49160 | tf_op jit(solution)/shard_map/ppermute | solution.py:16
  131.8 4.7 %collective-permute-start.7 = (f32[4096]{0:T(1024)S(1)}, f32[4096]{0:T(1024)S(1)}, u32[]{:S(2)}, u32[]{:S(2)}) collective-permute-start(f32[4096]{0:T(1024)S(1)} %add.122), channel_id=1, source_target_pairs={{0,8},{8,0},{16,24},{24,16},{32,40},{40,32},{48,56},{56,48},{1,9},... | collective-permute-start | bytes 49160 | tf_op jit(solution)/shard_map/ppermute | solution.py:16
  136.5 4.6 %collective-permute-start.8 = (f32[4096]{0:T(1024)S(1)}, f32[4096]{0:T(1024)S(1)}, u32[]{:S(2)}, u32[]{:S(2)}) collective-permute-start(f32[4096]{0:T(1024)S(1)} %add.123), channel_id=1, source_target_pairs={{0,16},{16,0},{8,24},{24,8},{32,48},{48,32},{40,56},{56,40},{1,17}... | collective-permute-start | bytes 49160 | tf_op jit(solution)/shard_map/ppermute | solution.py:16
  141.2 7.6 %collective-permute-start.9 = (f32[4096]{0:T(1024)S(1)}, f32[4096]{0:T(1024)S(1)}, u32[]{:S(2)}, u32[]{:S(2)}) collective-permute-start(f32[4096]{0:T(1024)S(1)} %add.124), channel_id=1, source_target_pairs={{0,32},{32,0},{8,40},{40,8},{16,48},{48,16},{24,56},{56,24},{1,33}... | collective-permute-start | bytes 49160 | tf_op jit(solution)/shard_map/ppermute | solution.py:16
  148.8 23.6 %collective-permute-start.10 = (f32[4096]{0:T(1024)S(1)}, f32[4096]{0:T(1024)S(1)}, u32[]{:S(2)}, u32[]{:S(2)}) collective-permute-start(f32[4096]{0:T(1024)S(1)} %add.125), channel_id=1, source_target_pairs={{0,4},{4,0},{1,5},{5,1},{2,6},{6,2},{3,7},{7,3},{8,12},{12,8},{9,1... | collective-permute-start | bytes 49160 | tf_op jit(solution)/shard_map/ppermute | solution.py:16
  148.9 11.0 %copy-start.2 = (f32[768]{0:T(1024)S(1)}, f32[768]{0:T(1024)}, u32[]{:S(2)}) copy-start(f32[768]{0:T(1024)} %param.8) | copy-start | bytes 9220
  148.9 28.7 %collective-permute-start.4 = (f32[8,4096]{1,0:T(8,128)S(1)}, f32[8,4096]{1,0:T(8,128)S(1)}, u32[]{:S(2)}, u32[]{:S(2)}) collective-permute-start(f32[8,4096]{1,0:T(8,128)S(1)} %add_select_fusion), channel_id=1, source_target_pairs={{0,2},{2,0},{1,3},{3,1},{4,6},{6,4},{5,7},{7,5},{8,10},{10,8},{9,1... | collective-permute-start | bytes 393224 | tf_op jit(solution)/shard_map/ppermute | solution.py:16
  172.3 3.8 %collective-permute-start.11 = (f32[768]{0:T(1024)S(1)}, f32[768]{0:T(1024)S(1)}, u32[]{:S(2)}, u32[]{:S(2)}) collective-permute-start(f32[768]{0:T(1024)S(1)} %get-tuple-element.11), channel_id=1, source_target_pairs={{0,1},{1,0},{2,3},{3,2},{4,5},{5,4},{6,7},{7,6},{8,9},{9,8},{10,11... | collective-permute-start | bytes 9224 | tf_op jit(solution)/shard_map/ppermute | solution.py:16
  176.2 5.3 %collective-permute-start.12 = (f32[768]{0:T(1024)S(1)}, f32[768]{0:T(1024)S(1)}, u32[]{:S(2)}, u32[]{:S(2)}) collective-permute-start(f32[768]{0:T(1024)S(1)} %add.127), channel_id=1, source_target_pairs={{0,2},{2,0},{1,3},{3,1},{4,6},{6,4},{5,7},{7,5},{8,10},{10,8},{9,1... | collective-permute-start | bytes 9224 | tf_op jit(solution)/shard_map/ppermute | solution.py:16
Sparse Core Ops, SparseCore 0:
  45.5 88.2 all-gather.1
  160.0 24.8 reduce-scatter.1

commit v7 on v6

--- a/solution.py
+++ b/solution.py
@@ -68,16 +68,22 @@
     ratio_weight = weight.astype(jnp.float32) / clip_weight
     tanh_weight = jnp.tanh(ratio_weight)
     quant_weight = (clip_weight * tanh_weight).astype(jnp.bfloat16)
+    quant_act, quant_weight = lax.optimization_barrier((quant_act, quant_weight))
+    all_act = lax.all_gather(quant_act, DP, axis=0, tiled=True)
     all_cot = lax.all_gather(cotangent, "tensor", axis=0, tiled=True)
     partial = lax.dot_general(
         all_cot, quant_weight, (((1,), (1,)), ((), ())), preferred_element_type=jnp.float32
     ).reshape(chips, cores, rows, width)
-    quant_act, partial = lax.optimization_barrier((quant_act, partial))
-    all_act = lax.all_gather(quant_act, DP, axis=0, tiled=True)
     pair = [(0, 1), (1, 0)]
+    mine = lax.dynamic_index_in_dim(partial, core, axis=1, keepdims=False)
+    other = lax.dynamic_index_in_dim(partial, cores - 1 - core, axis=1, keepdims=False)
+    chip_sum = mine + lax.ppermute(other.astype(jnp.bfloat16), "dc", pair).astype(jnp.float32)
+    pieces = lax.all_to_all(chip_sum.astype(jnp.bfloat16), CHIPS, 0, 0, tiled=True)
+    all_act, pieces = lax.optimization_barrier((all_act, pieces))
     block = all_act
+    proj_part = jnp.dot(block, quant_weight, preferred_element_type=jnp.float32)
     projected = lax.psum_scatter(
-        jnp.dot(block, quant_weight, preferred_element_type=jnp.float32),
+        proj_part,
         "tensor",
         scatter_dimension=0,
         tiled=True,
@@ -89,12 +95,9 @@
     weight_grad = (weight_prod * slope_weight).astype(jnp.bfloat16)
     weight_terms = jnp.sum(weight_prod * (tanh_weight - ratio_weight * slope_weight), axis=0)
     clip_weight_grad = butterfly_sum(weight_terms, "tensor")
-    mine = lax.dynamic_index_in_dim(partial, core, axis=1, keepdims=False)
-    other = lax.dynamic_index_in_dim(partial, cores - 1 - core, axis=1, keepdims=False)
-    chip_sum = mine + lax.ppermute(other.astype(jnp.bfloat16), "dc", pair).astype(jnp.float32)
-    pieces = lax.all_to_all(chip_sum.astype(jnp.bfloat16), CHIPS, 0, 0, tiled=True)
     act_prod = jnp.sum(pieces.astype(jnp.float32), axis=0)
     act_terms = jnp.sum(act_prod * edge_act, axis=0)
+    act_terms, _ = lax.optimization_barrier((act_terms, proj_part))
     for axis in DP:
         act_terms = butterfly_sum(act_terms, axis)
     clip_act_grad = act_terms

time: 194 us -> 198 us (1.021)
  blocking collectives: 80.1 us -> 82.9 us
  starting transfers between devices: 20.1 us -> 22.9 us
  matrix products: 31 us -> 28.3 us
    all_gather x1, waiting for transfers between devices: 0.01 us -> 3.37 us  [body(): all_act = lax.all_gather(quant_act, DP, axis=0, tiled=True)]
    unnamed x6 -> x8, local copies, waits for them, and re-layouts: 0.02 us -> 3.23 us
    all_to_all x1, blocking collectives: 66.2 us -> 69.2 us  [body(): lax.all_to_all(chip_sum.astype(jnp.bfloat16), CHIPS, 0, 0, tiled=True)]
    dot_general x1, matrix products: 8.42 us -> 5.57 us  [body(): lax.dot_general(all_cot, quant_weight, (((1,), (1,)), ((), ())), preferre...]
    ppermute x12, starting transfers between devices: 20 us -> 22.7 us  [swapped(): return lax.ppermute(block, axis, route)]
    reduce_scatter x1, waiting for transfers between devices: 2.76 us -> 0.01 us  [body(): lax.psum_scatter(proj_part, 'tensor', scatter_dimension=0, tiled=True)]
    convert_element_type x1, local copies, waits for them, and re-layouts: 2.46 us -> 0.27 us  [body(): other.astype(jnp.bfloat16)]
  transfers between devices with their start and end apart: 15 -> 15, of which waited for: 9 -> 9; matrix products, arithmetic and copies ran while one was open for 22% -> 20% of each run, Pallas kernels for 0% -> 0%
where the time goes in v7:
time: 198 us; the launch traced here: 196 us
  blocking collectives  82.9 us (42%)
  matrix products  28.3 us (14%)
  waiting for transfers between devices  27.6 us (14%)
  starting transfers between devices  22.9 us (12%)
  other arithmetic  15.4 us (8%)
  between operations  14.2 us (7%)
  local copies, waits for them, and re-layouts  4.87 us (2%)
    all_to_all x1, blocking collectives, body(): lax.all_to_all(chip_sum.astype(jnp.bfloat16), CHIPS, 0, 0, tiled=True)  69.2 us
    ppermute x12, starting transfers between devices, swapped(): return lax.ppermute(block, axis, route)  22.7 us
    ppermute x12, waiting for transfers between devices, swapped(): return lax.ppermute(block, axis, route)  19.9 us
    all_gather x1, blocking collectives, body(): all_cot = lax.all_gather(cotangent, 'tensor', axis=0, tiled=True)  13.6 us
    dot_general x1, matrix products, body(): lax.dot_general(all_act, all_cot, (((0,), (0,)), ((), ())), preferred_ele...  12.6 us
    dot_general x1, matrix products, body(): proj_part = jnp.dot(block, quant_weight, preferred_element_type=jnp.float32)  8.63 us
    convert_element_type x1, other arithmetic, body(): quant_weight = (clip_weight * tanh_weight).astype(jnp.bfloat16)  7.31 us
    dot_general x1, matrix products, body(): lax.dot_general(all_cot, quant_weight, (((1,), (1,)), ((), ())), preferre...  5.57 us
  transfers between devices with their start and end apart: 15, of which 9 were waited for; matrix products, arithmetic and copies ran while one was open for 20% of the time, Pallas kernels for 0%

profile of v7, /device:TPU:2, one launch (start us, length us, event | category | flops | bytes accessed | tf_op | source)
XLA Modules:
  0.0 196.1 jit_solution(5010458219826886488)
XLA Ops:
  7.2 1.0 reshape.28
  9.1 1.7 collective-permute-start
  10.8 7.3 %multiply_convert_fusion.1 = bf16[4096,768]{1,0:T(8,128)(2,1)} fusion(f32[768]{0:T(1024)} %param.8, bf16[4096,768]{1,0:T(8,128)(2,1)} %param.7), kind=kLoop, calls=%fused_computation.3 | loop fusion | flops 12582912 | bytes 12585984 | tf_op jit(solution)/shard_map/convert_element_type | solution.py:70
  18.1 3.0 %collective-permute-start.1 = (f32[8,4096]{1,0:T(8,128)S(1)}, f32[8,4096]{1,0:T(8,128)S(1)}, u32[]{:S(2)}, u32[]{:S(2)}) collective-permute-start(f32[8,4096]{1,0:T(8,128)S(1)} %add_select_fusion.1), channel_id=1, source_target_pairs={{0,2},{2,0},{1,3},{3,1},{4,6},{6,4},{5,7},{7,5},{8,10},{10,8},{9,1... | collective-permute-start | bytes 393224 | tf_op jit(solution)/shard_map/ppermute | solution.py:16
  21.1 13.6 %all_gather.7 = bf16[512,768]{1,0:T(8,128)(2,1)S(1)} all-gather(bf16[128,768]{1,0:T(8,128)(2,1)S(1)} %copy-done.1), channel_id=1, replica_groups=mesh['dx'=4,'dz'=8,'dc'=2,'tensor'=4] {'tensor'}, dimensions={0}, use_global_device_ids=true | all-gather | bytes 983040 | tf_op jit(solution)/shard_map/all_gather | solution.py:73
  34.7 0.7 multiply_convert_fusion.2
  35.5 5.6 %fusion.35 = f32[4096,512]{0,1:T(8,128)S(1)} fusion(bf16[4096,768]{1,0:T(8,128)(2,1)} %multiply_convert_fusion.1, bf16[512,768]{1,0:T(8,128)(2,1)S(1)} %all_gather.7), kind=kOutput, calls=%fused_computation.55 | convolution fusion | flops 3221225472 | bytes 15466496 | tf_op jit(solution)/shard_map/dot_general | solution.py:74
  41.1 3.2 %copy-done = f32[4096,512]{0,1:T(8,128)} copy-done((f32[4096,512]{0,1:T(8,128)}, f32[4096,512]{0,1:T(8,128)S(1)}, u32[]{:S(2)}) %copy-start) | copy-done | bytes 8388632
  44.7 4.3 %collective-permute-done.2 = bf16[32,8,4096]{2,1,0:T(8,128)(2,1)} collective-permute-done((bf16[32,8,4096]{2,1,0:T(8,128)(2,1)S(1)}, bf16[32,8,4096]{2,1,0:T(8,128)(2,1)}, u32[]{:S(2)}, u32[]{:S(2)}) %collective-permute-start.2) | collective-permute-done | bytes 2097184 | tf_op jit(solution)/shard_map/ppermute | solution.py:80
  49.0 3.4 %fusion = bf16[32,8,4096]{2,1,0:T(8,128)(2,1)S(1)} fusion(bf16[32,8,4096]{2,1,0:T(8,128)(2,1)} %collective-permute-done.2, f32[32,2,8,4096]{3,2,1,0:T(8,128)} %bitcast.33, s32[]{:T(128)S(6)} %select_n.33), kind=kLoop, calls=%fused_computation.6 | loop fusion | flops 3145728 | bytes 8388612 | tf_op jit(solution)/shard_map/convert_element_type | solution.py:81
  52.4 69.2 %all_to_all.5 = bf16[32,8,4096]{2,1,0:T(8,128)(2,1)S(1)} all-to-all(bf16[32,8,4096]{2,1,0:T(8,128)(2,1)S(1)} %fusion), channel_id=1, replica_groups=mesh['dx'=4,'dz'=8,'dc'=2,'tensor'=4] {'dx','dz'}, dimensions={0} | all-to-all | bytes 4194304 | tf_op jit(solution)/shard_map/all_to_all | solution.py:81
  121.6 3.4 %all-gather.2.cloned.1.call-done = bf16[512,4096]{1,0:T(8,128)(2,1)} async-done(((bf16[8,4096]{1,0:T(8,128)(2,1)}), bf16[512,4096]{1,0:T(8,128)(2,1)}) %all-gather.2.cloned.1.call-update) | async-done | bytes 4194320 | tf_op jit(solution)/shard_map/all_gather | solution.py:72
  126.4 0.9 collective-permute-start.3
  127.3 8.6 %fusion.36 = f32[512,768]{1,0:T(8,128)} fusion(bf16[512,4096]{1,0:T(8,128)(2,1)} %all-gather.2.cloned.1.call-done, bf16[4096,768]{1,0:T(8,128)(2,1)} %multiply_convert_fusion.1), kind=kOutput, calls=%fused_computation.56 | convolution fusion | flops 3221225472 | bytes 12058624 | tf_op jit(solution)/shard_map/dot_general | solution.py:84
  135.9 2.1 %collective-permute-start.5 = (f32[4096]{0:T(1024)S(1)}, f32[4096]{0:T(1024)S(1)}, u32[]{:S(2)}, u32[]{:S(2)}) collective-permute-start(f32[4096]{0:T(1024)S(1)} %get-tuple-element.14), channel_id=1, source_target_pairs={{0,64},{64,0},{128,192},{192,128},{1,65},{65,1},{129,193},{193,129... | collective-permute-start | bytes 49160 | tf_op jit(solution)/shard_map/ppermute | solution.py:16
  138.0 1.7 collective-permute-done.5
  139.7 2.2 %collective-permute-start.6 = (f32[4096]{0:T(1024)S(1)}, f32[4096]{0:T(1024)S(1)}, u32[]{:S(2)}, u32[]{:S(2)}) collective-permute-start(f32[4096]{0:T(1024)S(1)} %add.121), channel_id=1, source_target_pairs={{0,128},{128,0},{64,192},{192,64},{1,129},{129,1},{65,193},{193,65... | collective-permute-start | bytes 49160 | tf_op jit(solution)/shard_map/ppermute | solution.py:16
  141.9 3.0 %collective-permute-done.6 = f32[4096]{0:T(1024)S(1)} collective-permute-done((f32[4096]{0:T(1024)S(1)}, f32[4096]{0:T(1024)S(1)}, u32[]{:S(2)}, u32[]{:S(2)}) %collective-permute-start.6) | collective-permute-done | bytes 16416 | tf_op jit(solution)/shard_map/ppermute | solution.py:16
  145.0 2.8 %collective-permute-start.7 = (f32[4096]{0:T(1024)S(1)}, f32[4096]{0:T(1024)S(1)}, u32[]{:S(2)}, u32[]{:S(2)}) collective-permute-start(f32[4096]{0:T(1024)S(1)} %add.122), channel_id=1, source_target_pairs={{0,8},{8,0},{16,24},{24,16},{32,40},{40,32},{48,56},{56,48},{1,9},... | collective-permute-start | bytes 49160 | tf_op jit(solution)/shard_map/ppermute | solution.py:16
  147.7 1.7 collective-permute-done.7
  149.5 2.3 %collective-permute-start.8 = (f32[4096]{0:T(1024)S(1)}, f32[4096]{0:T(1024)S(1)}, u32[]{:S(2)}, u32[]{:S(2)}) collective-permute-start(f32[4096]{0:T(1024)S(1)} %add.123), channel_id=1, source_target_pairs={{0,16},{16,0},{8,24},{24,8},{32,48},{48,32},{40,56},{56,40},{1,17}... | collective-permute-start | bytes 49160 | tf_op jit(solution)/shard_map/ppermute | solution.py:16
  151.8 2.3 %collective-permute-done.8 = f32[4096]{0:T(1024)S(1)} collective-permute-done((f32[4096]{0:T(1024)S(1)}, f32[4096]{0:T(1024)S(1)}, u32[]{:S(2)}, u32[]{:S(2)}) %collective-permute-start.8) | collective-permute-done | bytes 16416 | tf_op jit(solution)/shard_map/ppermute | solution.py:16
  154.1 4.3 %collective-permute-start.9 = (f32[4096]{0:T(1024)S(1)}, f32[4096]{0:T(1024)S(1)}, u32[]{:S(2)}, u32[]{:S(2)}) collective-permute-start(f32[4096]{0:T(1024)S(1)} %add.124), channel_id=1, source_target_pairs={{0,32},{32,0},{8,40},{40,8},{16,48},{48,16},{24,56},{56,24},{1,33}... | collective-permute-start | bytes 49160 | tf_op jit(solution)/shard_map/ppermute | solution.py:16
  158.4 3.4 %collective-permute-done.9 = f32[4096]{0:T(1024)S(1)} collective-permute-done((f32[4096]{0:T(1024)S(1)}, f32[4096]{0:T(1024)S(1)}, u32[]{:S(2)}, u32[]{:S(2)}) %collective-permute-start.9) | collective-permute-done | bytes 16416 | tf_op jit(solution)/shard_map/ppermute | solution.py:16
  161.8 2.6 %collective-permute-start.4 = (f32[8,4096]{1,0:T(8,128)S(1)}, f32[8,4096]{1,0:T(8,128)S(1)}, u32[]{:S(2)}, u32[]{:S(2)}) collective-permute-start(f32[8,4096]{1,0:T(8,128)S(1)} %add_select_fusion), channel_id=1, source_target_pairs={{0,2},{2,0},{1,3},{3,1},{4,6},{6,4},{5,7},{7,5},{8,10},{10,8},{9,1... | collective-permute-start | bytes 393224 | tf_op jit(solution)/shard_map/ppermute | solution.py:16
  164.4 12.6 %multiply_reduce_fusion = (f32[768]{0:T(1024)S(1)}, bf16[4096,768]{1,0:T(8,128)(2,1)}) fusion(f32[768]{0:T(1024)S(1)} %copy-done.3, bf16[4096,768]{1,0:T(8,128)(2,1)} %param.7, bf16[512,4096]{1,0:T(8,128)(2,1)} %all-gather.2.cloned.1.call-done, bf16[512,768]{1,0:T(8,128)(2,1)S(1)} %all_gather.7), kind=kOutput, calls=%fused_computation | convolution fusion | flops 3252681984 | bytes 17569792 | tf_op jit(solution)/shard_map/dot_general | solution.py:91
  177.1 3.5 %collective-permute-done.11 = f32[768]{0:T(1024)S(1)} collective-permute-done((f32[768]{0:T(1024)S(1)}, f32[768]{0:T(1024)S(1)}, u32[]{:S(2)}, u32[]{:S(2)}) %collective-permute-start.11) | collective-permute-done | bytes 3104 | tf_op jit(solution)/shard_map/ppermute | solution.py:16
  180.6 0.9 collective-permute-start.12
  181.5 4.2 %collective-permute-done.12 = f32[768]{0:T(1024)S(1)} collective-permute-done((f32[768]{0:T(1024)S(1)}, f32[768]{0:T(1024)S(1)}, u32[]{:S(2)}, u32[]{:S(2)}) %collective-permute-start.12) | collective-permute-done | bytes 3104 | tf_op jit(solution)/shard_map/ppermute | solution.py:16
  186.3 0.6 add.126
  186.9 0.6 select_convert_fusion
  187.6 1.7 convert_element_type.54
  (39 shorter events, 3.4 us)
Async XLA Ops:
  7.2 117.8 %all-gather.2.cloned.1.call-start = ((), (), s32[]{:S(2)}) async-start(), calls=%async_computation.2 | async-start | bytes 4259840 | tf_op jit(solution)/shard_map/all_gather | solution.py:72
  9.1 12.0 %copy-start.1 = (bf16[128,768]{1,0:T(8,128)(2,1)S(1)}, bf16[128,768]{1,0:T(8,128)(2,1)}, u32[]{:S(2)}) copy-start(bf16[128,768]{1,0:T(8,128)(2,1)} %param.9) | copy-start | bytes 589828
  9.1 25.7 %copy-start.2 = (f32[4096]{0:T(1024)S(1)}, f32[4096]{0:T(1024)}, u32[]{:S(2)}) copy-start(f32[4096]{0:T(1024)} %param.6) | copy-start | bytes 49156
  9.1 9.0 %collective-permute-start = (f32[8,4096]{1,0:T(8,128)S(1)}, f32[8,4096]{1,0:T(8,128)S(1)}, u32[]{:S(2)}, u32[]{:S(2)}) collective-permute-start(f32[8,4096]{1,0:T(8,128)S(1)} %mul.67), channel_id=1, source_target_pairs={{0,1},{1,0},{2,3},{3,2},{4,5},{5,4},{6,7},{7,6},{8,9},{9,8},{10,11... | collective-permute-start | bytes 393224 | tf_op jit(solution)/shard_map/ppermute | solution.py:16
  18.1 16.6 %collective-permute-start.1 = (f32[8,4096]{1,0:T(8,128)S(1)}, f32[8,4096]{1,0:T(8,128)S(1)}, u32[]{:S(2)}, u32[]{:S(2)}) collective-permute-start(f32[8,4096]{1,0:T(8,128)S(1)} %add_select_fusion.1), channel_id=1, source_target_pairs={{0,2},{2,0},{1,3},{3,1},{4,6},{6,4},{5,7},{7,5},{8,10},{10,8},{9,1... | collective-permute-start | bytes 393224 | tf_op jit(solution)/shard_map/ppermute | solution.py:16
  35.5 152.1 %reduce-scatter.2.cloned.1.call-start = ((), (), s32[]{:S(2)}) async-start(), calls=%async_computation.3 | async-start | bytes 1966080 | tf_op jit(solution)/shard_map/reduce_scatter | solution.py:85
  41.1 3.2 %copy-start = (f32[4096,512]{0,1:T(8,128)}, f32[4096,512]{0,1:T(8,128)S(1)}, u32[]{:S(2)}) copy-start(f32[4096,512]{0,1:T(8,128)S(1)} %fusion.35) | copy-start | bytes 25165828
  44.6 4.4 %collective-permute-start.2 = (bf16[32,8,4096]{2,1,0:T(8,128)(2,1)S(1)}, bf16[32,8,4096]{2,1,0:T(8,128)(2,1)}, u32[]{:S(2)}, u32[]{:S(2)}) collective-permute-start(bf16[32,8,4096]{2,1,0:T(8,128)(2,1)S(1)} %fusion.1), channel_id=1, source_target_pairs={{0,4},{4,0},{1,5},{5,1},{2,6},{6,2},{3,7},{7,3},{8,12},{12,8},{9,1... | collective-permute-start | bytes 6291464 | tf_op jit(solution)/shard_map/ppermute | solution.py:80
  126.4 38.0 %copy-start.3 = (f32[768]{0:T(1024)S(1)}, f32[768]{0:T(1024)}, u32[]{:S(2)}) copy-start(f32[768]{0:T(1024)} %param.8) | copy-start | bytes 9220
  126.4 35.4 %collective-permute-start.3 = (f32[8,4096]{1,0:T(8,128)S(1)}, f32[8,4096]{1,0:T(8,128)S(1)}, u32[]{:S(2)}, u32[]{:S(2)}) collective-permute-start(f32[8,4096]{1,0:T(8,128)S(1)} %mul.74), channel_id=1, source_target_pairs={{0,1},{1,0},{2,3},{3,2},{4,5},{5,4},{6,7},{7,6},{8,9},{9,8},{10,11... | collective-permute-start | bytes 393224 | tf_op jit(solution)/shard_map/ppermute | solution.py:16
  135.9 3.8 %collective-permute-start.5 = (f32[4096]{0:T(1024)S(1)}, f32[4096]{0:T(1024)S(1)}, u32[]{:S(2)}, u32[]{:S(2)}) collective-permute-start(f32[4096]{0:T(1024)S(1)} %get-tuple-element.14), channel_id=1, source_target_pairs={{0,64},{64,0},{128,192},{192,128},{1,65},{65,1},{129,193},{193,129... | collective-permute-start | bytes 49160 | tf_op jit(solution)/shard_map/ppermute | solution.py:16
  139.7 5.2 %collective-permute-start.6 = (f32[4096]{0:T(1024)S(1)}, f32[4096]{0:T(1024)S(1)}, u32[]{:S(2)}, u32[]{:S(2)}) collective-permute-start(f32[4096]{0:T(1024)S(1)} %add.121), channel_id=1, source_target_pairs={{0,128},{128,0},{64,192},{192,64},{1,129},{129,1},{65,193},{193,65... | collective-permute-start | bytes 49160 | tf_op jit(solution)/shard_map/ppermute | solution.py:16
  145.0 4.5 %collective-permute-start.7 = (f32[4096]{0:T(1024)S(1)}, f32[4096]{0:T(1024)S(1)}, u32[]{:S(2)}, u32[]{:S(2)}) collective-permute-start(f32[4096]{0:T(1024)S(1)} %add.122), channel_id=1, source_target_pairs={{0,8},{8,0},{16,24},{24,16},{32,40},{40,32},{48,56},{56,48},{1,9},... | collective-permute-start | bytes 49160 | tf_op jit(solution)/shard_map/ppermute | solution.py:16
  149.5 4.6 %collective-permute-start.8 = (f32[4096]{0:T(1024)S(1)}, f32[4096]{0:T(1024)S(1)}, u32[]{:S(2)}, u32[]{:S(2)}) collective-permute-start(f32[4096]{0:T(1024)S(1)} %add.123), channel_id=1, source_target_pairs={{0,16},{16,0},{8,24},{24,8},{32,48},{48,32},{40,56},{56,40},{1,17}... | collective-permute-start | bytes 49160 | tf_op jit(solution)/shard_map/ppermute | solution.py:16
  154.1 7.7 %collective-permute-start.9 = (f32[4096]{0:T(1024)S(1)}, f32[4096]{0:T(1024)S(1)}, u32[]{:S(2)}, u32[]{:S(2)}) collective-permute-start(f32[4096]{0:T(1024)S(1)} %add.124), channel_id=1, source_target_pairs={{0,32},{32,0},{8,40},{40,8},{16,48},{48,16},{24,56},{56,24},{1,33}... | collective-permute-start | bytes 49160 | tf_op jit(solution)/shard_map/ppermute | solution.py:16
  161.8 24.5 %collective-permute-start.10 = (f32[4096]{0:T(1024)S(1)}, f32[4096]{0:T(1024)S(1)}, u32[]{:S(2)}, u32[]{:S(2)}) collective-permute-start(f32[4096]{0:T(1024)S(1)} %add.125), channel_id=1, source_target_pairs={{0,4},{4,0},{1,5},{5,1},{2,6},{6,2},{3,7},{7,3},{8,12},{12,8},{9,1... | collective-permute-start | bytes 49160 | tf_op jit(solution)/shard_map/ppermute | solution.py:16
  161.8 25.1 %collective-permute-start.4 = (f32[8,4096]{1,0:T(8,128)S(1)}, f32[8,4096]{1,0:T(8,128)S(1)}, u32[]{:S(2)}, u32[]{:S(2)}) collective-permute-start(f32[8,4096]{1,0:T(8,128)S(1)} %add_select_fusion), channel_id=1, source_target_pairs={{0,2},{2,0},{1,3},{3,1},{4,6},{6,4},{5,7},{7,5},{8,10},{10,8},{9,1... | collective-permute-start | bytes 393224 | tf_op jit(solution)/shard_map/ppermute | solution.py:16
  177.0 3.6 %collective-permute-start.11 = (f32[768]{0:T(1024)S(1)}, f32[768]{0:T(1024)S(1)}, u32[]{:S(2)}, u32[]{:S(2)}) collective-permute-start(f32[768]{0:T(1024)S(1)} %get-tuple-element.17), channel_id=1, source_target_pairs={{0,1},{1,0},{2,3},{3,2},{4,5},{5,4},{6,7},{7,6},{8,9},{9,8},{10,11... | collective-permute-start | bytes 9224 | tf_op jit(solution)/shard_map/ppermute | solution.py:16
  180.6 5.1 %collective-permute-start.12 = (f32[768]{0:T(1024)S(1)}, f32[768]{0:T(1024)S(1)}, u32[]{:S(2)}, u32[]{:S(2)}) collective-permute-start(f32[768]{0:T(1024)S(1)} %add.127), channel_id=1, source_target_pairs={{0,2},{2,0},{1,3},{3,1},{4,6},{6,4},{5,7},{7,5},{8,10},{10,8},{9,1... | collective-permute-start | bytes 9224 | tf_op jit(solution)/shard_map/ppermute | solution.py:16
Sparse Core Ops, SparseCore 0:
  35.6 89.3 all-gather.1
  158.5 25.4 reduce-scatter.1

commit v8 on v7

--- a/solution.py
+++ b/solution.py
@@ -94,13 +94,13 @@
     slope_weight = 1.0 - tanh_weight * tanh_weight
     weight_grad = (weight_prod * slope_weight).astype(jnp.bfloat16)
     weight_terms = jnp.sum(weight_prod * (tanh_weight - ratio_weight * slope_weight), axis=0)
-    clip_weight_grad = butterfly_sum(weight_terms, "tensor")
     act_prod = jnp.sum(pieces.astype(jnp.float32), axis=0)
     act_terms = jnp.sum(act_prod * edge_act, axis=0)
-    act_terms, _ = lax.optimization_barrier((act_terms, proj_part))
+    act_terms, _, weight_terms = lax.optimization_barrier((act_terms, proj_part, weight_terms))
     for axis in DP:
         act_terms = butterfly_sum(act_terms, axis)
     clip_act_grad = act_terms
+    clip_weight_grad = butterfly_sum(weight_terms, "tensor")
     pre_rotation = act_prod * slope_act
     token_grad = rotate(pre_rotation).astype(jnp.bfloat16)
     return (projected, token_grad, weight_grad, clip_act_grad, clip_weight_grad)

time: 198 us -> 198 us (level)
  no operation moved by 1% of the time
where the time goes in v8:
time: 198 us; the launch traced here: 196 us
  blocking collectives  82.9 us (42%)
  matrix products  28.2 us (14%)
  waiting for transfers between devices  27.5 us (14%)
  starting transfers between devices  23.3 us (12%)
  other arithmetic  15.4 us (8%)
  between operations  14.2 us (7%)
  local copies, waits for them, and re-layouts  4.87 us (2%)
    all_to_all x1, blocking collectives, body(): lax.all_to_all(chip_sum.astype(jnp.bfloat16), CHIPS, 0, 0, tiled=True)  69.2 us
    ppermute x12, starting transfers between devices, swapped(): return lax.ppermute(block, axis, route)  23.1 us
    ppermute x12, waiting for transfers between devices, swapped(): return lax.ppermute(block, axis, route)  19.8 us
    all_gather x1, blocking collectives, body(): all_cot = lax.all_gather(cotangent, 'tensor', axis=0, tiled=True)  13.6 us
    dot_general x1, matrix products, body(): lax.dot_general(all_act, all_cot, (((0,), (0,)), ((), ())), preferred_ele...  12.4 us
    dot_general x1, matrix products, body(): proj_part = jnp.dot(block, quant_weight, preferred_element_type=jnp.float32)  8.63 us
    convert_element_type x1, other arithmetic, body(): quant_weight = (clip_weight * tanh_weight).astype(jnp.bfloat16)  7.31 us
    dot_general x1, matrix products, body(): lax.dot_general(all_cot, quant_weight, (((1,), (1,)), ((), ())), preferre...  5.57 us
  transfers between devices with their start and end apart: 15, of which 9 were waited for; matrix products, arithmetic and copies ran while one was open for 20% of the time, Pallas kernels for 0%

profile of v8, /device:TPU:2, one launch (start us, length us, event | category | flops | bytes accessed | tf_op | source)
XLA Modules:
  0.0 196.3 jit_solution(3998113025731446155)
XLA Ops:
  7.2 1.0 reshape.28
  9.1 1.7 collective-permute-start
  10.8 7.3 %multiply_convert_fusion.1 = bf16[4096,768]{1,0:T(8,128)(2,1)} fusion(f32[768]{0:T(1024)} %param.8, bf16[4096,768]{1,0:T(8,128)(2,1)} %param.7), kind=kLoop, calls=%fused_computation.3 | loop fusion | flops 12582912 | bytes 12585984 | tf_op jit(solution)/shard_map/convert_element_type | solution.py:70
  18.1 3.0 %collective-permute-start.1 = (f32[8,4096]{1,0:T(8,128)S(1)}, f32[8,4096]{1,0:T(8,128)S(1)}, u32[]{:S(2)}, u32[]{:S(2)}) collective-permute-start(f32[8,4096]{1,0:T(8,128)S(1)} %add_select_fusion.1), channel_id=1, source_target_pairs={{0,2},{2,0},{1,3},{3,1},{4,6},{6,4},{5,7},{7,5},{8,10},{10,8},{9,1... | collective-permute-start | bytes 393224 | tf_op jit(solution)/shard_map/ppermute | solution.py:16
  21.1 13.6 %all_gather.7 = bf16[512,768]{1,0:T(8,128)(2,1)S(1)} all-gather(bf16[128,768]{1,0:T(8,128)(2,1)S(1)} %copy-done.1), channel_id=1, replica_groups=mesh['dx'=4,'dz'=8,'dc'=2,'tensor'=4] {'tensor'}, dimensions={0}, use_global_device_ids=true | all-gather | bytes 983040 | tf_op jit(solution)/shard_map/all_gather | solution.py:73
  34.7 0.7 multiply_convert_fusion.2
  35.5 5.6 %fusion.35 = f32[4096,512]{0,1:T(8,128)S(1)} fusion(bf16[4096,768]{1,0:T(8,128)(2,1)} %multiply_convert_fusion.1, bf16[512,768]{1,0:T(8,128)(2,1)S(1)} %all_gather.7), kind=kOutput, calls=%fused_computation.55 | convolution fusion | flops 3221225472 | bytes 15466496 | tf_op jit(solution)/shard_map/dot_general | solution.py:74
  41.1 3.2 %copy-done = f32[4096,512]{0,1:T(8,128)} copy-done((f32[4096,512]{0,1:T(8,128)}, f32[4096,512]{0,1:T(8,128)S(1)}, u32[]{:S(2)}) %copy-start) | copy-done | bytes 8388632
  44.7 4.3 %collective-permute-done.2 = bf16[32,8,4096]{2,1,0:T(8,128)(2,1)} collective-permute-done((bf16[32,8,4096]{2,1,0:T(8,128)(2,1)S(1)}, bf16[32,8,4096]{2,1,0:T(8,128)(2,1)}, u32[]{:S(2)}, u32[]{:S(2)}) %collective-permute-start.2) | collective-permute-done | bytes 2097184 | tf_op jit(solution)/shard_map/ppermute | solution.py:80
  49.0 3.4 %fusion = bf16[32,8,4096]{2,1,0:T(8,128)(2,1)S(1)} fusion(bf16[32,8,4096]{2,1,0:T(8,128)(2,1)} %collective-permute-done.2, f32[32,2,8,4096]{3,2,1,0:T(8,128)} %bitcast.33, s32[]{:T(128)S(6)} %select_n.33), kind=kLoop, calls=%fused_computation.6 | loop fusion | flops 3145728 | bytes 8388612 | tf_op jit(solution)/shard_map/convert_element_type | solution.py:81
  52.4 69.2 %all_to_all.5 = bf16[32,8,4096]{2,1,0:T(8,128)(2,1)S(1)} all-to-all(bf16[32,8,4096]{2,1,0:T(8,128)(2,1)S(1)} %fusion), channel_id=1, replica_groups=mesh['dx'=4,'dz'=8,'dc'=2,'tensor'=4] {'dx','dz'}, dimensions={0} | all-to-all | bytes 4194304 | tf_op jit(solution)/shard_map/all_to_all | solution.py:81
  121.6 3.4 %all-gather.2.cloned.1.call-done = bf16[512,4096]{1,0:T(8,128)(2,1)} async-done(((bf16[8,4096]{1,0:T(8,128)(2,1)}), bf16[512,4096]{1,0:T(8,128)(2,1)}) %all-gather.2.cloned.1.call-update) | async-done | bytes 4194320 | tf_op jit(solution)/shard_map/all_gather | solution.py:72
  126.4 0.9 collective-permute-start.3
  127.3 8.6 %fusion.36 = f32[512,768]{1,0:T(8,128)} fusion(bf16[512,4096]{1,0:T(8,128)(2,1)} %all-gather.2.cloned.1.call-done, bf16[4096,768]{1,0:T(8,128)(2,1)} %multiply_convert_fusion.1), kind=kOutput, calls=%fused_computation.56 | convolution fusion | flops 3221225472 | bytes 12058624 | tf_op jit(solution)/shard_map/dot_general | solution.py:84
  136.0 2.9 %collective-permute-start.4 = (f32[8,4096]{1,0:T(8,128)S(1)}, f32[8,4096]{1,0:T(8,128)S(1)}, u32[]{:S(2)}, u32[]{:S(2)}) collective-permute-start(f32[8,4096]{1,0:T(8,128)S(1)} %add_select_fusion), channel_id=1, source_target_pairs={{0,2},{2,0},{1,3},{3,1},{4,6},{6,4},{5,7},{7,5},{8,10},{10,8},{9,1... | collective-permute-start | bytes 393224 | tf_op jit(solution)/shard_map/ppermute | solution.py:16
  138.9 12.4 %multiply_reduce_fusion = (f32[768]{0:T(1024)S(1)}, bf16[4096,768]{1,0:T(8,128)(2,1)}) fusion(f32[768]{0:T(1024)S(1)} %copy-done.3, bf16[4096,768]{1,0:T(8,128)(2,1)} %param.7, bf16[512,4096]{1,0:T(8,128)(2,1)} %all-gather.2.cloned.1.call-done, bf16[512,768]{1,0:T(8,128)(2,1)S(1)} %all_gather.7), kind=kOutput, calls=%fused_computation | convolution fusion | flops 3252681984 | bytes 17569792 | tf_op jit(solution)/shard_map/dot_general | solution.py:91
  151.4 2.0 %collective-permute-start.5 = (f32[4096]{0:T(1024)S(1)}, f32[4096]{0:T(1024)S(1)}, u32[]{:S(2)}, u32[]{:S(2)}) collective-permute-start(f32[4096]{0:T(1024)S(1)} %get-tuple-element.15), channel_id=1, source_target_pairs={{0,64},{64,0},{128,192},{192,128},{1,65},{65,1},{129,193},{193,129... | collective-permute-start | bytes 49160 | tf_op jit(solution)/shard_map/ppermute | solution.py:16
  153.4 1.7 collective-permute-done.5
  155.1 2.0 %collective-permute-start.6 = (f32[4096]{0:T(1024)S(1)}, f32[4096]{0:T(1024)S(1)}, u32[]{:S(2)}, u32[]{:S(2)}) collective-permute-start(f32[4096]{0:T(1024)S(1)} %add.121), channel_id=1, source_target_pairs={{0,128},{128,0},{64,192},{192,64},{1,129},{129,1},{65,193},{193,65... | collective-permute-start | bytes 49160 | tf_op jit(solution)/shard_map/ppermute | solution.py:16
  157.1 3.2 %collective-permute-done.6 = f32[4096]{0:T(1024)S(1)} collective-permute-done((f32[4096]{0:T(1024)S(1)}, f32[4096]{0:T(1024)S(1)}, u32[]{:S(2)}, u32[]{:S(2)}) %collective-permute-start.6) | collective-permute-done | bytes 16416 | tf_op jit(solution)/shard_map/ppermute | solution.py:16
  160.3 2.7 %collective-permute-start.7 = (f32[4096]{0:T(1024)S(1)}, f32[4096]{0:T(1024)S(1)}, u32[]{:S(2)}, u32[]{:S(2)}) collective-permute-start(f32[4096]{0:T(1024)S(1)} %add.122), channel_id=1, source_target_pairs={{0,8},{8,0},{16,24},{24,16},{32,40},{40,32},{48,56},{56,48},{1,9},... | collective-permute-start | bytes 49160 | tf_op jit(solution)/shard_map/ppermute | solution.py:16
  163.0 1.7 collective-permute-done.7
  164.7 2.4 %collective-permute-start.8 = (f32[4096]{0:T(1024)S(1)}, f32[4096]{0:T(1024)S(1)}, u32[]{:S(2)}, u32[]{:S(2)}) collective-permute-start(f32[4096]{0:T(1024)S(1)} %add.123), channel_id=1, source_target_pairs={{0,16},{16,0},{8,24},{24,8},{32,48},{48,32},{40,56},{56,40},{1,17}... | collective-permute-start | bytes 49160 | tf_op jit(solution)/shard_map/ppermute | solution.py:16
  167.1 2.3 %collective-permute-done.8 = f32[4096]{0:T(1024)S(1)} collective-permute-done((f32[4096]{0:T(1024)S(1)}, f32[4096]{0:T(1024)S(1)}, u32[]{:S(2)}, u32[]{:S(2)}) %collective-permute-start.8) | collective-permute-done | bytes 16416 | tf_op jit(solution)/shard_map/ppermute | solution.py:16
  169.4 4.2 %collective-permute-start.9 = (f32[4096]{0:T(1024)S(1)}, f32[4096]{0:T(1024)S(1)}, u32[]{:S(2)}, u32[]{:S(2)}) collective-permute-start(f32[4096]{0:T(1024)S(1)} %add.124), channel_id=1, source_target_pairs={{0,32},{32,0},{8,40},{40,8},{16,48},{48,16},{24,56},{56,24},{1,33}... | collective-permute-start | bytes 49160 | tf_op jit(solution)/shard_map/ppermute | solution.py:16
  173.6 3.5 %collective-permute-done.9 = f32[4096]{0:T(1024)S(1)} collective-permute-done((f32[4096]{0:T(1024)S(1)}, f32[4096]{0:T(1024)S(1)}, u32[]{:S(2)}, u32[]{:S(2)}) %collective-permute-start.9) | collective-permute-done | bytes 16416 | tf_op jit(solution)/shard_map/ppermute | solution.py:16
  177.4 3.3 %collective-permute-done.11 = f32[768]{0:T(1024)S(1)} collective-permute-done((f32[768]{0:T(1024)S(1)}, f32[768]{0:T(1024)S(1)}, u32[]{:S(2)}, u32[]{:S(2)}) %collective-permute-start.11) | collective-permute-done | bytes 3104 | tf_op jit(solution)/shard_map/ppermute | solution.py:16
  180.7 1.0 collective-permute-start.12
  181.8 4.1 %collective-permute-done.12 = f32[768]{0:T(1024)S(1)} collective-permute-done((f32[768]{0:T(1024)S(1)}, f32[768]{0:T(1024)S(1)}, u32[]{:S(2)}, u32[]{:S(2)}) %collective-permute-start.12) | collective-permute-done | bytes 3104 | tf_op jit(solution)/shard_map/ppermute | solution.py:16
  186.5 0.6 add.126
  187.1 0.6 select_convert_fusion
  187.7 1.7 convert_element_type.54
  (39 shorter events, 3.8 us)
Async XLA Ops:
  7.2 117.8 %all-gather.2.cloned.1.call-start = ((), (), s32[]{:S(2)}) async-start(), calls=%async_computation.2 | async-start | bytes 4259840 | tf_op jit(solution)/shard_map/all_gather | solution.py:72
  9.1 12.0 %copy-start.1 = (bf16[128,768]{1,0:T(8,128)(2,1)S(1)}, bf16[128,768]{1,0:T(8,128)(2,1)}, u32[]{:S(2)}) copy-start(bf16[128,768]{1,0:T(8,128)(2,1)} %param.9) | copy-start | bytes 589828
  9.1 25.7 %copy-start.2 = (f32[4096]{0:T(1024)S(1)}, f32[4096]{0:T(1024)}, u32[]{:S(2)}) copy-start(f32[4096]{0:T(1024)} %param.6) | copy-start | bytes 49156
  9.1 9.0 %collective-permute-start = (f32[8,4096]{1,0:T(8,128)S(1)}, f32[8,4096]{1,0:T(8,128)S(1)}, u32[]{:S(2)}, u32[]{:S(2)}) collective-permute-start(f32[8,4096]{1,0:T(8,128)S(1)} %mul.67), channel_id=1, source_target_pairs={{0,1},{1,0},{2,3},{3,2},{4,5},{5,4},{6,7},{7,6},{8,9},{9,8},{10,11... | collective-permute-start | bytes 393224 | tf_op jit(solution)/shard_map/ppermute | solution.py:16
  18.1 16.6 %collective-permute-start.1 = (f32[8,4096]{1,0:T(8,128)S(1)}, f32[8,4096]{1,0:T(8,128)S(1)}, u32[]{:S(2)}, u32[]{:S(2)}) collective-permute-start(f32[8,4096]{1,0:T(8,128)S(1)} %add_select_fusion.1), channel_id=1, source_target_pairs={{0,2},{2,0},{1,3},{3,1},{4,6},{6,4},{5,7},{7,5},{8,10},{10,8},{9,1... | collective-permute-start | bytes 393224 | tf_op jit(solution)/shard_map/ppermute | solution.py:16
  35.5 152.3 %reduce-scatter.2.cloned.1.call-start = ((), (), s32[]{:S(2)}) async-start(), calls=%async_computation.3 | async-start | bytes 1966080 | tf_op jit(solution)/shard_map/reduce_scatter | solution.py:85
  41.1 3.2 %copy-start = (f32[4096,512]{0,1:T(8,128)}, f32[4096,512]{0,1:T(8,128)S(1)}, u32[]{:S(2)}) copy-start(f32[4096,512]{0,1:T(8,128)S(1)} %fusion.35) | copy-start | bytes 25165828
  44.6 4.4 %collective-permute-start.2 = (bf16[32,8,4096]{2,1,0:T(8,128)(2,1)S(1)}, bf16[32,8,4096]{2,1,0:T(8,128)(2,1)}, u32[]{:S(2)}, u32[]{:S(2)}) collective-permute-start(bf16[32,8,4096]{2,1,0:T(8,128)(2,1)S(1)} %fusion.1), channel_id=1, source_target_pairs={{0,4},{4,0},{1,5},{5,1},{2,6},{6,2},{3,7},{7,3},{8,12},{12,8},{9,1... | collective-permute-start | bytes 6291464 | tf_op jit(solution)/shard_map/ppermute | solution.py:80
  126.4 12.5 %copy-start.3 = (f32[768]{0:T(1024)S(1)}, f32[768]{0:T(1024)}, u32[]{:S(2)}) copy-start(f32[768]{0:T(1024)} %param.8) | copy-start | bytes 9220
  126.4 9.6 %collective-permute-start.3 = (f32[8,4096]{1,0:T(8,128)S(1)}, f32[8,4096]{1,0:T(8,128)S(1)}, u32[]{:S(2)}, u32[]{:S(2)}) collective-permute-start(f32[8,4096]{1,0:T(8,128)S(1)} %mul.74), channel_id=1, source_target_pairs={{0,1},{1,0},{2,3},{3,2},{4,5},{5,4},{6,7},{7,6},{8,9},{9,8},{10,11... | collective-permute-start | bytes 393224 | tf_op jit(solution)/shard_map/ppermute | solution.py:16
  136.0 51.1 %collective-permute-start.4 = (f32[8,4096]{1,0:T(8,128)S(1)}, f32[8,4096]{1,0:T(8,128)S(1)}, u32[]{:S(2)}, u32[]{:S(2)}) collective-permute-start(f32[8,4096]{1,0:T(8,128)S(1)} %add_select_fusion), channel_id=1, source_target_pairs={{0,2},{2,0},{1,3},{3,1},{4,6},{6,4},{5,7},{7,5},{8,10},{10,8},{9,1... | collective-permute-start | bytes 393224 | tf_op jit(solution)/shard_map/ppermute | solution.py:16
  151.4 3.7 %collective-permute-start.5 = (f32[4096]{0:T(1024)S(1)}, f32[4096]{0:T(1024)S(1)}, u32[]{:S(2)}, u32[]{:S(2)}) collective-permute-start(f32[4096]{0:T(1024)S(1)} %get-tuple-element.15), channel_id=1, source_target_pairs={{0,64},{64,0},{128,192},{192,128},{1,65},{65,1},{129,193},{193,129... | collective-permute-start | bytes 49160 | tf_op jit(solution)/shard_map/ppermute | solution.py:16
  155.1 5.2 %collective-permute-start.6 = (f32[4096]{0:T(1024)S(1)}, f32[4096]{0:T(1024)S(1)}, u32[]{:S(2)}, u32[]{:S(2)}) collective-permute-start(f32[4096]{0:T(1024)S(1)} %add.121), channel_id=1, source_target_pairs={{0,128},{128,0},{64,192},{192,64},{1,129},{129,1},{65,193},{193,65... | collective-permute-start | bytes 49160 | tf_op jit(solution)/shard_map/ppermute | solution.py:16
  160.3 4.4 %collective-permute-start.7 = (f32[4096]{0:T(1024)S(1)}, f32[4096]{0:T(1024)S(1)}, u32[]{:S(2)}, u32[]{:S(2)}) collective-permute-start(f32[4096]{0:T(1024)S(1)} %add.122), channel_id=1, source_target_pairs={{0,8},{8,0},{16,24},{24,16},{32,40},{40,32},{48,56},{56,48},{1,9},... | collective-permute-start | bytes 49160 | tf_op jit(solution)/shard_map/ppermute | solution.py:16
  164.7 4.6 %collective-permute-start.8 = (f32[4096]{0:T(1024)S(1)}, f32[4096]{0:T(1024)S(1)}, u32[]{:S(2)}, u32[]{:S(2)}) collective-permute-start(f32[4096]{0:T(1024)S(1)} %add.123), channel_id=1, source_target_pairs={{0,16},{16,0},{8,24},{24,8},{32,48},{48,32},{40,56},{56,40},{1,17}... | collective-permute-start | bytes 49160 | tf_op jit(solution)/shard_map/ppermute | solution.py:16
  169.4 7.7 %collective-permute-start.9 = (f32[4096]{0:T(1024)S(1)}, f32[4096]{0:T(1024)S(1)}, u32[]{:S(2)}, u32[]{:S(2)}) collective-permute-start(f32[4096]{0:T(1024)S(1)} %add.124), channel_id=1, source_target_pairs={{0,32},{32,0},{8,40},{40,8},{16,48},{48,16},{24,56},{56,24},{1,33}... | collective-permute-start | bytes 49160 | tf_op jit(solution)/shard_map/ppermute | solution.py:16
  177.0 9.4 %collective-permute-start.10 = (f32[4096]{0:T(1024)S(1)}, f32[4096]{0:T(1024)S(1)}, u32[]{:S(2)}, u32[]{:S(2)}) collective-permute-start(f32[4096]{0:T(1024)S(1)} %add.125), channel_id=1, source_target_pairs={{0,4},{4,0},{1,5},{5,1},{2,6},{6,2},{3,7},{7,3},{8,12},{12,8},{9,1... | collective-permute-start | bytes 49160 | tf_op jit(solution)/shard_map/ppermute | solution.py:16
  177.0 3.7 %collective-permute-start.11 = (f32[768]{0:T(1024)S(1)}, f32[768]{0:T(1024)S(1)}, u32[]{:S(2)}, u32[]{:S(2)}) collective-permute-start(f32[768]{0:T(1024)S(1)} %get-tuple-element.16), channel_id=1, source_target_pairs={{0,1},{1,0},{2,3},{3,2},{4,5},{5,4},{6,7},{7,6},{8,9},{9,8},{10,11... | collective-permute-start | bytes 9224 | tf_op jit(solution)/shard_map/ppermute | solution.py:16
  180.7 5.1 %collective-permute-start.12 = (f32[768]{0:T(1024)S(1)}, f32[768]{0:T(1024)S(1)}, u32[]{:S(2)}, u32[]{:S(2)}) collective-permute-start(f32[768]{0:T(1024)S(1)} %add.127), channel_id=1, source_target_pairs={{0,2},{2,0},{1,3},{3,1},{4,6},{6,4},{5,7},{7,5},{8,10},{10,8},{9,1... | collective-permute-start | bytes 9224 | tf_op jit(solution)/shard_map/ppermute | solution.py:16
Sparse Core Ops, SparseCore 0:
  35.6 89.3 all-gather.1
  136.1 28.2 reduce-scatter.1

commit v9 on v6

--- a/solution.py
+++ b/solution.py
@@ -95,9 +95,9 @@
     pieces = lax.all_to_all(chip_sum.astype(jnp.bfloat16), CHIPS, 0, 0, tiled=True)
     act_prod = jnp.sum(pieces.astype(jnp.float32), axis=0)
     act_terms = jnp.sum(act_prod * edge_act, axis=0)
-    for axis in DP:
-        act_terms = butterfly_sum(act_terms, axis)
-    clip_act_grad = act_terms
+    act_terms = lax.psum(act_terms, "dc")
+    spread = jnp.broadcast_to(act_terms[None], (chips,) + act_terms.shape)
+    clip_act_grad = jnp.sum(lax.all_to_all(spread, CHIPS, 0, 0, tiled=True), axis=0)
     pre_rotation = act_prod * slope_act
     token_grad = rotate(pre_rotation).astype(jnp.bfloat16)
     return (projected, token_grad, weight_grad, clip_act_grad, clip_weight_grad)

time: 194 us -> 183 us (0.943)
  waiting for transfers between devices: 28.7 us -> 16.2 us
  blocking collectives: 80.1 us -> 83.5 us
  starting transfers between devices: 20.1 us -> 17.3 us
    ppermute x12 -> x6, waiting for transfers between devices: 21.7 us -> 6.05 us  [swapped(): return lax.ppermute(block, axis, route)]
    ppermute x12 -> x6, starting transfers between devices: 20 us -> 8.6 us  [swapped(): return lax.ppermute(block, axis, route)]
    all_to_all x0 -> x1, starting transfers between devices: none -> 8.52 us  [body(): lax.all_to_all(spread, CHIPS, 0, 0, tiled=True)]
    psum x0 -> x1, blocking collectives: none -> 3.35 us  [body(): act_terms = lax.psum(act_terms, 'dc')]
    reduce_scatter x1, waiting for transfers between devices: 2.76 us -> 5.81 us  [body(): lax.psum_scatter(jnp.dot(block, quant_weight, preferred_element_type=jnp....]
  transfers between devices with their start and end apart: 15 -> 10, of which waited for: 9 -> 4; matrix products, arithmetic and copies ran while one was open for 22% -> 25% of each run, Pallas kernels for 0% -> 0%
where the time goes in v9:
time: 183 us
  blocking collectives  83.5 us (46%)
  matrix products  31 us (17%)
  starting transfers between devices  17.3 us (9%)
  waiting for transfers between devices  16.2 us (9%)
  other arithmetic  15.7 us (9%)
  between operations  14.2 us (8%)
  local copies, waits for them, and re-layouts  5.1 us (3%)
    all_to_all x1, blocking collectives, body(): lax.all_to_all(chip_sum.astype(jnp.bfloat16), CHIPS, 0, 0, tiled=True)  66.2 us
    all_gather x1, blocking collectives, body(): all_cot = lax.all_gather(cotangent, 'tensor', axis=0, tiled=True)  14 us
    dot_general x1, matrix products, body(): lax.dot_general(all_act, all_cot, (((0,), (0,)), ((), ())), preferred_ele...  12.5 us
    dot_general x1, matrix products, body(): jnp.dot(block, quant_weight, preferred_element_type=jnp.float32)  8.63 us
    ppermute x6, starting transfers between devices, swapped(): return lax.ppermute(block, axis, route)  8.6 us
    all_to_all x1, starting transfers between devices, body(): lax.all_to_all(spread, CHIPS, 0, 0, tiled=True)  8.52 us
    dot_general x1, matrix products, body(): lax.dot_general(all_cot, quant_weight, (((1,), (1,)), ((), ())), preferre...  8.42 us
    convert_element_type x1, other arithmetic, body(): quant_weight = (clip_weight * tanh_weight).astype(jnp.bfloat16)  7.31 us
  transfers between devices with their start and end apart: 10, of which 4 were waited for; matrix products, arithmetic and copies ran while one was open for 25% of the time, Pallas kernels for 0%

profile of v9, /device:TPU:2, one launch (start us, length us, event | category | flops | bytes accessed | tf_op | source)
XLA Modules:
  0.0 182.9 jit_solution(15071539731830729120)
XLA Ops:
  7.2 1.0 reshape.34
  8.2 0.3 convolution_bitcast_fusion.1
  8.6 0.4 convolution_multiply_fusion.1
  9.0 0.1 mul.67
  9.1 1.7 collective-permute-start
  10.8 7.3 %multiply_convert_fusion.1 = bf16[4096,768]{1,0:T(8,128)(2,1)} fusion(f32[768]{0:T(1024)} %param.8, bf16[4096,768]{1,0:T(8,128)(2,1)} %param.7), kind=kLoop, calls=%fused_computation.3 | loop fusion | flops 12582912 | bytes 12585984 | tf_op jit(solution)/shard_map/convert_element_type | solution.py:70
  18.1 14.0 %all_gather.6 = bf16[512,768]{1,0:T(8,128)(2,1)S(1)} all-gather(bf16[128,768]{1,0:T(8,128)(2,1)S(1)} %copy-done), channel_id=1, replica_groups=mesh['dx'=4,'dz'=8,'dc'=2,'tensor'=4] {'tensor'}, dimensions={0}, use_global_device_ids=true | all-gather | bytes 983040 | tf_op jit(solution)/shard_map/all_gather | solution.py:71
  32.1 1.5 collective-permute-start.1
  33.6 8.4 %fusion.35 = f32[4096,512]{0,1:T(8,128)} fusion(bf16[4096,768]{1,0:T(8,128)(2,1)} %multiply_convert_fusion.1, bf16[512,768]{1,0:T(8,128)(2,1)S(1)} %all_gather.6), kind=kOutput, calls=%fused_computation.55 | convolution fusion | flops 3221225472 | bytes 15466496 | tf_op jit(solution)/shard_map/dot_general | solution.py:72
  42.1 0.7 multiply_convert_fusion.2
  42.7 2.5 %fusion.1 = bf16[32,8,4096]{2,1,0:T(8,128)(2,1)S(1)} fusion(f32[32,2,8,4096]{3,2,1,0:T(8,128)} %bitcast.34, s32[]{:T(128)S(6)} %select_n.34), kind=kLoop, calls=%fused_computation.9 | loop fusion | bytes 4194308 | tf_op jit(solution)/shard_map/convert_element_type | solution.py:94
  45.3 4.3 %collective-permute-done.2 = bf16[32,8,4096]{2,1,0:T(8,128)(2,1)} collective-permute-done((bf16[32,8,4096]{2,1,0:T(8,128)(2,1)S(1)}, bf16[32,8,4096]{2,1,0:T(8,128)(2,1)}, u32[]{:S(2)}, u32[]{:S(2)}) %collective-permute-start.2) | collective-permute-done | bytes 2097184 | tf_op jit(solution)/shard_map/ppermute | solution.py:94
  49.6 3.4 %fusion = bf16[32,8,4096]{2,1,0:T(8,128)(2,1)S(1)} fusion(bf16[32,8,4096]{2,1,0:T(8,128)(2,1)} %collective-permute-done.2, f32[32,2,8,4096]{3,2,1,0:T(8,128)} %bitcast.35, s32[]{:T(128)S(6)} %select_n.33), kind=kLoop, calls=%fused_computation.6 | loop fusion | flops 3145728 | bytes 8388612 | tf_op jit(solution)/shard_map/convert_element_type | solution.py:95
  53.0 66.2 %all_to_all.11 = bf16[32,8,4096]{2,1,0:T(8,128)(2,1)S(1)} all-to-all(bf16[32,8,4096]{2,1,0:T(8,128)(2,1)S(1)} %fusion), channel_id=1, replica_groups=mesh['dx'=4,'dz'=8,'dc'=2,'tensor'=4] {'dx','dz'}, dimensions={0} | all-to-all | bytes 4194304 | tf_op jit(solution)/shard_map/all_to_all | solution.py:95
  119.1 0.3 convert_reduce_fusion
  119.6 0.4 convolution_bitcast_fusion
  120.0 0.4 convolution_multiply_fusion
  120.5 1.6 collective-permute-start.3
  122.1 3.3 %psum.7 = f32[4096]{0:T(1024)S(1)} all-reduce(f32[4096]{0:T(1024)S(1)} %get-tuple-element.13), channel_id=1, replica_groups=mesh['dx'=4,'dz'=8,'dc'=2,'tensor'=4] {'dc'}, use_global_device_ids=true, to_apply=%region_3.4 | all-reduce | flops 4096 | bytes 32768 | tf_op jit(solution)/shard_map/psum | solution.py:98
  125.5 1.3 broadcast_in_dim.2
  126.7 8.5 %all-to-all-start.1 = ((f32[32,1,4096]{2,1,0:T(1,128)}), f32[32,1,4096]{2,1,0:T(1,128)S(1)}, u32[]{:S(2)}, u32[]{:S(2)}) async-start(f32[32,1,4096]{2,1,0:T(1,128)} %broadcast_in_dim.2), calls=%async_computation.2 | async-start | bytes 1048576 | tf_op jit(solution)/shard_map/all_to_all | solution.py:100
  135.4 2.3 %collective-permute-start.4 = (f32[8,4096]{1,0:T(8,128)S(1)}, f32[8,4096]{1,0:T(8,128)S(1)}, u32[]{:S(2)}, u32[]{:S(2)}) collective-permute-start(f32[8,4096]{1,0:T(8,128)S(1)} %add_select_fusion), channel_id=1, source_target_pairs={{0,2},{2,0},{1,3},{3,1},{4,6},{6,4},{5,7},{7,5},{8,10},{10,8},{9,1... | collective-permute-start | bytes 393224 | tf_op jit(solution)/shard_map/ppermute | solution.py:16
  137.7 8.6 %fusion.36 = f32[512,768]{1,0:T(8,128)} fusion(bf16[512,4096]{1,0:T(8,128)(2,1)} %all-gather.2.cloned.1.call-done, bf16[4096,768]{1,0:T(8,128)(2,1)} %multiply_convert_fusion.1), kind=kOutput, calls=%fused_computation.56 | convolution fusion | flops 3221225472 | bytes 12058624 | tf_op jit(solution)/shard_map/dot_general | solution.py:80
  146.4 12.5 %multiply_reduce_fusion = (f32[768]{0:T(1024)S(1)}, bf16[4096,768]{1,0:T(8,128)(2,1)}) fusion(f32[768]{0:T(1024)S(1)} %copy-done.2, bf16[4096,768]{1,0:T(8,128)(2,1)} %param.7, bf16[512,4096]{1,0:T(8,128)(2,1)} %all-gather.2.cloned.1.call-done, bf16[512,768]{1,0:T(8,128)(2,1)S(1)} %all_gather.6), kind=kOutput, calls=%fused_computation | convolution fusion | flops 3252681984 | bytes 17569792 | tf_op jit(solution)/shard_map/dot_general | solution.py:85
  158.8 3.8 %collective-permute-done.5 = f32[768]{0:T(1024)S(1)} collective-permute-done((f32[768]{0:T(1024)S(1)}, f32[768]{0:T(1024)S(1)}, u32[]{:S(2)}, u32[]{:S(2)}) %collective-permute-start.5) | collective-permute-done | bytes 3104 | tf_op jit(solution)/shard_map/ppermute | solution.py:16
  162.6 1.5 collective-permute-start.6
  164.1 0.6 select_convert_fusion
  164.8 1.0 reduce_sum.38
  165.7 2.2 %collective-permute-done.6 = f32[768]{0:T(1024)S(1)} collective-permute-done((f32[768]{0:T(1024)S(1)}, f32[768]{0:T(1024)S(1)}, u32[]{:S(2)}, u32[]{:S(2)}) %collective-permute-start.6) | collective-permute-done | bytes 3104 | tf_op jit(solution)/shard_map/ppermute | solution.py:16
  168.0 0.6 add.106
  168.6 5.8 %reduce-scatter.2.cloned.1.call-done = f32[128,768]{1,0:T(8,128)} async-done(((f32[512,768]{1,0:T(8,128)}), f32[128,768]{1,0:T(8,128)}) %reduce-scatter.2.cloned.1.call-update) | async-done | bytes 393232 | tf_op jit(solution)/shard_map/reduce_scatter | solution.py:79
  174.4 1.7 convert_element_type.50
  (24 shorter events, 0.6 us)
Async XLA Ops:
  7.2 130.5 %all-gather.2.cloned.1.call-start = ((), (), s32[]{:S(2)}) async-start(), calls=%async_computation.3 | async-start | bytes 4259840 | tf_op jit(solution)/shard_map/all_gather | solution.py:76
  9.1 9.0 %copy-start = (bf16[128,768]{1,0:T(8,128)(2,1)S(1)}, bf16[128,768]{1,0:T(8,128)(2,1)}, u32[]{:S(2)}) copy-start(bf16[128,768]{1,0:T(8,128)(2,1)} %param.9) | copy-start | bytes 589828
  9.1 23.0 %collective-permute-start = (f32[8,4096]{1,0:T(8,128)S(1)}, f32[8,4096]{1,0:T(8,128)S(1)}, u32[]{:S(2)}, u32[]{:S(2)}) collective-permute-start(f32[8,4096]{1,0:T(8,128)S(1)} %mul.67), channel_id=1, source_target_pairs={{0,1},{1,0},{2,3},{3,2},{4,5},{5,4},{6,7},{7,6},{8,9},{9,8},{10,11... | collective-permute-start | bytes 393224 | tf_op jit(solution)/shard_map/ppermute | solution.py:16
  32.1 10.0 %copy-start.1 = (f32[4096]{0:T(1024)S(1)}, f32[4096]{0:T(1024)}, u32[]{:S(2)}) copy-start(f32[4096]{0:T(1024)} %param.6) | copy-start | bytes 49156
  32.1 10.0 %collective-permute-start.1 = (f32[8,4096]{1,0:T(8,128)S(1)}, f32[8,4096]{1,0:T(8,128)S(1)}, u32[]{:S(2)}, u32[]{:S(2)}) collective-permute-start(f32[8,4096]{1,0:T(8,128)S(1)} %add_select_fusion.1), channel_id=1, source_target_pairs={{0,2},{2,0},{1,3},{3,1},{4,6},{6,4},{5,7},{7,5},{8,10},{10,8},{9,1... | collective-permute-start | bytes 393224 | tf_op jit(solution)/shard_map/ppermute | solution.py:16
  45.2 4.4 %collective-permute-start.2 = (bf16[32,8,4096]{2,1,0:T(8,128)(2,1)S(1)}, bf16[32,8,4096]{2,1,0:T(8,128)(2,1)}, u32[]{:S(2)}, u32[]{:S(2)}) collective-permute-start(bf16[32,8,4096]{2,1,0:T(8,128)(2,1)S(1)} %fusion.1), channel_id=1, source_target_pairs={{0,4},{4,0},{1,5},{5,1},{2,6},{6,2},{3,7},{7,3},{8,12},{12,8},{9,1... | collective-permute-start | bytes 6291464 | tf_op jit(solution)/shard_map/ppermute | solution.py:94
  120.5 14.8 %collective-permute-start.3 = (f32[8,4096]{1,0:T(8,128)S(1)}, f32[8,4096]{1,0:T(8,128)S(1)}, u32[]{:S(2)}, u32[]{:S(2)}) collective-permute-start(f32[8,4096]{1,0:T(8,128)S(1)} %mul.74), channel_id=1, source_target_pairs={{0,1},{1,0},{2,3},{3,2},{4,5},{5,4},{6,7},{7,6},{8,9},{9,8},{10,11... | collective-permute-start | bytes 393224 | tf_op jit(solution)/shard_map/ppermute | solution.py:16
  126.7 38.0 %all-to-all-start.1 = ((f32[32,1,4096]{2,1,0:T(1,128)}), f32[32,1,4096]{2,1,0:T(1,128)S(1)}, u32[]{:S(2)}, u32[]{:S(2)}) async-start(f32[32,1,4096]{2,1,0:T(1,128)} %broadcast_in_dim.2), calls=%async_computation.2 | async-start | bytes 1048576 | tf_op jit(solution)/shard_map/all_to_all | solution.py:100
  135.3 39.1 %reduce-scatter.2.cloned.1.call-start = ((), (), s32[]{:S(2)}) async-start(), calls=%async_computation.4 | async-start | bytes 1966080 | tf_op jit(solution)/shard_map/reduce_scatter | solution.py:79
  135.3 11.0 %copy-start.2 = (f32[768]{0:T(1024)S(1)}, f32[768]{0:T(1024)}, u32[]{:S(2)}) copy-start(f32[768]{0:T(1024)} %param.8) | copy-start | bytes 9220
  135.4 28.7 %collective-permute-start.4 = (f32[8,4096]{1,0:T(8,128)S(1)}, f32[8,4096]{1,0:T(8,128)S(1)}, u32[]{:S(2)}, u32[]{:S(2)}) collective-permute-start(f32[8,4096]{1,0:T(8,128)S(1)} %add_select_fusion), channel_id=1, source_target_pairs={{0,2},{2,0},{1,3},{3,1},{4,6},{6,4},{5,7},{7,5},{8,10},{10,8},{9,1... | collective-permute-start | bytes 393224 | tf_op jit(solution)/shard_map/ppermute | solution.py:16
  158.8 3.8 %collective-permute-start.5 = (f32[768]{0:T(1024)S(1)}, f32[768]{0:T(1024)S(1)}, u32[]{:S(2)}, u32[]{:S(2)}) collective-permute-start(f32[768]{0:T(1024)S(1)} %get-tuple-element.11), channel_id=1, source_target_pairs={{0,1},{1,0},{2,3},{3,2},{4,5},{5,4},{6,7},{7,6},{8,9},{9,8},{10,11... | collective-permute-start | bytes 9224 | tf_op jit(solution)/shard_map/ppermute | solution.py:16
  162.6 5.3 %collective-permute-start.6 = (f32[768]{0:T(1024)S(1)}, f32[768]{0:T(1024)S(1)}, u32[]{:S(2)}, u32[]{:S(2)}) collective-permute-start(f32[768]{0:T(1024)S(1)} %add.105), channel_id=1, source_target_pairs={{0,2},{2,0},{1,3},{3,1},{4,6},{6,4},{5,7},{7,5},{8,10},{10,8},{9,1... | collective-permute-start | bytes 9224 | tf_op jit(solution)/shard_map/ppermute | solution.py:16
Sparse Core Ops, SparseCore 0:
  45.5 88.2 all-gather.1
  146.5 27.8 reduce-scatter.1

commit v10 on v9

--- a/solution.py
+++ b/solution.py
@@ -76,8 +76,9 @@
     all_act = lax.all_gather(quant_act, DP, axis=0, tiled=True)
     pair = [(0, 1), (1, 0)]
     block = all_act
+    proj_part = jnp.dot(block, quant_weight, preferred_element_type=jnp.float32)
     projected = lax.psum_scatter(
-        jnp.dot(block, quant_weight, preferred_element_type=jnp.float32),
+        proj_part,
         "tensor",
         scatter_dimension=0,
         tiled=True,
@@ -95,6 +96,7 @@
     pieces = lax.all_to_all(chip_sum.astype(jnp.bfloat16), CHIPS, 0, 0, tiled=True)
     act_prod = jnp.sum(pieces.astype(jnp.float32), axis=0)
     act_terms = jnp.sum(act_prod * edge_act, axis=0)
+    act_terms, _ = lax.optimization_barrier((act_terms, proj_part))
     act_terms = lax.psum(act_terms, "dc")
     spread = jnp.broadcast_to(act_terms[None], (chips,) + act_terms.shape)
     clip_act_grad = jnp.sum(lax.all_to_all(spread, CHIPS, 0, 0, tiled=True), axis=0)

time: 183 us -> 186 us (1.016)
    all_gather x1, waiting for transfers between devices: 0.01 us -> 6.04 us  [body(): all_act = lax.all_gather(quant_act, DP, axis=0, tiled=True)]
    reduce_scatter x1, waiting for transfers between devices: 5.81 us -> 0.01 us  [body(): lax.psum_scatter(proj_part, 'tensor', scatter_dimension=0, tiled=True)]
    ppermute x6, starting transfers between devices: 8.6 us -> 10.7 us  [swapped(): return lax.ppermute(block, axis, route)]
  transfers between devices with their start and end apart: 10 -> 10, of which waited for: 4 -> 5; matrix products, arithmetic and copies ran while one was open for 25% -> 24% of each run, Pallas kernels for 0% -> 0%
where the time goes in v10:
time: 186 us
  blocking collectives  83.5 us (45%)
  matrix products  31 us (17%)
  starting transfers between devices  18 us (10%)
  waiting for transfers between devices  18 us (10%)
  other arithmetic  15.7 us (8%)
  between operations  14.2 us (8%)
  local copies, waits for them, and re-layouts  5.1 us (3%)
    all_to_all x1, blocking collectives, body(): lax.all_to_all(chip_sum.astype(jnp.bfloat16), CHIPS, 0, 0, tiled=True)  66.2 us
    all_gather x1, blocking collectives, body(): all_cot = lax.all_gather(cotangent, 'tensor', axis=0, tiled=True)  14 us
    dot_general x1, matrix products, body(): lax.dot_general(all_act, all_cot, (((0,), (0,)), ((), ())), preferred_ele...  12.5 us
    ppermute x6, starting transfers between devices, swapped(): return lax.ppermute(block, axis, route)  10.7 us
    dot_general x1, matrix products, body(): proj_part = jnp.dot(block, quant_weight, preferred_element_type=jnp.float32)  8.63 us
    dot_general x1, matrix products, body(): lax.dot_general(all_cot, quant_weight, (((1,), (1,)), ((), ())), preferre...  8.42 us
    ppermute x6, waiting for transfers between devices, swapped(): return lax.ppermute(block, axis, route)  7.74 us
    convert_element_type x1, other arithmetic, body(): quant_weight = (clip_weight * tanh_weight).astype(jnp.bfloat16)  7.31 us
  transfers between devices with their start and end apart: 10, of which 5 were waited for; matrix products, arithmetic and copies ran while one was open for 24% of the time, Pallas kernels for 0%

profile of v10, /device:TPU:2, one launch (start us, length us, event | category | flops | bytes accessed | tf_op | source)
XLA Modules:
  0.0 185.6 jit_solution(15020473618873394486)
XLA Ops:
  7.2 1.0 reshape.34
  8.2 0.3 convolution_bitcast_fusion.1
  8.6 0.4 convolution_multiply_fusion.1
  9.1 1.7 collective-permute-start
  10.8 7.3 %multiply_convert_fusion.1 = bf16[4096,768]{1,0:T(8,128)(2,1)} fusion(f32[768]{0:T(1024)} %param.8, bf16[4096,768]{1,0:T(8,128)(2,1)} %param.7), kind=kLoop, calls=%fused_computation.3 | loop fusion | flops 12582912 | bytes 12585984 | tf_op jit(solution)/shard_map/convert_element_type | solution.py:70
  18.1 14.0 %all_gather.6 = bf16[512,768]{1,0:T(8,128)(2,1)S(1)} all-gather(bf16[128,768]{1,0:T(8,128)(2,1)S(1)} %copy-done), channel_id=1, replica_groups=mesh['dx'=4,'dz'=8,'dc'=2,'tensor'=4] {'tensor'}, dimensions={0}, use_global_device_ids=true | all-gather | bytes 983040 | tf_op jit(solution)/shard_map/all_gather | solution.py:71
  32.1 1.5 collective-permute-start.1
  33.6 8.4 %fusion.35 = f32[4096,512]{0,1:T(8,128)} fusion(bf16[4096,768]{1,0:T(8,128)(2,1)} %multiply_convert_fusion.1, bf16[512,768]{1,0:T(8,128)(2,1)S(1)} %all_gather.6), kind=kOutput, calls=%fused_computation.55 | convolution fusion | flops 3221225472 | bytes 15466496 | tf_op jit(solution)/shard_map/dot_general | solution.py:72
  42.1 0.7 multiply_convert_fusion.2
  42.7 2.5 %fusion.1 = bf16[32,8,4096]{2,1,0:T(8,128)(2,1)S(1)} fusion(f32[32,2,8,4096]{3,2,1,0:T(8,128)} %bitcast.34, s32[]{:T(128)S(6)} %select_n.34), kind=kLoop, calls=%fused_computation.9 | loop fusion | bytes 4194308 | tf_op jit(solution)/shard_map/convert_element_type | solution.py:95
  45.4 4.2 %collective-permute-done.2 = bf16[32,8,4096]{2,1,0:T(8,128)(2,1)} collective-permute-done((bf16[32,8,4096]{2,1,0:T(8,128)(2,1)S(1)}, bf16[32,8,4096]{2,1,0:T(8,128)(2,1)}, u32[]{:S(2)}, u32[]{:S(2)}) %collective-permute-start.2) | collective-permute-done | bytes 2097184 | tf_op jit(solution)/shard_map/ppermute | solution.py:95
  49.6 3.4 %fusion = bf16[32,8,4096]{2,1,0:T(8,128)(2,1)S(1)} fusion(bf16[32,8,4096]{2,1,0:T(8,128)(2,1)} %collective-permute-done.2, f32[32,2,8,4096]{3,2,1,0:T(8,128)} %bitcast.35, s32[]{:T(128)S(6)} %select_n.33), kind=kLoop, calls=%fused_computation.6 | loop fusion | flops 3145728 | bytes 8388612 | tf_op jit(solution)/shard_map/convert_element_type | solution.py:96
  53.0 66.2 %all_to_all.11 = bf16[32,8,4096]{2,1,0:T(8,128)(2,1)S(1)} all-to-all(bf16[32,8,4096]{2,1,0:T(8,128)(2,1)S(1)} %fusion), channel_id=1, replica_groups=mesh['dx'=4,'dz'=8,'dc'=2,'tensor'=4] {'dx','dz'}, dimensions={0} | all-to-all | bytes 4194304 | tf_op jit(solution)/shard_map/all_to_all | solution.py:96
  119.6 0.4 convolution_bitcast_fusion
  120.0 0.4 convolution_multiply_fusion
  120.5 1.6 collective-permute-start.3
  122.1 3.5 %collective-permute-done.3 = f32[8,4096]{1,0:T(8,128)S(1)} collective-permute-done((f32[8,4096]{1,0:T(8,128)S(1)}, f32[8,4096]{1,0:T(8,128)S(1)}, u32[]{:S(2)}, u32[]{:S(2)}) %collective-permute-start.3) | collective-permute-done | bytes 131104 | tf_op jit(solution)/shard_map/ppermute | solution.py:16
  125.6 2.1 %collective-permute-start.4 = (f32[8,4096]{1,0:T(8,128)S(1)}, f32[8,4096]{1,0:T(8,128)S(1)}, u32[]{:S(2)}, u32[]{:S(2)}) collective-permute-start(f32[8,4096]{1,0:T(8,128)S(1)} %add_select_fusion), channel_id=1, source_target_pairs={{0,2},{2,0},{1,3},{3,1},{4,6},{6,4},{5,7},{7,5},{8,10},{10,8},{9,1... | collective-permute-start | bytes 393224 | tf_op jit(solution)/shard_map/ppermute | solution.py:16
  127.7 6.0 %all-gather.2.cloned.1.call-done = bf16[512,4096]{1,0:T(8,128)(2,1)} async-done(((bf16[8,4096]{1,0:T(8,128)(2,1)}), bf16[512,4096]{1,0:T(8,128)(2,1)}) %all-gather.2.cloned.1.call-update) | async-done | bytes 4194320 | tf_op jit(solution)/shard_map/all_gather | solution.py:76
  133.8 8.6 %fusion.36 = f32[512,768]{1,0:T(8,128)} fusion(bf16[512,4096]{1,0:T(8,128)(2,1)} %all-gather.2.cloned.1.call-done, bf16[4096,768]{1,0:T(8,128)(2,1)} %multiply_convert_fusion.1), kind=kOutput, calls=%fused_computation.56 | convolution fusion | flops 3221225472 | bytes 12058624 | tf_op jit(solution)/shard_map/dot_general | solution.py:79
  142.4 3.4 %psum.7 = f32[4096]{0:T(1024)S(1)} all-reduce(f32[4096]{0:T(1024)S(1)} %get-tuple-element.10), channel_id=1, replica_groups=mesh['dx'=4,'dz'=8,'dc'=2,'tensor'=4] {'dc'}, use_global_device_ids=true, to_apply=%region_3.4 | all-reduce | flops 4096 | bytes 32768 | tf_op jit(solution)/shard_map/psum | solution.py:100
  145.9 1.3 broadcast_in_dim.2
  147.1 7.2 %all-to-all-start.1 = ((f32[32,1,4096]{2,1,0:T(1,128)}), f32[32,1,4096]{2,1,0:T(1,128)S(1)}, u32[]{:S(2)}, u32[]{:S(2)}) async-start(f32[32,1,4096]{2,1,0:T(1,128)} %broadcast_in_dim.2), calls=%async_computation.2 | async-start | bytes 1048576 | tf_op jit(solution)/shard_map/all_to_all | solution.py:102
  154.3 12.5 %multiply_reduce_fusion = (f32[768]{0:T(1024)S(1)}, bf16[4096,768]{1,0:T(8,128)(2,1)}) fusion(f32[768]{0:T(1024)S(1)} %copy-done.2, bf16[4096,768]{1,0:T(8,128)(2,1)} %param.7, bf16[512,4096]{1,0:T(8,128)(2,1)} %all-gather.2.cloned.1.call-done, bf16[512,768]{1,0:T(8,128)(2,1)S(1)} %all_gather.6), kind=kOutput, calls=%fused_computation | convolution fusion | flops 3252681984 | bytes 17569792 | tf_op jit(solution)/shard_map/dot_general | solution.py:86
  166.7 1.5 collective-permute-start.5
  168.3 2.1 %collective-permute-done.5 = f32[768]{0:T(1024)S(1)} collective-permute-done((f32[768]{0:T(1024)S(1)}, f32[768]{0:T(1024)S(1)}, u32[]{:S(2)}, u32[]{:S(2)}) %collective-permute-start.5) | collective-permute-done | bytes 3104 | tf_op jit(solution)/shard_map/ppermute | solution.py:16
  170.4 2.3 %collective-permute-start.6 = (f32[768]{0:T(1024)S(1)}, f32[768]{0:T(1024)S(1)}, u32[]{:S(2)}, u32[]{:S(2)}) collective-permute-start(f32[768]{0:T(1024)S(1)} %add.105), channel_id=1, source_target_pairs={{0,2},{2,0},{1,3},{3,1},{4,6},{6,4},{5,7},{7,5},{8,10},{10,8},{9,1... | collective-permute-start | bytes 9224 | tf_op jit(solution)/shard_map/ppermute | solution.py:16
  172.7 0.6 select_convert_fusion
  173.3 2.2 %collective-permute-done.6 = f32[768]{0:T(1024)S(1)} collective-permute-done((f32[768]{0:T(1024)S(1)}, f32[768]{0:T(1024)S(1)}, u32[]{:S(2)}, u32[]{:S(2)}) %collective-permute-start.6) | collective-permute-done | bytes 3104 | tf_op jit(solution)/shard_map/ppermute | solution.py:16
  175.5 0.6 add.106
  176.1 1.0 reduce_sum.38
  177.1 1.7 convert_element_type.50
  (24 shorter events, 1.0 us)
Async XLA Ops:
  7.2 126.6 %all-gather.2.cloned.1.call-start = ((), (), s32[]{:S(2)}) async-start(), calls=%async_computation.3 | async-start | bytes 4259840 | tf_op jit(solution)/shard_map/all_gather | solution.py:76
  9.1 9.0 %copy-start = (bf16[128,768]{1,0:T(8,128)(2,1)S(1)}, bf16[128,768]{1,0:T(8,128)(2,1)}, u32[]{:S(2)}) copy-start(bf16[128,768]{1,0:T(8,128)(2,1)} %param.9) | copy-start | bytes 589828
  9.1 23.0 %collective-permute-start = (f32[8,4096]{1,0:T(8,128)S(1)}, f32[8,4096]{1,0:T(8,128)S(1)}, u32[]{:S(2)}, u32[]{:S(2)}) collective-permute-start(f32[8,4096]{1,0:T(8,128)S(1)} %mul.67), channel_id=1, source_target_pairs={{0,1},{1,0},{2,3},{3,2},{4,5},{5,4},{6,7},{7,6},{8,9},{9,8},{10,11... | collective-permute-start | bytes 393224 | tf_op jit(solution)/shard_map/ppermute | solution.py:16
  32.1 10.0 %copy-start.1 = (f32[4096]{0:T(1024)S(1)}, f32[4096]{0:T(1024)}, u32[]{:S(2)}) copy-start(f32[4096]{0:T(1024)} %param.6) | copy-start | bytes 49156
  32.1 10.0 %collective-permute-start.1 = (f32[8,4096]{1,0:T(8,128)S(1)}, f32[8,4096]{1,0:T(8,128)S(1)}, u32[]{:S(2)}, u32[]{:S(2)}) collective-permute-start(f32[8,4096]{1,0:T(8,128)S(1)} %add_select_fusion.1), channel_id=1, source_target_pairs={{0,2},{2,0},{1,3},{3,1},{4,6},{6,4},{5,7},{7,5},{8,10},{10,8},{9,1... | collective-permute-start | bytes 393224 | tf_op jit(solution)/shard_map/ppermute | solution.py:16
  45.2 4.4 %collective-permute-start.2 = (bf16[32,8,4096]{2,1,0:T(8,128)(2,1)S(1)}, bf16[32,8,4096]{2,1,0:T(8,128)(2,1)}, u32[]{:S(2)}, u32[]{:S(2)}) collective-permute-start(bf16[32,8,4096]{2,1,0:T(8,128)(2,1)S(1)} %fusion.1), channel_id=1, source_target_pairs={{0,4},{4,0},{1,5},{5,1},{2,6},{6,2},{3,7},{7,3},{8,12},{12,8},{9,1... | collective-permute-start | bytes 6291464 | tf_op jit(solution)/shard_map/ppermute | solution.py:95
  45.3 131.7 %reduce-scatter.2.cloned.1.call-start = ((), (), s32[]{:S(2)}) async-start(), calls=%async_computation.4 | async-start | bytes 1966080 | tf_op jit(solution)/shard_map/reduce_scatter | solution.py:80
  120.5 5.1 %collective-permute-start.3 = (f32[8,4096]{1,0:T(8,128)S(1)}, f32[8,4096]{1,0:T(8,128)S(1)}, u32[]{:S(2)}, u32[]{:S(2)}) collective-permute-start(f32[8,4096]{1,0:T(8,128)S(1)} %mul.74), channel_id=1, source_target_pairs={{0,1},{1,0},{2,3},{3,2},{4,5},{5,4},{6,7},{7,6},{8,9},{9,8},{10,11... | collective-permute-start | bytes 393224 | tf_op jit(solution)/shard_map/ppermute | solution.py:16
  125.6 28.7 %copy-start.2 = (f32[768]{0:T(1024)S(1)}, f32[768]{0:T(1024)}, u32[]{:S(2)}) copy-start(f32[768]{0:T(1024)} %param.8) | copy-start | bytes 9220
  125.6 47.0 %collective-permute-start.4 = (f32[8,4096]{1,0:T(8,128)S(1)}, f32[8,4096]{1,0:T(8,128)S(1)}, u32[]{:S(2)}, u32[]{:S(2)}) collective-permute-start(f32[8,4096]{1,0:T(8,128)S(1)} %add_select_fusion), channel_id=1, source_target_pairs={{0,2},{2,0},{1,3},{3,1},{4,6},{6,4},{5,7},{7,5},{8,10},{10,8},{9,1... | collective-permute-start | bytes 393224 | tf_op jit(solution)/shard_map/ppermute | solution.py:16
  147.1 29.0 %all-to-all-start.1 = ((f32[32,1,4096]{2,1,0:T(1,128)}), f32[32,1,4096]{2,1,0:T(1,128)S(1)}, u32[]{:S(2)}, u32[]{:S(2)}) async-start(f32[32,1,4096]{2,1,0:T(1,128)} %broadcast_in_dim.2), calls=%async_computation.2 | async-start | bytes 1048576 | tf_op jit(solution)/shard_map/all_to_all | solution.py:102
  166.7 3.6 %collective-permute-start.5 = (f32[768]{0:T(1024)S(1)}, f32[768]{0:T(1024)S(1)}, u32[]{:S(2)}, u32[]{:S(2)}) collective-permute-start(f32[768]{0:T(1024)S(1)} %get-tuple-element.13), channel_id=1, source_target_pairs={{0,1},{1,0},{2,3},{3,2},{4,5},{5,4},{6,7},{7,6},{8,9},{9,8},{10,11... | collective-permute-start | bytes 9224 | tf_op jit(solution)/shard_map/ppermute | solution.py:16
  170.4 5.1 %collective-permute-start.6 = (f32[768]{0:T(1024)S(1)}, f32[768]{0:T(1024)S(1)}, u32[]{:S(2)}, u32[]{:S(2)}) collective-permute-start(f32[768]{0:T(1024)S(1)} %add.105), channel_id=1, source_target_pairs={{0,2},{2,0},{1,3},{3,1},{4,6},{6,4},{5,7},{7,5},{8,10},{10,8},{9,1... | collective-permute-start | bytes 9224 | tf_op jit(solution)/shard_map/ppermute | solution.py:16
Sparse Core Ops, SparseCore 0:
  45.5 88.2 all-gather.1
  142.6 25.8 reduce-scatter.1

commit v11 on v9

--- a/solution.py
+++ b/solution.py
@@ -68,7 +68,16 @@
     ratio_weight = weight.astype(jnp.float32) / clip_weight
     tanh_weight = jnp.tanh(ratio_weight)
     quant_weight = (clip_weight * tanh_weight).astype(jnp.bfloat16)
-    all_cot = lax.all_gather(cotangent, "tensor", axis=0, tiled=True)
+    all_cot = cotangent
+    position = lax.axis_index("tensor")
+    for bit_number in range(lax.axis_size("tensor").bit_length() - 1):
+        partner = swapped(all_cot, "tensor", bit_number)
+        upper = jnp.bitwise_and(jnp.right_shift(position, bit_number), 1) == 1
+        all_cot = jnp.where(
+            upper,
+            jnp.concatenate([partner, all_cot]),
+            jnp.concatenate([all_cot, partner]),
+        )
     partial = lax.dot_general(
         all_cot, quant_weight, (((1,), (1,)), ((), ())), preferred_element_type=jnp.float32
     ).reshape(chips, cores, rows, width)

time: 183 us -> 186 us (1.016)
  waiting for transfers between devices: 16.2 us -> 30.8 us
  blocking collectives: 83.5 us -> 69.6 us
    all_gather x1 -> x0, blocking collectives: 14 us -> none  [body(): all_cot = lax.all_gather(cotangent, 'tensor', axis=0, tiled=True)]
    ppermute x6 -> x8, waiting for transfers between devices: 6.05 us -> 19.3 us  [swapped(): return lax.ppermute(block, axis, route)]
    ppermute x6 -> x8, starting transfers between devices: 8.6 us -> 9.93 us  [swapped(): return lax.ppermute(block, axis, route)]
  transfers between devices with their start and end apart: 10 -> 12, of which waited for: 4 -> 6; matrix products, arithmetic and copies ran while one was open for 25% -> 20% of each run, Pallas kernels for 0% -> 0%
where the time goes in v11:
time: 186 us; the launch traced here: 185 us
  blocking collectives  69.6 us (37%)
  matrix products  30.8 us (17%)
  waiting for transfers between devices  30.8 us (17%)
  starting transfers between devices  18.8 us (10%)
  other arithmetic  15.8 us (8%)
  between operations  14.2 us (8%)
  local copies, waits for them, and re-layouts  5.1 us (3%)
    all_to_all x1, blocking collectives, body(): lax.all_to_all(chip_sum.astype(jnp.bfloat16), CHIPS, 0, 0, tiled=True)  66.3 us
    ppermute x8, waiting for transfers between devices, swapped(): return lax.ppermute(block, axis, route)  19.3 us
    dot_general x1, matrix products, body(): lax.dot_general(all_act, all_cot, (((0,), (0,)), ((), ())), preferred_ele...  11.8 us
    ppermute x8, starting transfers between devices, swapped(): return lax.ppermute(block, axis, route)  9.93 us
    dot_general x1, matrix products, body(): lax.dot_general(all_cot, quant_weight, (((1,), (1,)), ((), ())), preferre...  8.87 us
    all_to_all x1, starting transfers between devices, body(): lax.all_to_all(spread, CHIPS, 0, 0, tiled=True)  8.73 us
    dot_general x1, matrix products, body(): jnp.dot(block, quant_weight, preferred_element_type=jnp.float32)  8.62 us
    convert_element_type x1, other arithmetic, body(): quant_weight = (clip_weight * tanh_weight).astype(jnp.bfloat16)  7.31 us
  transfers between devices with their start and end apart: 12, of which 6 were waited for; matrix products, arithmetic and copies ran while one was open for 20% of the time, Pallas kernels for 0%

profile of v11, /device:TPU:2, one launch (start us, length us, event | category | flops | bytes accessed | tf_op | source)
XLA Modules:
  0.0 185.1 jit_solution(13887591131109044826)
XLA Ops:
  7.2 1.0 reshape.34
  8.6 0.4 convolution_multiply_fusion.1
  9.1 1.7 collective-permute-start
  10.7 0.5 collective-permute-start.2
  11.2 4.3 %collective-permute-done = f32[8,4096]{1,0:T(8,128)S(1)} collective-permute-done((f32[8,4096]{1,0:T(8,128)S(1)}, f32[8,4096]{1,0:T(8,128)S(1)}, u32[]{:S(2)}, u32[]{:S(2)}) %collective-permute-start) | collective-permute-done | bytes 131104 | tf_op jit(solution)/shard_map/ppermute | solution.py:16
  15.6 3.3 %collective-permute-start.1 = (f32[8,4096]{1,0:T(8,128)S(1)}, f32[8,4096]{1,0:T(8,128)S(1)}, u32[]{:S(2)}, u32[]{:S(2)}) collective-permute-start(f32[8,4096]{1,0:T(8,128)S(1)} %add_select_fusion.1), channel_id=1, source_target_pairs={{0,2},{2,0},{1,3},{3,1},{4,6},{6,4},{5,7},{7,5},{8,10},{10,8},{9,1... | collective-permute-start | bytes 393224 | tf_op jit(solution)/shard_map/ppermute | solution.py:16
  18.9 7.3 %multiply_convert_fusion.1 = bf16[4096,768]{1,0:T(8,128)(2,1)} fusion(f32[768]{0:T(1024)} %param.8, bf16[4096,768]{1,0:T(8,128)(2,1)} %param.7), kind=kLoop, calls=%fused_computation.3 | loop fusion | flops 12582912 | bytes 12585984 | tf_op jit(solution)/shard_map/convert_element_type | solution.py:70
  26.3 0.4 collective-permute-start.3
  26.7 0.7 multiply_convert_fusion.2
  27.4 9.1 %collective-permute-done.3 = bf16[256,768]{1,0:T(8,128)(2,1)S(1)} collective-permute-done((bf16[256,768]{1,0:T(8,128)(2,1)S(1)}, bf16[256,768]{1,0:T(8,128)(2,1)S(1)}, u32[]{:S(2)}, u32[]{:S(2)}) %collective-permute-start.3) | collective-permute-done | bytes 393248 | tf_op jit(solution)/shard_map/ppermute | solution.py:16
  36.5 8.9 %fusion.3 = f32[512,4096]{1,0:T(8,128)} fusion(bf16[4096,768]{1,0:T(8,128)(2,1)} %multiply_convert_fusion.1, bf16[256,768]{1,0:T(8,128)(2,1)S(1)} %maximum_select_fusion.1, bf16[256,768]{1,0:T(8,128)(2,1)S(1)} %collective-permute-done.3, pred[]{:T(512)S(6)} %eq.4), kind=kOutput, calls=%fused_computation.17 | convolution fusion | flops 3224764416 | bytes 15466497 | tf_op jit(solution)/shard_map/dot_general | solution.py:81
  45.3 2.5 %fusion.1 = bf16[32,8,4096]{2,1,0:T(8,128)(2,1)S(1)} fusion(f32[32,2,8,4096]{3,2,1,0:T(8,128)} %bitcast.30, s32[]{:T(128)S(6)} %select_n.54), kind=kLoop, calls=%fused_computation.9 | loop fusion | bytes 4194308 | tf_op jit(solution)/shard_map/convert_element_type | solution.py:103
  47.9 4.3 %collective-permute-done.4 = bf16[32,8,4096]{2,1,0:T(8,128)(2,1)} collective-permute-done((bf16[32,8,4096]{2,1,0:T(8,128)(2,1)S(1)}, bf16[32,8,4096]{2,1,0:T(8,128)(2,1)}, u32[]{:S(2)}, u32[]{:S(2)}) %collective-permute-start.4) | collective-permute-done | bytes 2097184 | tf_op jit(solution)/shard_map/ppermute | solution.py:103
  52.2 3.4 %fusion = bf16[32,8,4096]{2,1,0:T(8,128)(2,1)S(1)} fusion(bf16[32,8,4096]{2,1,0:T(8,128)(2,1)} %collective-permute-done.4, f32[32,2,8,4096]{3,2,1,0:T(8,128)} %bitcast.31, s32[]{:T(128)S(6)} %select_n.53), kind=kLoop, calls=%fused_computation.6 | loop fusion | flops 3145728 | bytes 8388612 | tf_op jit(solution)/shard_map/convert_element_type | solution.py:104
  55.6 66.3 %all_to_all.11 = bf16[32,8,4096]{2,1,0:T(8,128)(2,1)S(1)} all-to-all(bf16[32,8,4096]{2,1,0:T(8,128)(2,1)S(1)} %fusion), channel_id=1, replica_groups=mesh['dx'=4,'dz'=8,'dc'=2,'tensor'=4] {'dx','dz'}, dimensions={0} | all-to-all | bytes 4194304 | tf_op jit(solution)/shard_map/all_to_all | solution.py:104
  122.3 0.4 convolution_bitcast_fusion
  122.7 0.4 convolution_multiply_fusion
  123.2 0.5 collective-permute-start.5
  123.7 3.3 %psum.7 = f32[4096]{0:T(1024)S(1)} all-reduce(f32[4096]{0:T(1024)S(1)} %get-tuple-element.13), channel_id=1, replica_groups=mesh['dx'=4,'dz'=8,'dc'=2,'tensor'=4] {'dc'}, use_global_device_ids=true, to_apply=%region_3.4 | all-reduce | flops 4096 | bytes 32768 | tf_op jit(solution)/shard_map/psum | solution.py:107
  127.1 1.3 broadcast_in_dim.2
  128.3 8.7 %all-to-all-start.1 = ((f32[32,1,4096]{2,1,0:T(1,128)}), f32[32,1,4096]{2,1,0:T(1,128)S(1)}, u32[]{:S(2)}, u32[]{:S(2)}) async-start(f32[32,1,4096]{2,1,0:T(1,128)} %broadcast_in_dim.2), calls=%async_computation.2 | async-start | bytes 1048576 | tf_op jit(solution)/shard_map/all_to_all | solution.py:109
  137.2 2.0 %collective-permute-start.6 = (f32[8,4096]{1,0:T(8,128)S(1)}, f32[8,4096]{1,0:T(8,128)S(1)}, u32[]{:S(2)}, u32[]{:S(2)}) collective-permute-start(f32[8,4096]{1,0:T(8,128)S(1)} %add_select_fusion), channel_id=1, source_target_pairs={{0,2},{2,0},{1,3},{3,1},{4,6},{6,4},{5,7},{7,5},{8,10},{10,8},{9,1... | collective-permute-start | bytes 393224 | tf_op jit(solution)/shard_map/ppermute | solution.py:16
  139.2 8.6 %fusion.39 = f32[512,768]{1,0:T(8,128)} fusion(bf16[512,4096]{1,0:T(8,128)(2,1)} %all-gather.2.cloned.1.call-done, bf16[4096,768]{1,0:T(8,128)(2,1)} %multiply_convert_fusion.1), kind=kOutput, calls=%fused_computation.61 | convolution fusion | flops 3221225472 | bytes 12058624 | tf_op jit(solution)/shard_map/dot_general | solution.py:89
  147.8 11.8 %multiply_reduce_fusion = (f32[768]{0:T(1024)S(1)}, bf16[4096,768]{1,0:T(8,128)(2,1)}) fusion(f32[768]{0:T(1024)S(1)} %copy-done.2, bf16[4096,768]{1,0:T(8,128)(2,1)} %param.7, bf16[512,4096]{1,0:T(8,128)(2,1)} %all-gather.2.cloned.1.call-done, bf16[256,768]{1,0:T(8,128)(2,1)S(1)} %maximum_select_fusion.1, bf16[256,768]{1,0:T(8,128)(2,1)S(1)} %collective-permute-done.3, ...), kind=kOutput, calls=%fused_computation | convolution fusion | flops 3256220928 | bytes 17569792 | tf_op jit(solution)/shard_map/dot_general | solution.py:94
  159.6 3.8 %collective-permute-done.7 = f32[768]{0:T(1024)S(1)} collective-permute-done((f32[768]{0:T(1024)S(1)}, f32[768]{0:T(1024)S(1)}, u32[]{:S(2)}, u32[]{:S(2)}) %collective-permute-start.7) | collective-permute-done | bytes 3104 | tf_op jit(solution)/shard_map/ppermute | solution.py:16
  163.4 1.6 collective-permute-start.8
  165.1 0.6 select_convert_fusion
  165.7 1.0 reduce_sum.38
  166.7 2.0 %collective-permute-done.8 = f32[768]{0:T(1024)S(1)} collective-permute-done((f32[768]{0:T(1024)S(1)}, f32[768]{0:T(1024)S(1)}, u32[]{:S(2)}, u32[]{:S(2)}) %collective-permute-start.8) | collective-permute-done | bytes 3104 | tf_op jit(solution)/shard_map/ppermute | solution.py:16
  168.8 0.6 add.106
  169.3 7.2 %reduce-scatter.2.cloned.1.call-done = f32[128,768]{1,0:T(8,128)} async-done(((f32[512,768]{1,0:T(8,128)}), f32[128,768]{1,0:T(8,128)}) %reduce-scatter.2.cloned.1.call-update) | async-done | bytes 393232 | tf_op jit(solution)/shard_map/reduce_scatter | solution.py:88
  176.6 1.7 convert_element_type.50
  (28 shorter events, 1.4 us)
Async XLA Ops:
  7.2 132.0 %all-gather.2.cloned.1.call-start = ((), (), s32[]{:S(2)}) async-start(), calls=%async_computation.3 | async-start | bytes 4259840 | tf_op jit(solution)/shard_map/all_gather | solution.py:85
  9.1 6.5 %collective-permute-start = (f32[8,4096]{1,0:T(8,128)S(1)}, f32[8,4096]{1,0:T(8,128)S(1)}, u32[]{:S(2)}, u32[]{:S(2)}) collective-permute-start(f32[8,4096]{1,0:T(8,128)S(1)} %mul.67), channel_id=1, source_target_pairs={{0,1},{1,0},{2,3},{3,2},{4,5},{5,4},{6,7},{7,6},{8,9},{9,8},{10,11... | collective-permute-start | bytes 393224 | tf_op jit(solution)/shard_map/ppermute | solution.py:16
  10.7 15.4 %collective-permute-start.2 = (bf16[128,768]{1,0:T(8,128)(2,1)}, bf16[128,768]{1,0:T(8,128)(2,1)S(1)}, u32[]{:S(2)}, u32[]{:S(2)}) collective-permute-start(bf16[128,768]{1,0:T(8,128)(2,1)} %param.9), channel_id=1, source_target_pairs={{0,1},{1,0},{2,3},{3,2},{4,5},{5,4},{6,7},{7,6},{8,9},{9,8},{10,11... | collective-permute-start | bytes 589832 | tf_op jit(solution)/shard_map/ppermute | solution.py:16
  15.6 10.6 %copy-start = (bf16[128,768]{1,0:T(8,128)(2,1)S(1)}, bf16[128,768]{1,0:T(8,128)(2,1)}, u32[]{:S(2)}) copy-start(bf16[128,768]{1,0:T(8,128)(2,1)} %param.9) | copy-start | bytes 589828
  15.6 11.1 %copy-start.1 = (f32[4096]{0:T(1024)S(1)}, f32[4096]{0:T(1024)}, u32[]{:S(2)}) copy-start(f32[4096]{0:T(1024)} %param.6) | copy-start | bytes 49156
  15.6 11.1 %collective-permute-start.1 = (f32[8,4096]{1,0:T(8,128)S(1)}, f32[8,4096]{1,0:T(8,128)S(1)}, u32[]{:S(2)}, u32[]{:S(2)}) collective-permute-start(f32[8,4096]{1,0:T(8,128)S(1)} %add_select_fusion.1), channel_id=1, source_target_pairs={{0,2},{2,0},{1,3},{3,1},{4,6},{6,4},{5,7},{7,5},{8,10},{10,8},{9,1... | collective-permute-start | bytes 393224 | tf_op jit(solution)/shard_map/ppermute | solution.py:16
  26.3 10.2 %collective-permute-start.3 = (bf16[256,768]{1,0:T(8,128)(2,1)S(1)}, bf16[256,768]{1,0:T(8,128)(2,1)S(1)}, u32[]{:S(2)}, u32[]{:S(2)}) collective-permute-start(bf16[256,768]{1,0:T(8,128)(2,1)S(1)} %maximum_select_fusion.1), channel_id=1, source_target_pairs={{0,2},{2,0},{1,3},{3,1},{4,6},{6,4},{5,7},{7,5},{8,10},{10,8},{9,1... | collective-permute-start | bytes 1179656 | tf_op jit(solution)/shard_map/ppermute | solution.py:16
  47.8 4.4 %collective-permute-start.4 = (bf16[32,8,4096]{2,1,0:T(8,128)(2,1)S(1)}, bf16[32,8,4096]{2,1,0:T(8,128)(2,1)}, u32[]{:S(2)}, u32[]{:S(2)}) collective-permute-start(bf16[32,8,4096]{2,1,0:T(8,128)(2,1)S(1)} %fusion.1), channel_id=1, source_target_pairs={{0,4},{4,0},{1,5},{5,1},{2,6},{6,2},{3,7},{7,3},{8,12},{12,8},{9,1... | collective-permute-start | bytes 6291464 | tf_op jit(solution)/shard_map/ppermute | solution.py:103
  123.2 13.9 %collective-permute-start.5 = (f32[8,4096]{1,0:T(8,128)S(1)}, f32[8,4096]{1,0:T(8,128)S(1)}, u32[]{:S(2)}, u32[]{:S(2)}) collective-permute-start(f32[8,4096]{1,0:T(8,128)S(1)} %mul.74), channel_id=1, source_target_pairs={{0,1},{1,0},{2,3},{3,2},{4,5},{5,4},{6,7},{7,6},{8,9},{9,8},{10,11... | collective-permute-start | bytes 393224 | tf_op jit(solution)/shard_map/ppermute | solution.py:16
  128.3 37.4 %all-to-all-start.1 = ((f32[32,1,4096]{2,1,0:T(1,128)}), f32[32,1,4096]{2,1,0:T(1,128)S(1)}, u32[]{:S(2)}, u32[]{:S(2)}) async-start(f32[32,1,4096]{2,1,0:T(1,128)} %broadcast_in_dim.2), calls=%async_computation.2 | async-start | bytes 1048576 | tf_op jit(solution)/shard_map/all_to_all | solution.py:109
  137.1 39.5 %reduce-scatter.2.cloned.1.call-start = ((), (), s32[]{:S(2)}) async-start(), calls=%async_computation.4 | async-start | bytes 1966080 | tf_op jit(solution)/shard_map/reduce_scatter | solution.py:88
  137.2 10.7 %copy-start.2 = (f32[768]{0:T(1024)S(1)}, f32[768]{0:T(1024)}, u32[]{:S(2)}) copy-start(f32[768]{0:T(1024)} %param.8) | copy-start | bytes 9220
  137.2 27.9 %collective-permute-start.6 = (f32[8,4096]{1,0:T(8,128)S(1)}, f32[8,4096]{1,0:T(8,128)S(1)}, u32[]{:S(2)}, u32[]{:S(2)}) collective-permute-start(f32[8,4096]{1,0:T(8,128)S(1)} %add_select_fusion), channel_id=1, source_target_pairs={{0,2},{2,0},{1,3},{3,1},{4,6},{6,4},{5,7},{7,5},{8,10},{10,8},{9,1... | collective-permute-start | bytes 393224 | tf_op jit(solution)/shard_map/ppermute | solution.py:16
  159.6 3.8 %collective-permute-start.7 = (f32[768]{0:T(1024)S(1)}, f32[768]{0:T(1024)S(1)}, u32[]{:S(2)}, u32[]{:S(2)}) collective-permute-start(f32[768]{0:T(1024)S(1)} %get-tuple-element.11), channel_id=1, source_target_pairs={{0,1},{1,0},{2,3},{3,2},{4,5},{5,4},{6,7},{7,6},{8,9},{9,8},{10,11... | collective-permute-start | bytes 9224 | tf_op jit(solution)/shard_map/ppermute | solution.py:16
  163.4 5.3 %collective-permute-start.8 = (f32[768]{0:T(1024)S(1)}, f32[768]{0:T(1024)S(1)}, u32[]{:S(2)}, u32[]{:S(2)}) collective-permute-start(f32[768]{0:T(1024)S(1)} %add.105), channel_id=1, source_target_pairs={{0,2},{2,0},{1,3},{3,1},{4,6},{6,4},{5,7},{7,5},{8,10},{10,8},{9,1... | collective-permute-start | bytes 9224 | tf_op jit(solution)/shard_map/ppermute | solution.py:16
Sparse Core Ops, SparseCore 0:
  48.0 86.7 all-gather.1
  147.9 28.6 reduce-scatter.1

commit v12 on v10

--- a/solution.py
+++ b/solution.py
@@ -77,12 +77,9 @@
     pair = [(0, 1), (1, 0)]
     block = all_act
     proj_part = jnp.dot(block, quant_weight, preferred_element_type=jnp.float32)
-    projected = lax.psum_scatter(
-        proj_part,
-        "tensor",
-        scatter_dimension=0,
-        tiled=True,
-    ).astype(jnp.bfloat16)
+    proj_pieces = proj_part.reshape((lax.axis_size("tensor"), -1) + proj_part.shape[1:])
+    proj_pieces = lax.all_to_all(proj_pieces.astype(jnp.bfloat16), "tensor", 0, 0, tiled=True)
+    projected = jnp.sum(proj_pieces.astype(jnp.float32), axis=0).astype(jnp.bfloat16)
     weight_prod = lax.dot_general(
         all_act, all_cot, (((0,), (0,)), ((), ())), preferred_element_type=jnp.float32
     )
@@ -96,7 +93,6 @@
     pieces = lax.all_to_all(chip_sum.astype(jnp.bfloat16), CHIPS, 0, 0, tiled=True)
     act_prod = jnp.sum(pieces.astype(jnp.float32), axis=0)
     act_terms = jnp.sum(act_prod * edge_act, axis=0)
-    act_terms, _ = lax.optimization_barrier((act_terms, proj_part))
     act_terms = lax.psum(act_terms, "dc")
     spread = jnp.broadcast_to(act_terms[None], (chips,) + act_terms.shape)
     clip_act_grad = jnp.sum(lax.all_to_all(spread, CHIPS, 0, 0, tiled=True), axis=0)

time: 186 us -> 183 us (0.984)
  waiting for transfers between devices: 18 us -> 13.6 us
  starting transfers between devices: 18 us -> 21.8 us
  matrix products: 31 us -> 29 us
    all_to_all x0 -> x1, waiting for transfers between devices: none -> 9.32 us  [body(): lax.all_to_all(proj_pieces.astype(jnp.bfloat16), 'tensor', 0, 0, tiled=True)]
    ppermute x6, waiting for transfers between devices: 7.74 us -> 0.02 us  [swapped(): return lax.ppermute(block, axis, route)]
    all_gather x1, waiting for transfers between devices: 6.04 us -> 0.01 us  [body(): all_act = lax.all_gather(quant_act, DP, axis=0, tiled=True)]
    all_to_all x0 -> x1, starting transfers between devices: none -> 3.49 us  [body(): lax.all_to_all(proj_pieces.astype(jnp.bfloat16), 'tensor', 0, 0, tiled=True)]
    dot_general x1, matrix products: 8.63 us -> 6.45 us  [body(): proj_part = jnp.dot(block, quant_weight, preferred_element_type=jnp.float32)]
  transfers between devices with their start and end apart: 10 -> 10, of which waited for: 5 -> 2; matrix products, arithmetic and copies ran while one was open for 24% -> 24% of each run, Pallas kernels for 0% -> 0%
where the time goes in v12:
time: 183 us; the launch traced here: 182 us
  blocking collectives  83.6 us (46%)
  matrix products  29 us (16%)
  starting transfers between devices  21.8 us (12%)
  other arithmetic  15 us (8%)
  between operations  14.2 us (8%)
  waiting for transfers between devices  13.6 us (7%)
  local copies, waits for them, and re-layouts  5.11 us (3%)
    all_to_all x1, blocking collectives, body(): lax.all_to_all(chip_sum.astype(jnp.bfloat16), CHIPS, 0, 0, tiled=True)  66.2 us
    all_gather x1, blocking collectives, body(): all_cot = lax.all_gather(cotangent, 'tensor', axis=0, tiled=True)  14 us
    dot_general x1, matrix products, body(): lax.dot_general(all_act, all_cot, (((0,), (0,)), ((), ())), preferred_ele...  12.6 us
    ppermute x6, starting transfers between devices, swapped(): return lax.ppermute(block, axis, route)  9.68 us
    all_to_all x1, waiting for transfers between devices, body(): lax.all_to_all(proj_pieces.astype(jnp.bfloat16), 'tensor', 0, 0, tiled=True)  9.32 us
    all_to_all x1, starting transfers between devices, body(): lax.all_to_all(spread, CHIPS, 0, 0, tiled=True)  8.51 us
    dot_general x1, matrix products, body(): lax.dot_general(all_cot, quant_weight, (((1,), (1,)), ((), ())), preferre...  8.41 us
    convert_element_type x1, other arithmetic, body(): quant_weight = (clip_weight * tanh_weight).astype(jnp.bfloat16)  7.38 us
  transfers between devices with their start and end apart: 10, of which 2 were waited for; matrix products, arithmetic and copies ran while one was open for 24% of the time, Pallas kernels for 0%

profile of v12, /device:TPU:2, one launch (start us, length us, event | category | flops | bytes accessed | tf_op | source)
XLA Modules:
  0.0 182.2 jit_solution(7978398714241349061)
XLA Ops:
  7.2 1.0 reshape.36
  8.2 0.3 convolution_bitcast_fusion.1
  8.6 0.4 convolution_multiply_fusion.1
  9.0 0.1 mul.67
  9.1 1.7 collective-permute-start
  10.8 7.4 %multiply_convert_fusion.1 = bf16[4096,768]{1,0:T(8,128)(2,1)} fusion(f32[768]{0:T(1024)} %param.8, bf16[4096,768]{1,0:T(8,128)(2,1)} %param.7), kind=kLoop, calls=%fused_computation.3 | loop fusion | flops 12582912 | bytes 12585984 | tf_op jit(solution)/shard_map/convert_element_type | solution.py:70
  18.1 14.0 %all_gather.6 = bf16[512,768]{1,0:T(8,128)(2,1)S(1)} all-gather(bf16[128,768]{1,0:T(8,128)(2,1)S(1)} %copy-done), channel_id=1, replica_groups=mesh['dx'=4,'dz'=8,'dc'=2,'tensor'=4] {'tensor'}, dimensions={0}, use_global_device_ids=true | all-gather | bytes 983040 | tf_op jit(solution)/shard_map/all_gather | solution.py:71
  32.2 1.5 collective-permute-start.1
  33.7 8.4 %fusion.35 = f32[4096,512]{0,1:T(8,128)} fusion(bf16[4096,768]{1,0:T(8,128)(2,1)} %multiply_convert_fusion.1, bf16[512,768]{1,0:T(8,128)(2,1)S(1)} %all_gather.6), kind=kOutput, calls=%fused_computation.56 | convolution fusion | flops 3221225472 | bytes 15466496 | tf_op jit(solution)/shard_map/dot_general | solution.py:72
  42.1 0.7 multiply_convert_fusion.2
  42.8 2.5 %fusion.1 = bf16[32,8,4096]{2,1,0:T(8,128)(2,1)S(1)} fusion(f32[32,2,8,4096]{3,2,1,0:T(8,128)} %bitcast.35, s32[]{:T(128)S(6)} %select_n.34), kind=kLoop, calls=%fused_computation.9 | loop fusion | bytes 4194308 | tf_op jit(solution)/shard_map/convert_element_type | solution.py:92
  45.4 4.3 %collective-permute-done.2 = bf16[32,8,4096]{2,1,0:T(8,128)(2,1)} collective-permute-done((bf16[32,8,4096]{2,1,0:T(8,128)(2,1)S(1)}, bf16[32,8,4096]{2,1,0:T(8,128)(2,1)}, u32[]{:S(2)}, u32[]{:S(2)}) %collective-permute-start.2) | collective-permute-done | bytes 2097184 | tf_op jit(solution)/shard_map/ppermute | solution.py:92
  49.6 3.4 %fusion = bf16[32,8,4096]{2,1,0:T(8,128)(2,1)S(1)} fusion(bf16[32,8,4096]{2,1,0:T(8,128)(2,1)} %collective-permute-done.2, f32[32,2,8,4096]{3,2,1,0:T(8,128)} %bitcast.36, s32[]{:T(128)S(6)} %select_n.33), kind=kLoop, calls=%fused_computation.6 | loop fusion | flops 3145728 | bytes 8388612 | tf_op jit(solution)/shard_map/convert_element_type | solution.py:93
  53.1 66.2 %all_to_all.16 = bf16[32,8,4096]{2,1,0:T(8,128)(2,1)S(1)} all-to-all(bf16[32,8,4096]{2,1,0:T(8,128)(2,1)S(1)} %fusion), channel_id=1, replica_groups=mesh['dx'=4,'dz'=8,'dc'=2,'tensor'=4] {'dx','dz'}, dimensions={0} | all-to-all | bytes 4194304 | tf_op jit(solution)/shard_map/all_to_all | solution.py:93
  119.3 0.3 convert_reduce_fusion
  119.8 0.4 convolution_bitcast_fusion
  120.2 0.4 convolution_multiply_fusion
  120.6 0.1 mul.74
  120.7 1.5 collective-permute-start.3
  122.2 3.3 %psum.7 = f32[4096]{0:T(1024)S(1)} all-reduce(f32[4096]{0:T(1024)S(1)} %get-tuple-element.13), channel_id=1, replica_groups=mesh['dx'=4,'dz'=8,'dc'=2,'tensor'=4] {'dc'}, use_global_device_ids=true, to_apply=%region_3.4 | all-reduce | flops 4096 | bytes 32768 | tf_op jit(solution)/shard_map/psum | solution.py:96
  125.6 1.3 broadcast_in_dim.2
  126.8 8.5 %all-to-all-start.2 = ((f32[32,1,4096]{2,1,0:T(1,128)}), f32[32,1,4096]{2,1,0:T(1,128)S(1)}, u32[]{:S(2)}, u32[]{:S(2)}) async-start(f32[32,1,4096]{2,1,0:T(1,128)} %broadcast_in_dim.2), calls=%async_computation.2 | async-start | bytes 1048576 | tf_op jit(solution)/shard_map/all_to_all | solution.py:98
  135.4 2.4 %collective-permute-start.4 = (f32[8,4096]{1,0:T(8,128)S(1)}, f32[8,4096]{1,0:T(8,128)S(1)}, u32[]{:S(2)}, u32[]{:S(2)}) collective-permute-start(f32[8,4096]{1,0:T(8,128)S(1)} %add_select_fusion), channel_id=1, source_target_pairs={{0,2},{2,0},{1,3},{3,1},{4,6},{6,4},{5,7},{7,5},{8,10},{10,8},{9,1... | collective-permute-start | bytes 393224 | tf_op jit(solution)/shard_map/ppermute | solution.py:16
  137.8 12.6 %multiply_reduce_fusion = (f32[768]{0:T(1024)S(1)}, bf16[4096,768]{1,0:T(8,128)(2,1)}) fusion(f32[768]{0:T(1024)S(1)} %copy-done.2, bf16[4096,768]{1,0:T(8,128)(2,1)} %param.7, bf16[512,4096]{1,0:T(8,128)(2,1)} %all-gather.2.cloned.1.call-done, bf16[512,768]{1,0:T(8,128)(2,1)S(1)} %all_gather.6), kind=kOutput, calls=%fused_computation | convolution fusion | flops 3252681984 | bytes 17569792 | tf_op jit(solution)/shard_map/dot_general | solution.py:83
  150.3 6.5 %convolution_convert_fusion = bf16[512,768]{1,0:T(8,128)(2,1)} fusion(bf16[512,4096]{1,0:T(8,128)(2,1)S(1)} %copy-done.3, bf16[4096,768]{1,0:T(8,128)(2,1)} %multiply_convert_fusion.1), kind=kOutput, calls=%fused_computation.10 | convolution fusion | flops 3221618688 | bytes 11272192 | tf_op jit(solution)/shard_map/dot_general | solution.py:79
  156.8 2.6 %collective-permute-start.6 = (f32[768]{0:T(1024)S(1)}, f32[768]{0:T(1024)S(1)}, u32[]{:S(2)}, u32[]{:S(2)}) collective-permute-start(f32[768]{0:T(1024)S(1)} %add.103), channel_id=1, source_target_pairs={{0,2},{2,0},{1,3},{3,1},{4,6},{6,4},{5,7},{7,5},{8,10},{10,8},{9,1... | collective-permute-start | bytes 9224 | tf_op jit(solution)/shard_map/ppermute | solution.py:16
  159.4 3.5 %all-to-all-start = ((bf16[4,128,768]{2,1,0:T(8,128)(2,1)}), bf16[4,128,768]{2,1,0:T(8,128)(2,1)S(1)}, u32[]{:S(2)}, u32[]{:S(2)}) async-start(bf16[4,128,768]{2,1,0:T(8,128)(2,1)} %bitcast.5), calls=%async_computation | async-start | bytes 1572864 | tf_op jit(solution)/shard_map/all_to_all | solution.py:81
  162.9 0.7 select_convert_fusion
  163.6 1.0 reduce_sum.51
  164.6 0.6 add.104
  165.2 9.3 %all-to-all-done = bf16[4,128,768]{2,1,0:T(8,128)(2,1)S(1)} async-done(((bf16[4,128,768]{2,1,0:T(8,128)(2,1)}), bf16[4,128,768]{2,1,0:T(8,128)(2,1)S(1)}, u32[]{:S(2)}, u32[]{:S(2)}) %all-to-all-start) | async-done | bytes 786464 | tf_op jit(solution)/shard_map/all_to_all | solution.py:81
  174.5 0.8 reduce_sum.48
  (25 shorter events, 0.4 us)
Async XLA Ops:
  7.2 130.6 %all-gather.2.cloned.1.call-start = ((), (), s32[]{:S(2)}) async-start(), calls=%async_computation.3 | async-start | bytes 4259840 | tf_op jit(solution)/shard_map/all_gather | solution.py:76
  9.1 9.1 %copy-start = (bf16[128,768]{1,0:T(8,128)(2,1)S(1)}, bf16[128,768]{1,0:T(8,128)(2,1)}, u32[]{:S(2)}) copy-start(bf16[128,768]{1,0:T(8,128)(2,1)} %param.9) | copy-start | bytes 589828
  9.1 23.0 %collective-permute-start = (f32[8,4096]{1,0:T(8,128)S(1)}, f32[8,4096]{1,0:T(8,128)S(1)}, u32[]{:S(2)}, u32[]{:S(2)}) collective-permute-start(f32[8,4096]{1,0:T(8,128)S(1)} %mul.67), channel_id=1, source_target_pairs={{0,1},{1,0},{2,3},{3,2},{4,5},{5,4},{6,7},{7,6},{8,9},{9,8},{10,11... | collective-permute-start | bytes 393224 | tf_op jit(solution)/shard_map/ppermute | solution.py:16
  32.1 10.0 %copy-start.1 = (f32[4096]{0:T(1024)S(1)}, f32[4096]{0:T(1024)}, u32[]{:S(2)}) copy-start(f32[4096]{0:T(1024)} %param.6) | copy-start | bytes 49156
  32.2 10.0 %collective-permute-start.1 = (f32[8,4096]{1,0:T(8,128)S(1)}, f32[8,4096]{1,0:T(8,128)S(1)}, u32[]{:S(2)}, u32[]{:S(2)}) collective-permute-start(f32[8,4096]{1,0:T(8,128)S(1)} %add_select_fusion.1), channel_id=1, source_target_pairs={{0,2},{2,0},{1,3},{3,1},{4,6},{6,4},{5,7},{7,5},{8,10},{10,8},{9,1... | collective-permute-start | bytes 393224 | tf_op jit(solution)/shard_map/ppermute | solution.py:16
  45.3 4.4 %collective-permute-start.2 = (bf16[32,8,4096]{2,1,0:T(8,128)(2,1)S(1)}, bf16[32,8,4096]{2,1,0:T(8,128)(2,1)}, u32[]{:S(2)}, u32[]{:S(2)}) collective-permute-start(bf16[32,8,4096]{2,1,0:T(8,128)(2,1)S(1)} %fusion.1), channel_id=1, source_target_pairs={{0,4},{4,0},{1,5},{5,1},{2,6},{6,2},{3,7},{7,3},{8,12},{12,8},{9,1... | collective-permute-start | bytes 6291464 | tf_op jit(solution)/shard_map/ppermute | solution.py:92
  53.0 84.7 %copy-start.2 = (f32[768]{0:T(1024)S(1)}, f32[768]{0:T(1024)}, u32[]{:S(2)}) copy-start(f32[768]{0:T(1024)} %param.8) | copy-start | bytes 9220
  120.7 14.7 %collective-permute-start.3 = (f32[8,4096]{1,0:T(8,128)S(1)}, f32[8,4096]{1,0:T(8,128)S(1)}, u32[]{:S(2)}, u32[]{:S(2)}) collective-permute-start(f32[8,4096]{1,0:T(8,128)S(1)} %mul.74), channel_id=1, source_target_pairs={{0,1},{1,0},{2,3},{3,2},{4,5},{5,4},{6,7},{7,6},{8,9},{9,8},{10,11... | collective-permute-start | bytes 393224 | tf_op jit(solution)/shard_map/ppermute | solution.py:16
  126.8 32.6 %all-to-all-start.2 = ((f32[32,1,4096]{2,1,0:T(1,128)}), f32[32,1,4096]{2,1,0:T(1,128)S(1)}, u32[]{:S(2)}, u32[]{:S(2)}) async-start(f32[32,1,4096]{2,1,0:T(1,128)} %broadcast_in_dim.2), calls=%async_computation.2 | async-start | bytes 1048576 | tf_op jit(solution)/shard_map/all_to_all | solution.py:98
  135.4 27.5 %collective-permute-start.4 = (f32[8,4096]{1,0:T(8,128)S(1)}, f32[8,4096]{1,0:T(8,128)S(1)}, u32[]{:S(2)}, u32[]{:S(2)}) collective-permute-start(f32[8,4096]{1,0:T(8,128)S(1)} %add_select_fusion), channel_id=1, source_target_pairs={{0,2},{2,0},{1,3},{3,1},{4,6},{6,4},{5,7},{7,5},{8,10},{10,8},{9,1... | collective-permute-start | bytes 393224 | tf_op jit(solution)/shard_map/ppermute | solution.py:16
  137.7 12.6 %copy-start.3 = (bf16[512,4096]{1,0:T(8,128)(2,1)S(1)}, bf16[512,4096]{1,0:T(8,128)(2,1)}, u32[]{:S(2)}) copy-start(bf16[512,4096]{1,0:T(8,128)(2,1)} %all-gather.2.cloned.1.call-done) | copy-start | bytes 12582916
  150.3 6.5 %collective-permute-start.5 = (f32[768]{0:T(1024)S(1)}, f32[768]{0:T(1024)S(1)}, u32[]{:S(2)}, u32[]{:S(2)}) collective-permute-start(f32[768]{0:T(1024)S(1)} %get-tuple-element.11), channel_id=1, source_target_pairs={{0,1},{1,0},{2,3},{3,2},{4,5},{5,4},{6,7},{7,6},{8,9},{9,8},{10,11... | collective-permute-start | bytes 9224 | tf_op jit(solution)/shard_map/ppermute | solution.py:16
  156.8 7.8 %collective-permute-start.6 = (f32[768]{0:T(1024)S(1)}, f32[768]{0:T(1024)S(1)}, u32[]{:S(2)}, u32[]{:S(2)}) collective-permute-start(f32[768]{0:T(1024)S(1)} %add.103), channel_id=1, source_target_pairs={{0,2},{2,0},{1,3},{3,1},{4,6},{6,4},{5,7},{7,5},{8,10},{10,8},{9,1... | collective-permute-start | bytes 9224 | tf_op jit(solution)/shard_map/ppermute | solution.py:16
  159.4 15.1 %all-to-all-start = ((bf16[4,128,768]{2,1,0:T(8,128)(2,1)}), bf16[4,128,768]{2,1,0:T(8,128)(2,1)S(1)}, u32[]{:S(2)}, u32[]{:S(2)}) async-start(bf16[4,128,768]{2,1,0:T(8,128)(2,1)} %bitcast.5), calls=%async_computation | async-start | bytes 1572864 | tf_op jit(solution)/shard_map/all_to_all | solution.py:81
Sparse Core Ops, SparseCore 0:
  45.5 88.0 all-gather.1
